TPU v7x, 256 devices: a whole 4x4x8 slice. The times are simulated.
256 devices in a mesh: dp: 8 (over x, z_hi), ctx: 32 (over z_lo, y, core).
Axes of the slice: x: 4, y: 4, z: 8 (z_hi: 2, z_lo: 4; z = z_hi * 4 + z_lo), core: 2. Of those that a mesh axis runs over, the one named last changes fastest.
Arguments:
- queries: bfloat16 [32768, 1024], P(('dp', 'ctx')), parts along dimension 0, may hold values from -8 to 8
- keys: bfloat16 [32768, 1024], P(('dp', 'ctx')), parts along dimension 0, may hold values from -8 to 8
- values: bfloat16 [32768, 1024], P(('dp', 'ctx')), parts along dimension 0, may hold values from -6 to 6
- grad_out: bfloat16 [32768, 1024], P(('dp', 'ctx')), parts along dimension 0, may hold values from -6 to 6
- rand_blocks: int32 [512, 3], P(('dp', 'ctx')), parts along dimension 0, may hold values from 0 to 1
- global_ids: int32 [16], P('dp'), parts along dimension 0, may hold values from 0 to 63
Outputs:
- attended: bfloat16 [32768, 1024], P(('dp', 'ctx')), parts along dimension 0
- grad_queries: bfloat16 [32768, 1024], P(('dp', 'ctx')), parts along dimension 0
- grad_keys: bfloat16 [32768, 1024], P(('dp', 'ctx')), parts along dimension 0
- grad_values: bfloat16 [32768, 1024], P(('dp', 'ctx')), parts along dimension 0
There are 8 independent parts, one for each index of `dp`. A program takes and returns all parts, laid end to end along the dimension named above; each array names one. Nothing has to cross between parts.
All inputs are finite; a program needn't handle non-finite values.
Results may differ from a plain program's by a relative error of at most 0.02.
Values may be sent and summed in bfloat16 or wider, within the bound.
No kernel may reach another device: no remote copies, remote signals or barrier semaphores. Data moves between devices by JAX's collectives and lax.ppermute only.
A program may use at most 128 MiB of HBM per device.

v0:
```python
import jax
import jax.numpy as jnp
from jax import lax
from jax.sharding import PartitionSpec as P

HEADS = 16
HEAD_DIM = 64
BLOCK = 64
RAND = 3
GLOBALS = 2


SCORE_FLOOR = -1e30


def padded_2(array, sides, width):
    for axis, dim in sides:
        size, length = (lax.axis_size(axis), array.shape[dim])
        up = [(i, (i + 1) % size) for i in range(size - 1)]
        down = [(j, i) for i, j in up]
        last = lax.slice_in_dim(array, length - width, length, axis=dim)
        first = lax.slice_in_dim(array, 0, width, axis=dim)
        before = lax.ppermute(last, axis, up)
        after = lax.ppermute(first, axis, down)
        array = jnp.concatenate([before, array, after], axis=dim)
    return array


def from_root(block, axis, source):
    block = jnp.where(lax.axis_index(axis) == source, block, jnp.zeros_like(block))
    return lax.psum(block, axis)


def partner_2(array, axis, distance):
    return lax.ppermute(array, axis, [(i, i ^ 1 << distance) for i in range(lax.axis_size(axis))])


def passed_along(array, axis, by):
    size = lax.axis_size(axis)
    pairs = [(i, i + by) for i in range(size) if 0 <= i + by < size]
    return lax.ppermute(array, axis, pairs)


def attend_blocks(query_blocks, key_blocks, value_blocks, grad_blocks, key_valid):
    scale_factor = HEAD_DIM ** (-0.5)
    scores = (
        jnp.einsum("jqhd,jkhd->jhqk", query_blocks, key_blocks, preferred_element_type=jnp.float32)
        * scale_factor
    )
    scores = jnp.where(key_valid[:, None, None, :], scores, SCORE_FLOOR)
    highest = jnp.max(scores, axis=-1, keepdims=True)
    raw_weights = jnp.exp(scores - highest)
    weight_total = jnp.sum(raw_weights, axis=-1, keepdims=True)
    probs = raw_weights / weight_total
    probs_low = probs.astype(jnp.bfloat16)
    attended = jnp.einsum(
        "jhqk,jkhd->jqhd", probs_low, value_blocks, preferred_element_type=jnp.float32
    )
    grad_probs = jnp.einsum(
        "jqhd,jkhd->jhqk", grad_blocks, value_blocks, preferred_element_type=jnp.float32
    )
    inner = jnp.sum(probs * grad_probs, axis=-1, keepdims=True)
    grad_scores = (scale_factor * probs * (grad_probs - inner)).astype(jnp.bfloat16)
    grad_query = jnp.einsum(
        "jhqk,jkhd->jqhd", grad_scores, key_blocks, preferred_element_type=jnp.float32
    )
    grad_key = jnp.einsum(
        "jhqk,jqhd->jkhd", grad_scores, query_blocks, preferred_element_type=jnp.float32
    )
    grad_value = jnp.einsum(
        "jhqk,jqhd->jkhd", probs_low, grad_blocks, preferred_element_type=jnp.float32
    )
    return (attended, grad_query, grad_key, grad_value, (highest, weight_total, inner))


def local(queries, keys, values, grad_out, rand_blocks, global_ids):
    tok_rows, width = queries.shape
    block_count = tok_rows // BLOCK
    listed = 3 + GLOBALS + RAND
    ctx_count = lax.axis_size("ctx")
    position = lax.axis_index("ctx")
    top_bit = ctx_count.bit_length() - 1
    block_iota = jnp.arange(block_count, dtype=jnp.int32)
    stacked = jnp.stack([keys, values])
    padded = padded_2(stacked, (("ctx", 1),), BLOCK)
    framed = padded.reshape(2, block_count + 2, BLOCK, width)
    window = jnp.concatenate([framed[:, :-2], framed[:, 1:-1], framed[:, 2:]], axis=2)
    owners = global_ids // block_count
    local_ids = global_ids % block_count
    own_pieces = jnp.stack(
        [
            lax.dynamic_slice_in_dim(stacked, local_ids[global_slot] * BLOCK, BLOCK, 1)
            for global_slot in range(GLOBALS)
        ],
        axis=1,
    )
    fetched = jnp.stack(
        [
            from_root(own_pieces[:, global_slot], "ctx", owners[global_slot])
            for global_slot in range(GLOBALS)
        ],
        axis=1,
    )
    global_part = jnp.broadcast_to(
        fetched.reshape(2, 1, GLOBALS * BLOCK, width), (2, block_count, GLOBALS * BLOCK, width)
    )
    pickers = []
    random_parts = []
    for matching in range(RAND):
        spread_bit = top_bit - 1 - matching
        picker = (rand_blocks[:, matching][:, None] == block_iota[None, :]).astype(jnp.bfloat16)
        partner = partner_2(stacked, "ctx", spread_bit).reshape(2, block_count, BLOCK, width)
        chosen = jnp.einsum(
            "jb,sbqd->sjqd", picker, partner, preferred_element_type=jnp.float32
        ).astype(jnp.bfloat16)
        pickers.append(picker)
        random_parts.append(chosen)
    every_key = jnp.concatenate([window, global_part] + random_parts, axis=2)
    key_blocks = every_key[0].reshape(block_count, listed * BLOCK, HEADS, HEAD_DIM)
    value_blocks = every_key[1].reshape(block_count, listed * BLOCK, HEADS, HEAD_DIM)
    global_block = position * block_count + block_iota
    seq_blocks = block_count * ctx_count
    left_ok = global_block > 0
    right_ok = global_block < seq_blocks - 1
    key_valid = jnp.concatenate(
        [
            jnp.broadcast_to(left_ok[:, None], (block_count, BLOCK)),
            jnp.ones((block_count, BLOCK), dtype=bool),
            jnp.broadcast_to(right_ok[:, None], (block_count, BLOCK)),
            jnp.ones((block_count, (GLOBALS + RAND) * BLOCK), dtype=bool),
        ],
        axis=1,
    )
    query_blocks = queries.reshape(block_count, BLOCK, HEADS, HEAD_DIM)
    grad_blocks = grad_out.reshape(block_count, BLOCK, HEADS, HEAD_DIM)
    attended, grad_query, grad_key, grad_value, softmax_stats = attend_blocks(
        query_blocks, key_blocks, value_blocks, grad_blocks, key_valid
    )
    split = jnp.stack([grad_key, grad_value]).reshape(2, block_count, listed, BLOCK, width)
    own_window = (
        jnp.pad(split[:, :, 0], ((0, 0), (0, 2), (0, 0), (0, 0)))
        + jnp.pad(split[:, :, 1], ((0, 0), (1, 1), (0, 0), (0, 0)))
        + jnp.pad(split[:, :, 2], ((0, 0), (2, 0), (0, 0), (0, 0)))
    )
    from_right = passed_along(own_window[:, 0], "ctx", -1)
    from_left = passed_along(own_window[:, -1], "ctx", 1)
    own_total = own_window[:, 1:-1]
    own_total = own_total.at[:, -1].add(from_right)
    own_total = own_total.at[:, 0].add(from_left)
    for matching in range(RAND):
        spread_bit = top_bit - 1 - matching
        terms = split[:, :, 3 + GLOBALS + matching]
        routed = jnp.einsum(
            "jb,sjqd->sbqd",
            pickers[matching].astype(jnp.float32),
            terms,
            precision=lax.Precision.HIGHEST,
        )
        own_total = own_total + partner_2(routed, "ctx", spread_bit)
    attended_out = attended.reshape(tok_rows, width).astype(jnp.bfloat16)
    grad_queries = grad_query.reshape(tok_rows, width).astype(jnp.bfloat16)
    grad_keys = own_total[0].reshape(tok_rows, width).astype(jnp.bfloat16)
    grad_values = own_total[1].reshape(tok_rows, width).astype(jnp.bfloat16)
    return (attended_out, grad_queries, grad_keys, grad_values)


def solution(mesh):
    placed = (
        P(("dp", "ctx"), None),
        P(("dp", "ctx"), None),
        P(("dp", "ctx"), None),
        P(("dp", "ctx"), None),
        P(("dp", "ctx"), None),
        P("dp"),
    )
    return jax.shard_map(
        local,
        mesh=mesh,
        in_specs=placed,
        out_specs=(
            P(("dp", "ctx"), None),
            P(("dp", "ctx"), None),
            P(("dp", "ctx"), None),
            P(("dp", "ctx"), None),
        ),
        check_vma=False,
    )
```

profile of v0, /device:TPU:192, one launch (start us, length us, event | category | flops | bytes accessed | tf_op | source)
XLA Modules:
  0.0 455.0 jit_solution(9011491721710918860)
XLA Ops:
  7.3 1.9 pad_maximum_fusion.2
  9.2 3.2 collective-permute-start.4
  12.4 1.5 collective-permute-start.2
  13.8 1.0 collective-permute-start.3
  14.9 0.7 and_select_fusion.1
  15.5 0.6 fusion.55
  18.7 2.2 fusion.34
  20.9 1.9 collective-permute-start
  22.9 5.8 %collective-permute-start.1 = (bf16[2,64,1024]{2,1,0:T(8,128)(2,1)S(1)}, bf16[2,64,1024]{2,1,0:T(8,128)(2,1)S(1)}, u32[]{:S(2)}, u32[]{:S(2)}) collective-permute-start(bf16[2,64,1024]{2,1,0:T(8,128)(2,1)S(1)} %get-tuple-element.48), channel_id=1, source_target_pairs={{1,0},{2,1},{3,2},{4,3},{5,4},{6,5},{7,6},{8,7},{9,8},{10,9},{11,1... | collective-permute-start | bytes 786440 | tf_op jit(solution)/shard_map/ppermute | solution.py:24
  28.8 1.3 reshape.131
  30.2 1.3 copy.49
  31.8 1.3 copy.51
  33.5 7.5 %collective-permute-done = bf16[2,64,1024]{2,1,0:T(8,128)(2,1)S(1)} collective-permute-done((bf16[2,64,1024]{2,1,0:T(8,128)(2,1)S(1)}, bf16[2,64,1024]{2,1,0:T(8,128)(2,1)S(1)}, u32[]{:S(2)}, u32[]{:S(2)}) %collective-permute-start) | collective-permute-done | bytes 262176 | tf_op jit(solution)/shard_map/ppermute | solution.py:23
  41.1 1.0 fusion.53
  42.6 0.5 copy.76
  43.1 1.5 copy.75
  44.6 2.6 fusion.15
  47.2 2.3 copy.44
  49.5 2.6 fusion.13
  52.1 2.3 copy.42
  54.4 2.6 fusion.14
  57.0 2.3 copy.43
  59.3 220.8 %all-reduce.6.cloned.1.call-done = (bf16[2,1,64,1024]{3,2,1,0:T(8,128)(2,1)}, bf16[2,1,64,1024]{3,2,0,1:T(8,128)(2,1)}) async-done(((bf16[2,1,64,1024]{3,2,1,0:T(8,128)(2,1)}, bf16[2,1,64,1024]{3,2,0,1:T(8,128)(2,1)}), (bf16[2,1,64,1024]{3,2,1,0:T(8,128)(2,1)}, bf16[2,1,64,1024]{3,2,0,1:T(8,128)(2,1)})) %all-reduce.6.cloned.1.call-update) | async-done | bytes 524304 | tf_op jit(solution)/shard_map/psum | solution.py:31
  280.1 1.9 pad_maximum_fusion.3
  282.0 2.1 copy.35
  284.0 2.2 broadcast_in_dim.25
  286.3 10.3 %concatenate.15 = bf16[2,2,512,1024]{2,3,1,0:T(8,128)(2,1)} concatenate(bf16[2,2,64,1024]{2,3,1,0:T(8,128)(2,1)S(1)} %copy.75, bf16[2,2,64,1024]{2,3,1,0:T(8,128)(2,1)S(1)} %copy.76, bf16[2,2,64,1024]{2,3,1,0:T(8,128)(2,1)S(1)} %copy.77, bf16[2,2,128,1024]{2,3,1,0:T(8,128)(2,1)} %broadcast_in_dim.25, bf16[2,2,64,1024]{2,3,1,0:T(8,128)(2,1)} %copy.42, ...), dimensions={2} | concatenate | bytes 8388608 | tf_op jit(solution)/shard_map/concatenate | solution.py:118
  296.6 4.0 fusion.51
  300.6 3.4 fusion.57
  304.0 5.0 %convolution_bitcast_fusion = f32[2,512,16,64]{1,3,2,0:T(8,128)} fusion(bf16[2,64,16,64]{1,3,2,0:T(8,128)(2,1)S(1)} %copy-done.10, f32[2,16,64,512]{3,2,1,0:T(8,128)} %get-tuple-element.57, f32[2,16,64]{2,1,0:T(8,128)S(1)} %get-tuple-element.56), kind=kOutput, calls=%fused_computation.11 | convolution fusion | flops 136314880 | bytes 8658944 | tf_op jit(solution)/shard_map/jhqk,jqhd->jkhd/dot_general | solution.py:70
  309.0 1.3 fusion.1
  310.3 1.0 fusion.3
  311.3 2.6 convolution_bitcast_fusion.1
  313.9 7.1 %reshape.141 = f32[1,2,8,64,1024]{3,2,4,1,0:T(8,128)} reshape(f32[2,512,16,64]{1,3,2,0:T(8,128)} %convolution_bitcast_fusion.1) | data formatting | bytes 8388608 | tf_op jit(solution)/shard_map/stack | solution.py:139
  321.0 8.6 %copy.53 = f32[1,2,8,64,1024]{4,1,3,0,2:T(2,128)} copy(f32[1,2,8,64,1024]{3,2,4,1,0:T(8,128)} %reshape.141) | data formatting | bytes 8388608 | tf_op jit(solution)/shard_map/stack | solution.py:139
  329.6 7.1 %reshape.142 = f32[1,2,8,64,1024]{3,2,4,1,0:T(8,128)} reshape(f32[2,512,16,64]{1,3,2,0:T(8,128)} %convolution_bitcast_fusion) | data formatting | bytes 8388608 | tf_op jit(solution)/shard_map/stack | solution.py:139
  336.7 8.6 %copy.54 = f32[1,2,8,64,1024]{4,1,3,0,2:T(2,128)} copy(f32[1,2,8,64,1024]{3,2,4,1,0:T(8,128)} %reshape.142) | data formatting | bytes 8388608 | tf_op jit(solution)/shard_map/stack | solution.py:139
  345.4 3.6 fusion.20
  349.2 2.3 fusion.19
  351.5 2.3 fusion.21
  353.8 1.7 maximum_bitcast_fusion.4
  355.5 1.3 copy.96
  356.8 1.3 copy.97
  358.1 1.3 copy.95
  359.4 1.3 pad_add_fusion
  360.7 2.1 fusion.52
  362.8 0.9 copy.98
  363.7 5.9 %collective-permute-start.5 = (f32[2,64,1024]{2,1,0:T(8,128)}, f32[2,64,1024]{2,1,0:T(8,128)}, u32[]{:S(2)}, u32[]{:S(2)}) collective-permute-start(f32[2,64,1024]{2,1,0:T(8,128)} %bitcast.131), channel_id=1, source_target_pairs={{1,0},{2,1},{3,2},{4,3},{5,4},{6,5},{7,6},{8,7},{9,8},{10,9},{11,1... | collective-permute-start | bytes 1572872 | tf_op jit(solution)/shard_map/ppermute | solution.py:41
  369.6 2.1 collective-permute-start.9
  371.7 21.1 %collective-permute-start.7 = (f32[2,2,64,1024]{3,2,0,1:T(8,128)}, f32[2,2,64,1024]{3,2,0,1:T(8,128)}, u32[]{:S(2)}, u32[]{:S(2)}) collective-permute-start(f32[2,2,64,1024]{3,2,0,1:T(8,128)} %bitcast.130), channel_id=1, source_target_pairs={{0,16},{1,17},{2,18},{3,19},{4,20},{5,21},{6,22},{7,23},{8,24},{9,... | collective-permute-start | bytes 3145736 | tf_op jit(solution)/shard_map/ppermute | solution.py:35
  392.8 1.6 fusion.11
  394.4 0.5 slice.168
  395.0 2.3 copy.46
  397.2 2.1 convert_element_type.71
  399.3 2.0 copy.99
  401.3 2.7 collective-permute-start.6
  404.1 3.1 fusion.12
  407.2 1.5 copy.48
  408.7 1.1 convert_element_type.75
  410.1 1.3 fusion.24
  411.4 32.6 %collective-permute-done.6 = f32[2,64,1024]{2,1,0:T(8,128)} collective-permute-done((f32[2,64,1024]{2,1,0:T(8,128)}, f32[2,64,1024]{2,1,0:T(8,128)}, u32[]{:S(2)}, u32[]{:S(2)}) %collective-permute-start.6) | collective-permute-done | bytes 524320 | tf_op jit(solution)/shard_map/ppermute | solution.py:41
  443.9 1.2 fusion.23
  445.2 2.2 add_convert_fusion
  447.4 0.8 fusion.54
  (50 shorter events, 2.0 us)
Async XLA Ops:
  7.2 33.9 %copy-start.6 = (bf16[128,1024]{1,0:T(8,128)(2,1)S(1)}, bf16[128,1024]{1,0:T(8,128)(2,1)}, u32[]{:S(2)}) copy-start(bf16[128,1024]{1,0:T(8,128)(2,1)} %param.12) | copy-start | bytes 786436
  7.2 33.8 %copy-start.5 = (bf16[128,1024]{1,0:T(8,128)(2,1)S(1)}, bf16[128,1024]{1,0:T(8,128)(2,1)}, u32[]{:S(2)}) copy-start(bf16[128,1024]{1,0:T(8,128)(2,1)} %param.11) | copy-start | bytes 786436
  7.2 24.3 %copy-start.11 = (bf16[128,1024]{1,0:T(8,128)(2,1)S(1)}, bf16[128,1024]{1,0:T(8,128)(2,1)}, u32[]{:S(2)}) copy-start(bf16[128,1024]{1,0:T(8,128)(2,1)} %param.13) | copy-start | bytes 786436
  7.2 26.1 %copy-start.12 = (s32[2,3]{1,0:T(2,128)S(1)}, s32[2,3]{1,0:T(2,128)}, u32[]{:S(2)}) copy-start(s32[2,3]{1,0:T(2,128)} %param.14) | copy-start | bytes 76
  7.2 272.9 %all-reduce.6.cloned.1.call-start = ((), (), s32[]{:S(2)}) async-start(), calls=%async_computation | async-start | bytes 1048576 | tf_op jit(solution)/shard_map/psum | solution.py:31
  9.2 35.4 %collective-permute-start.4 = (bf16[2,128,1024]{2,1,0:T(8,128)(2,1)}, bf16[2,128,1024]{2,1,0:T(8,128)(2,1)}, u32[]{:S(2)}, u32[]{:S(2)}) collective-permute-start(bf16[2,128,1024]{2,1,0:T(8,128)(2,1)} %pad_maximum_fusion.2), channel_id=1, source_target_pairs={{0,4},{1,5},{2,6},{3,7},{4,0},{5,1},{6,2},{7,3},{8,12},{9,13},{10,... | collective-permute-start | bytes 1572872 | tf_op jit(solution)/shard_map/ppermute | solution.py:35
  12.4 37.1 %collective-permute-start.2 = (bf16[2,128,1024]{2,1,0:T(8,128)(2,1)}, bf16[2,128,1024]{2,1,0:T(8,128)(2,1)}, u32[]{:S(2)}, u32[]{:S(2)}) collective-permute-start(bf16[2,128,1024]{2,1,0:T(8,128)(2,1)} %pad_maximum_fusion.2), channel_id=1, source_target_pairs={{0,16},{1,17},{2,18},{3,19},{4,20},{5,21},{6,22},{7,23},{8,24},{9,... | collective-permute-start | bytes 1572872 | tf_op jit(solution)/shard_map/ppermute | solution.py:35
  13.8 40.6 %collective-permute-start.3 = (bf16[2,128,1024]{2,1,0:T(8,128)(2,1)}, bf16[2,128,1024]{2,1,0:T(8,128)(2,1)}, u32[]{:S(2)}, u32[]{:S(2)}) collective-permute-start(bf16[2,128,1024]{2,1,0:T(8,128)(2,1)} %pad_maximum_fusion.2), channel_id=1, source_target_pairs={{0,8},{1,9},{2,10},{3,11},{4,12},{5,13},{6,14},{7,15},{8,0},{9,1},... | collective-permute-start | bytes 1572872 | tf_op jit(solution)/shard_map/ppermute | solution.py:35
  20.9 20.1 %collective-permute-start = (bf16[2,64,1024]{2,1,0:T(8,128)(2,1)S(1)}, bf16[2,64,1024]{2,1,0:T(8,128)(2,1)S(1)}, u32[]{:S(2)}, u32[]{:S(2)}) collective-permute-start(bf16[2,64,1024]{2,1,0:T(8,128)(2,1)S(1)} %get-tuple-element.47), channel_id=1, source_target_pairs={{0,1},{1,2},{2,3},{3,4},{4,5},{5,6},{6,7},{7,8},{8,9},{9,10},{10,1... | collective-permute-start | bytes 786440 | tf_op jit(solution)/shard_map/ppermute | solution.py:23
  22.9 18.2 %collective-permute-start.1 = (bf16[2,64,1024]{2,1,0:T(8,128)(2,1)S(1)}, bf16[2,64,1024]{2,1,0:T(8,128)(2,1)S(1)}, u32[]{:S(2)}, u32[]{:S(2)}) collective-permute-start(bf16[2,64,1024]{2,1,0:T(8,128)(2,1)S(1)} %get-tuple-element.48), channel_id=1, source_target_pairs={{1,0},{2,1},{3,2},{4,3},{5,4},{6,5},{7,6},{8,7},{9,8},{10,9},{11,1... | collective-permute-start | bytes 786440 | tf_op jit(solution)/shard_map/ppermute | solution.py:24
  296.6 4.0 copy-start.9
  300.6 8.4 %copy-start.2 = (bf16[1,2,512,1024]{2,3,1,0:T(8,128)(2,1)}, bf16[1,2,512,1024]{2,3,1,0:T(8,128)(2,1)S(1)}, u32[]{:S(2)}) copy-start(bf16[1,2,512,1024]{2,3,1,0:T(8,128)(2,1)S(1)} %get-tuple-element.36) | copy-start | bytes 6291460
  300.6 3.4 copy-start.10
  304.0 5.0 %copy-start.3 = (f32[2,16,64,512]{3,2,1,0:T(8,128)S(1)}, f32[2,16,64,512]{3,2,1,0:T(8,128)}, u32[]{:S(2)}) copy-start(f32[2,16,64,512]{3,2,1,0:T(8,128)} %get-tuple-element.57) | copy-start | bytes 12582916
  304.0 5.0 %copy-start.7 = (bf16[1,2,512,1024]{2,3,1,0:T(8,128)(2,1)S(1)}, bf16[1,2,512,1024]{2,3,1,0:T(8,128)(2,1)}, u32[]{:S(2)}) copy-start(bf16[1,2,512,1024]{2,3,1,0:T(8,128)(2,1)} %get-tuple-element.37) | copy-start | bytes 6291460
  345.4 3.6 copy-start
  345.4 3.8 copy-start.1
  359.4 33.4 %copy-start.4 = (f32[2,16,64,512]{3,2,1,0:T(8,128)S(1)}, f32[2,16,64,512]{3,2,1,0:T(8,128)}, u32[]{:S(2)}) copy-start(f32[2,16,64,512]{3,2,1,0:T(8,128)} %get-tuple-element.57) | copy-start | bytes 12582916
  359.4 33.4 %copy-start.8 = (bf16[1,2,512,1024]{2,3,1,0:T(8,128)(2,1)S(1)}, bf16[1,2,512,1024]{2,3,1,0:T(8,128)(2,1)}, u32[]{:S(2)}) copy-start(bf16[1,2,512,1024]{2,3,1,0:T(8,128)(2,1)} %get-tuple-element.37) | copy-start | bytes 6291460
  363.7 46.4 %collective-permute-start.5 = (f32[2,64,1024]{2,1,0:T(8,128)}, f32[2,64,1024]{2,1,0:T(8,128)}, u32[]{:S(2)}, u32[]{:S(2)}) collective-permute-start(f32[2,64,1024]{2,1,0:T(8,128)} %bitcast.131), channel_id=1, source_target_pairs={{1,0},{2,1},{3,2},{4,3},{5,4},{6,5},{7,6},{8,7},{9,8},{10,9},{11,1... | collective-permute-start | bytes 1572872 | tf_op jit(solution)/shard_map/ppermute | solution.py:41
  369.6 75.6 %collective-permute-start.9 = (f32[2,2,64,1024]{3,2,0,1:T(8,128)}, f32[2,2,64,1024]{3,2,0,1:T(8,128)}, u32[]{:S(2)}, u32[]{:S(2)}) collective-permute-start(f32[2,2,64,1024]{3,2,0,1:T(8,128)} %bitcast.128), channel_id=1, source_target_pairs={{0,4},{1,5},{2,6},{3,7},{4,0},{5,1},{6,2},{7,3},{8,12},{9,13},{10,... | collective-permute-start | bytes 3145736 | tf_op jit(solution)/shard_map/ppermute | solution.py:35
  371.7 73.5 %collective-permute-start.7 = (f32[2,2,64,1024]{3,2,0,1:T(8,128)}, f32[2,2,64,1024]{3,2,0,1:T(8,128)}, u32[]{:S(2)}, u32[]{:S(2)}) collective-permute-start(f32[2,2,64,1024]{3,2,0,1:T(8,128)} %bitcast.130), channel_id=1, source_target_pairs={{0,16},{1,17},{2,18},{3,19},{4,20},{5,21},{6,22},{7,23},{8,24},{9,... | collective-permute-start | bytes 3145736 | tf_op jit(solution)/shard_map/ppermute | solution.py:35
  392.8 52.4 %collective-permute-start.8 = (f32[2,2,64,1024]{3,2,0,1:T(8,128)}, f32[2,2,64,1024]{3,2,0,1:T(8,128)}, u32[]{:S(2)}, u32[]{:S(2)}) collective-permute-start(f32[2,2,64,1024]{3,2,0,1:T(8,128)} %bitcast.129), channel_id=1, source_target_pairs={{0,8},{1,9},{2,10},{3,11},{4,12},{5,13},{6,14},{7,15},{8,0},{9,1},... | collective-permute-start | bytes 3145736 | tf_op jit(solution)/shard_map/ppermute | solution.py:35
  401.3 42.6 %collective-permute-start.6 = (f32[2,64,1024]{2,1,0:T(8,128)}, f32[2,64,1024]{2,1,0:T(8,128)}, u32[]{:S(2)}, u32[]{:S(2)}) collective-permute-start(f32[2,64,1024]{2,1,0:T(8,128)} %bitcast.132), channel_id=1, source_target_pairs={{0,1},{1,2},{2,3},{3,4},{4,5},{5,6},{6,7},{7,8},{8,9},{9,10},{10,1... | collective-permute-start | bytes 1572872 | tf_op jit(solution)/shard_map/ppermute | solution.py:41
Sparse Core Ops, SparseCore 0:
  28.8 251.2 all-reduce.5
where the time goes:
time: 461 us; the launch traced here: 455 us
  waiting for transfers between devices  261 us (57%)
  local copies, waits for them, and re-layouts  83.4 us (18%)
  starting transfers between devices  45.2 us (10%)
  matrix products  33.2 us (7%)
  between operations  16.9 us (4%)
  other arithmetic  15.4 us (3%)
    psum x1, waiting for transfers between devices, from_root(): return lax.psum(block, axis)  221 us
    ppermute x2, waiting for transfers between devices, passed_along(): return lax.ppermute(array, axis, pairs)  32.6 us
    another operation x4, local copies, waits for them, and re-layouts, local(): jnp.stack([grad_key, grad_value])  31.5 us
    ppermute x6, starting transfers between devices, partner_2(): lax.ppermute(array, axis, [(i, i ^ 1 << distance) for i in range(lax.axis...  28.9 us
    concatenate x1, local copies, waits for them, and re-layouts, local(): every_key = jnp.concatenate([window, global_part] + random_parts, axis=2)  10.3 us
  transfers between devices with their start and end apart: 11, of which 3 were waited for; matrix products, arithmetic and copies ran while one was open for 10% of the time, Pallas kernels for 0%

commit v1 on v0

--- a/solution.py
+++ b/solution.py
@@ -26,9 +26,16 @@
     return array
 
 
-def from_root(block, axis, source):
-    block = jnp.where(lax.axis_index(axis) == source, block, jnp.zeros_like(block))
-    return lax.psum(block, axis)
+def from_root(blocks, axis, sources):
+    size = lax.axis_size(axis)
+    position = lax.axis_index(axis)
+    shape = (-1,) + (1,) * (blocks.ndim - 1)
+    for level in range(size.bit_length() - 1):
+        step = 1 << level
+        received = lax.ppermute(blocks, axis, [(i, i ^ step) for i in range(size)])
+        partner_holds = ((position ^ step) >> level) == (sources >> level)
+        blocks = jnp.where(partner_holds.reshape(shape), received, blocks)
+    return blocks
 
 
 def partner_2(array, axis, distance):
@@ -94,13 +101,7 @@
         ],
         axis=1,
     )
-    fetched = jnp.stack(
-        [
-            from_root(own_pieces[:, global_slot], "ctx", owners[global_slot])
-            for global_slot in range(GLOBALS)
-        ],
-        axis=1,
-    )
+    fetched = jnp.swapaxes(from_root(jnp.swapaxes(own_pieces, 0, 1), "ctx", owners), 0, 1)
     global_part = jnp.broadcast_to(
         fetched.reshape(2, 1, GLOBALS * BLOCK, width), (2, block_count, GLOBALS * BLOCK, width)
     )
@@ -108,11 +109,11 @@
     random_parts = []
     for matching in range(RAND):
         spread_bit = top_bit - 1 - matching
-        picker = (rand_blocks[:, matching][:, None] == block_iota[None, :]).astype(jnp.bfloat16)
+        picker = rand_blocks[:, matching][:, None] == block_iota[None, :]
         partner = partner_2(stacked, "ctx", spread_bit).reshape(2, block_count, BLOCK, width)
-        chosen = jnp.einsum(
-            "jb,sbqd->sjqd", picker, partner, preferred_element_type=jnp.float32
-        ).astype(jnp.bfloat16)
+        chosen = jnp.broadcast_to(partner[:, :1], (2, block_count, BLOCK, width))
+        for b in range(1, block_count):
+            chosen = jnp.where(picker[None, :, b, None, None], partner[:, b : b + 1], chosen)
         pickers.append(picker)
         random_parts.append(chosen)
     every_key = jnp.concatenate([window, global_part] + random_parts, axis=2)
@@ -150,11 +151,9 @@
     for matching in range(RAND):
         spread_bit = top_bit - 1 - matching
         terms = split[:, :, 3 + GLOBALS + matching]
-        routed = jnp.einsum(
-            "jb,sjqd->sbqd",
-            pickers[matching].astype(jnp.float32),
-            terms,
-            precision=lax.Precision.HIGHEST,
+        routed = sum(
+            jnp.where(pickers[matching][None, j, :, None, None], terms[:, j : j + 1], 0.0)
+            for j in range(block_count)
         )
         own_total = own_total + partner_2(routed, "ctx", spread_bit)
     attended_out = attended.reshape(tok_rows, width).astype(jnp.bfloat16)

time: 461 us -> 237 us (0.51)
  waiting for transfers between devices: 261 us -> 94.5 us
  starting transfers between devices: 45.2 us -> 21.2 us
  between operations: 16.9 us -> 2.33 us
  matrix products: 33.2 us -> 18.8 us
  local copies, waits for them, and re-layouts: 83.4 us -> 71.4 us
  other arithmetic: 15.4 us -> 26.8 us
    psum x1 -> x0, waiting for transfers between devices: 221 us -> none  [from_root(): return lax.psum(block, axis)]
    ppermute x0 -> x5, waiting for transfers between devices: none -> 47.5 us  [from_root(): received = lax.ppermute(blocks, axis, [(i, i ^ step) for i in range(size)])]
    ppermute x6, starting transfers between devices: 28.9 us -> 9.23 us  [partner_2(): lax.ppermute(array, axis, [(i, i ^ 1 << distance) for i in range(lax.axis...]
    dot_general x6 -> x0, matrix products: 16.1 us -> none  [the longest x3 8.28 us: local(): jnp.einsum('jb,sjqd->sbqd', pickers[matching].astype(jnp.float32), terms,...]
    convert_element_type x3 -> x0, local copies, waits for them, and re-layouts: 6.86 us -> none  [local(): chosen = jnp.einsum('jb,sbqd->sjqd', picker, partner, preferred_element_t...]
    ppermute x2, waiting for transfers between devices: 32.6 us -> 38.2 us  [passed_along(): return lax.ppermute(array, axis, pairs)]
    broadcast_in_dim x0 -> x15, local copies, waits for them, and re-layouts: none -> 5.6 us  [the longest x6 3.8 us: local(): jnp.where(picker[None, :, b, None, None], partner[:, b:b + 1], chosen)]
    select_n x1 -> x9, other arithmetic: 0.66 us -> 5.6 us  [the longest x5 4.45 us: from_root(): blocks = jnp.where(partner_holds.reshape(shape), received, blocks)]
  transfers between devices with their start and end apart: 11 -> 15, of which waited for: 3 -> 6; matrix products, arithmetic and copies ran while one was open for 10% -> 18% of each run, Pallas kernels for 0% -> 0%
where the time goes in v1:
time: 237 us; the launch traced here: 235 us
  waiting for transfers between devices  94.5 us (40%)
  local copies, waits for them, and re-layouts  71.4 us (30%)
  other arithmetic  26.8 us (11%)
  starting transfers between devices  21.2 us (9%)
  matrix products  18.8 us (8%)
    ppermute x5, waiting for transfers between devices, from_root(): received = lax.ppermute(blocks, axis, [(i, i ^ step) for i in range(size)])  47.5 us
    ppermute x2, waiting for transfers between devices, passed_along(): return lax.ppermute(array, axis, pairs)  38.2 us
    another operation x4, local copies, waits for them, and re-layouts, local(): jnp.stack([grad_key, grad_value])  27.9 us
    concatenate x1, local copies, waits for them, and re-layouts, local(): every_key = jnp.concatenate([window, global_part] + random_parts, axis=2)  9.59 us
    ppermute x6, starting transfers between devices, partner_2(): lax.ppermute(array, axis, [(i, i ^ 1 << distance) for i in range(lax.axis...  9.23 us
    ppermute x1, waiting for transfers between devices, padded_2(): before = lax.ppermute(last, axis, up)  8.69 us
    dot_general x1, matrix products, attend_blocks(): jnp.einsum('jhqk,jqhd->jkhd', probs_low, grad_blocks, preferred_element_t...  5.05 us
  transfers between devices with their start and end apart: 15, of which 6 were waited for; matrix products, arithmetic and copies ran while one was open for 18% of the time, Pallas kernels for 0%

profile of v1, /device:TPU:192, one launch (start us, length us, event | category | flops | bytes accessed | tf_op | source)
XLA Modules:
  0.0 235.1 jit_solution(12832006468362301961)
XLA Ops:
  0.7 1.9 pad_maximum_fusion.2
  2.6 1.5 collective-permute-start.7
  4.0 1.0 collective-permute-start.8
  5.0 3.2 %collective-permute-start.9 = (bf16[2,128,1024]{2,1,0:T(8,128)(2,1)}, bf16[2,128,1024]{2,1,0:T(8,128)(2,1)}, u32[]{:S(2)}, u32[]{:S(2)}) collective-permute-start(bf16[2,128,1024]{2,1,0:T(8,128)(2,1)} %pad_maximum_fusion.2), channel_id=1, source_target_pairs={{0,4},{1,5},{2,6},{3,7},{4,0},{5,1},{6,2},{7,3},{8,12},{9,13},{10,... | collective-permute-start | bytes 1572872 | tf_op jit(solution)/shard_map/ppermute | solution.py:42
  8.2 0.7 and_select_fusion
  8.9 0.6 fusion.34
  10.8 2.2 fusion.24
  13.0 2.0 collective-permute-start.1
  15.6 1.0 slice_reduce_fusion.3
  17.3 1.3 reshape.150
  18.6 1.3 copy.44
  20.3 1.3 copy.46
  22.0 0.8 collective-permute-start.3
  22.9 13.1 %collective-permute-done.3 = bf16[2,2,64,1024]{3,2,0,1:T(8,128)(2,1)S(1)} collective-permute-done((bf16[2,2,64,1024]{3,2,0,1:T(8,128)(2,1)S(1)}, bf16[2,2,64,1024]{3,2,0,1:T(8,128)(2,1)S(1)}, u32[]{:S(2)}, u32[]{:S(2)}) %collective-permute-start.3) | collective-permute-done | bytes 524320 | tf_op jit(solution)/shard_map/ppermute | solution.py:35
  36.0 1.9 collective-permute-start
  38.1 1.3 collective-permute-start.4
  39.4 8.7 %collective-permute-done = bf16[2,64,1024]{2,1,0:T(8,128)(2,1)S(1)} collective-permute-done((bf16[2,64,1024]{2,1,0:T(8,128)(2,1)}, bf16[2,64,1024]{2,1,0:T(8,128)(2,1)S(1)}, u32[]{:S(2)}, u32[]{:S(2)}) %collective-permute-start) | collective-permute-done | bytes 262176 | tf_op jit(solution)/shard_map/ppermute | solution.py:23
  48.1 1.0 pad_maximum_fusion.1
  49.3 1.4 copy.55
  50.7 1.3 copy.56
  52.0 1.3 copy.57
  53.3 1.1 slice_bitcast_fusion.14
  54.4 1.9 collective-permute-done.4
  56.3 2.0 broadcast_select_fusion.5
  59.7 1.1 slice_bitcast_fusion.10
  60.8 1.0 copy.39
  61.8 1.1 copy.38
  63.0 10.2 %collective-permute-done.5 = bf16[2,2,64,1024]{3,2,0,1:T(8,128)(2,1)} collective-permute-done((bf16[2,2,64,1024]{3,2,0,1:T(8,128)(2,1)}, bf16[2,2,64,1024]{3,2,0,1:T(8,128)(2,1)}, u32[]{:S(2)}, u32[]{:S(2)}) %collective-permute-start.5) | collective-permute-done | bytes 524320 | tf_op jit(solution)/shard_map/ppermute | solution.py:35
  73.3 1.3 broadcast_select_fusion.6
  74.6 0.6 collective-permute-start.6
  75.5 22.3 %collective-permute-done.6 = bf16[2,2,64,1024]{3,2,0,1:T(8,128)(2,1)S(1)} collective-permute-done((bf16[2,2,64,1024]{3,2,0,1:T(8,128)(2,1)S(1)}, bf16[2,2,64,1024]{3,2,0,1:T(8,128)(2,1)S(1)}, u32[]{:S(2)}, u32[]{:S(2)}) %collective-permute-start.6) | collective-permute-done | bytes 524320 | tf_op jit(solution)/shard_map/ppermute | solution.py:35
  97.9 0.9 broadcast_select_fusion.7
  98.8 2.0 copy.33
  100.8 2.3 broadcast_in_dim.246
  103.1 9.6 %concatenate.15 = bf16[2,2,512,1024]{2,3,1,0:T(8,128)(2,1)} concatenate(bf16[2,2,64,1024]{2,3,1,0:T(8,128)(2,1)} %copy.55, bf16[2,2,64,1024]{2,3,1,0:T(8,128)(2,1)} %copy.56, bf16[2,2,64,1024]{2,3,1,0:T(8,128)(2,1)} %copy.57, bf16[2,2,128,1024]{2,3,1,0:T(8,128)(2,1)} %broadcast_in_dim.246, bf16[2,2,64,1024]{2,3,1,0:T(8,128)(2,1)S(1)} %broadcast_select_fusion.2, ...), dimensions={2} | concatenate | bytes 8388608 | tf_op jit(solution)/shard_map/concatenate | solution.py:119
  112.7 4.1 %fusion.31 = (bf16[1,2,512,1024]{2,3,1,0:T(8,128)(2,1)S(1)}, bf16[1,2,512,1024]{2,3,1,0:T(8,128)(2,1)}) fusion(bf16[2,2,512,1024]{2,3,1,0:T(8,128)(2,1)} %concatenate.15), kind=kLoop, calls=%fused_computation.111 | loop fusion | bytes 8388608 | tf_op jit(solution)/shard_map/slice | solution.py:120
  116.8 3.4 %fusion.35 = (f32[2,16,64]{2,1,0:T(8,128)S(1)}, f32[2,16,64,512]{3,2,1,0:T(8,128)}) fusion(pred[2,512]{1,0:T(4,128)(4,1)S(1)} %add_add_fusion, bf16[2,64,16,64]{1,3,2,0:T(8,128)(2,1)S(1)} %copy-done.10, bf16[2,512,16,64]{1,3,2,0:T(8,128)(2,1)S(1)} %bitcast.145), kind=kOutput, calls=%fused_computation.115 | convolution fusion | flops 138412544 | bytes 6562816 | tf_op jit(solution)/shard_map/sub | solution.py:59
  120.2 5.0 %convolution_bitcast_fusion = f32[2,512,16,64]{1,3,2,0:T(8,128)} fusion(bf16[2,64,16,64]{1,3,2,0:T(8,128)(2,1)S(1)} %copy-done.11, f32[2,16,64,512]{3,2,1,0:T(8,128)} %get-tuple-element.77, f32[2,16,64]{2,1,0:T(8,128)S(1)} %get-tuple-element.76), kind=kOutput, calls=%fused_computation.11 | convolution fusion | flops 136314880 | bytes 8658944 | tf_op jit(solution)/shard_map/jhqk,jqhd->jkhd/dot_general | solution.py:77
  125.2 3.0 %fusion.1 = (f32[2,16,64]{2,1,0:T(8,128)S(1)}, f32[2,16,512,64]{2,3,1,0:T(8,128)}) fusion(f32[2,16,64,512]{3,2,1,0:T(8,128)S(1)} %copy-done.2, f32[2,16,64]{2,1,0:T(8,128)S(1)} %get-tuple-element.76, bf16[2,64,16,64]{1,3,2,0:T(8,128)(2,1)S(1)} %copy-done.11, bf16[2,512,16,64]{1,3,2,0:T(8,128)(2,1)S(1)} %bitcast.155), kind=kOutput, calls=%fused_computation.3 | convolution fusion | flops 137361408 | bytes 10764288 | tf_op jit(solution)/shard_map/jqhd,jkhd->jhqk/dot_general | solution.py:66
  128.2 7.1 %reshape.155 = f32[1,2,8,64,1024]{3,2,4,1,0:T(8,128)} reshape(f32[2,512,16,64]{1,3,2,0:T(8,128)} %convolution_bitcast_fusion) | data formatting | bytes 8388608 | tf_op jit(solution)/shard_map/stack | solution.py:140
  135.3 6.9 %copy.54 = f32[1,2,8,64,1024]{4,3,2,1,0:T(8,128)} copy(f32[1,2,8,64,1024]{3,2,4,1,0:T(8,128)} %reshape.155) | data formatting | bytes 8388608 | tf_op jit(solution)/shard_map/stack | solution.py:140
  142.2 3.9 %fusion.3 = bf16[2,16,64,512]{3,2,1,0:T(8,128)(2,1)S(1)} fusion(f32[2,16,512,64]{2,3,1,0:T(8,128)} %get-tuple-element.79, f32[2,16,64]{2,1,0:T(8,128)S(1)} %get-tuple-element.78, f32[2,16,64,512]{3,2,1,0:T(8,128)} %get-tuple-element.77, f32[2,16,64]{2,1,0:T(8,128)S(1)} %get-tuple-element.76), kind=kLoop, calls=%fused_computation.5 | loop fusion | flops 5242880 | bytes 10502144 | tf_op jit(solution)/shard_map/convert_element_type | solution.py:70
  146.2 2.6 %convolution_bitcast_fusion.1 = f32[2,512,16,64]{1,3,2,0:T(8,128)} fusion(bf16[2,64,16,64]{1,3,2,0:T(8,128)(2,1)S(1)} %copy-done.10, bf16[2,16,64,512]{3,2,1,0:T(8,128)(2,1)S(1)} %fusion.3), kind=kOutput, calls=%fused_computation.12 | convolution fusion | flops 134217728 | bytes 6553600 | tf_op jit(solution)/shard_map/jhqk,jqhd->jkhd/dot_general | solution.py:74
  148.8 7.1 %reshape.154 = f32[1,2,8,64,1024]{3,2,4,1,0:T(8,128)} reshape(f32[2,512,16,64]{1,3,2,0:T(8,128)} %convolution_bitcast_fusion.1) | data formatting | bytes 8388608 | tf_op jit(solution)/shard_map/stack | solution.py:140
  155.9 6.8 %copy.53 = f32[1,2,8,64,1024]{4,3,2,1,0:T(8,128)} copy(f32[1,2,8,64,1024]{3,2,4,1,0:T(8,128)} %reshape.154) | data formatting | bytes 8388608 | tf_op jit(solution)/shard_map/stack | solution.py:140
  162.7 3.4 %maximum_bitcast_fusion.1 = (f32[2,2,64,1024]{3,2,1,0:T(8,128)S(1)}, f32[2,2,64,1024]{3,2,1,0:T(8,128)S(1)}, f32[2,2,64,1024]{3,2,1,0:T(8,128)S(1)}, f32[2,2,64,...) fusion(f32[1,2,8,64,1024]{4,3,2,1,0:T(8,128)} %copy.54, ...), kind=kLoop, calls=%fused_computation.25 | loop fusion | flops 1572864 | bytes 14680064 | tf_op jit(solution)/shard_map/squeeze | solution.py:153
  166.1 1.2 select_add_fusion
  167.9 1.2 select_add_fusion.1
  169.1 3.1 %collective-permute-start.13 = (f32[2,2,64,1024]{3,2,0,1:T(8,128)}, f32[2,2,64,1024]{3,2,0,1:T(8,128)}, u32[]{:S(2)}, u32[]{:S(2)}) collective-permute-start(f32[2,2,64,1024]{3,2,0,1:T(8,128)} %select_add_fusion.1), channel_id=1, source_target_pairs={{0,8},{1,9},{2,10},{3,11},{4,12},{5,13},{6,14},{7,15},{8,0},{9,1},... | collective-permute-start | bytes 3145736 | tf_op jit(solution)/shard_map/ppermute | solution.py:42
  172.5 1.1 slice_bitcast_fusion.6
  173.5 2.3 collective-permute-start.10
  175.9 1.3 select_add_fusion.2
  177.2 1.7 fusion.11
  178.9 2.3 copy.41
  181.2 2.1 convert_element_type.41
  183.4 2.3 collective-permute-start.11
  185.6 3.1 %fusion.12 = bf16[2,64,16,64]{1,3,2,0:T(8,128)(2,1)} fusion(bf16[2,512,16,64]{1,3,2,0:T(8,128)(2,1)} %bitcast.146, bf16[2,16,64,512]{3,2,1,0:T(8,128)(2,1)S(1)} %fusion.3), kind=kOutput, calls=%fused_computation.21 | convolution fusion | flops 134348800 | bytes 4456448 | tf_op jit(solution)/shard_map/jhqk,jkhd->jqhd/dot_general | solution.py:71
  188.7 1.5 copy.43
  190.2 1.1 convert_element_type.45
  191.3 1.3 fusion.18
  192.6 38.2 %collective-permute-done.11 = f32[2,64,1024]{2,1,0:T(8,128)} collective-permute-done((f32[2,64,1024]{2,1,0:T(8,128)}, f32[2,64,1024]{2,1,0:T(8,128)}, u32[]{:S(2)}, u32[]{:S(2)}) %collective-permute-start.11) | collective-permute-done | bytes 524320 | tf_op jit(solution)/shard_map/ppermute | solution.py:48
  230.8 1.2 fusion.16
  232.1 2.2 add_convert_fusion
  234.3 0.8 fusion.33
  (79 shorter events, 5.4 us)
Async XLA Ops:
  0.6 21.1 %copy-start.13 = (s32[2]{0:T(128)S(1)}, s32[2]{0:T(128)}, u32[]{:S(2)}) copy-start(s32[2]{0:T(128)} %param.15) | copy-start | bytes 28
  0.6 19.3 %copy-start.12 = (bf16[128,1024]{1,0:T(8,128)(2,1)S(1)}, bf16[128,1024]{1,0:T(8,128)(2,1)}, u32[]{:S(2)}) copy-start(bf16[128,1024]{1,0:T(8,128)(2,1)} %param.13) | copy-start | bytes 786436
  2.6 50.7 %collective-permute-start.7 = (bf16[2,128,1024]{2,1,0:T(8,128)(2,1)}, bf16[2,128,1024]{2,1,0:T(8,128)(2,1)}, u32[]{:S(2)}, u32[]{:S(2)}) collective-permute-start(bf16[2,128,1024]{2,1,0:T(8,128)(2,1)} %pad_maximum_fusion.2), channel_id=1, source_target_pairs={{0,16},{1,17},{2,18},{3,19},{4,20},{5,21},{6,22},{7,23},{8,24},{9,... | collective-permute-start | bytes 1572872 | tf_op jit(solution)/shard_map/ppermute | solution.py:42
  4.0 54.5 %collective-permute-start.8 = (bf16[2,128,1024]{2,1,0:T(8,128)(2,1)}, bf16[2,128,1024]{2,1,0:T(8,128)(2,1)S(1)}, u32[]{:S(2)}, u32[]{:S(2)}) collective-permute-start(bf16[2,128,1024]{2,1,0:T(8,128)(2,1)} %pad_maximum_fusion.2), channel_id=1, source_target_pairs={{0,8},{1,9},{2,10},{3,11},{4,12},{5,13},{6,14},{7,15},{8,0},{9,1},... | collective-permute-start | bytes 1572872 | tf_op jit(solution)/shard_map/ppermute | solution.py:42
  5.0 54.7 %collective-permute-start.9 = (bf16[2,128,1024]{2,1,0:T(8,128)(2,1)}, bf16[2,128,1024]{2,1,0:T(8,128)(2,1)}, u32[]{:S(2)}, u32[]{:S(2)}) collective-permute-start(bf16[2,128,1024]{2,1,0:T(8,128)(2,1)} %pad_maximum_fusion.2), channel_id=1, source_target_pairs={{0,4},{1,5},{2,6},{3,7},{4,0},{5,1},{6,2},{7,3},{8,12},{9,13},{10,... | collective-permute-start | bytes 1572872 | tf_op jit(solution)/shard_map/ppermute | solution.py:42
  13.0 25.1 %collective-permute-start.1 = (bf16[2,64,1024]{2,1,0:T(8,128)(2,1)}, bf16[2,64,1024]{2,1,0:T(8,128)(2,1)}, u32[]{:S(2)}, u32[]{:S(2)}) collective-permute-start(bf16[2,64,1024]{2,1,0:T(8,128)(2,1)} %get-tuple-element.62), channel_id=1, source_target_pairs={{1,0},{2,1},{3,2},{4,3},{5,4},{6,5},{7,6},{8,7},{9,8},{10,9},{11,1... | collective-permute-start | bytes 786440 | tf_op jit(solution)/shard_map/ppermute | solution.py:24
  15.0 33.1 %copy-start.4 = (bf16[128,1024]{1,0:T(8,128)(2,1)S(1)}, bf16[128,1024]{1,0:T(8,128)(2,1)}, u32[]{:S(2)}) copy-start(bf16[128,1024]{1,0:T(8,128)(2,1)} %param.11) | copy-start | bytes 786436
  15.0 33.1 %copy-start.5 = (bf16[128,1024]{1,0:T(8,128)(2,1)S(1)}, bf16[128,1024]{1,0:T(8,128)(2,1)}, u32[]{:S(2)}) copy-start(bf16[128,1024]{1,0:T(8,128)(2,1)} %param.12) | copy-start | bytes 786436
  15.1 6.8 %collective-permute-start.2 = (bf16[2,2,64,1024]{3,2,0,1:T(8,128)(2,1)S(1)}, bf16[2,2,64,1024]{3,2,0,1:T(8,128)(2,1)S(1)}, u32[]{:S(2)}, u32[]{:S(2)}) collective-permute-start(bf16[2,2,64,1024]{3,2,0,1:T(8,128)(2,1)S(1)} %maximum_bitcast_fusion.5), channel_id=1, source_target_pairs={{0,1},{1,0},{2,3},{3,2},{4,5},{5,4},{6,7},{7,6},{8,9},{9,8},{10,11... | collective-permute-start | bytes 1572872 | tf_op jit(solution)/shard_map/ppermute | solution.py:35
  22.0 14.0 %collective-permute-start.3 = (bf16[2,2,64,1024]{3,2,0,1:T(8,128)(2,1)S(1)}, bf16[2,2,64,1024]{3,2,0,1:T(8,128)(2,1)S(1)}, u32[]{:S(2)}, u32[]{:S(2)}) collective-permute-start(bf16[2,2,64,1024]{3,2,0,1:T(8,128)(2,1)S(1)} %broadcast_select_fusion.3), channel_id=1, source_target_pairs={{0,2},{1,3},{2,0},{3,1},{4,6},{5,7},{6,4},{7,5},{8,10},{9,11},{10,... | collective-permute-start | bytes 1572872 | tf_op jit(solution)/shard_map/ppermute | solution.py:35
  36.0 12.1 %collective-permute-start = (bf16[2,64,1024]{2,1,0:T(8,128)(2,1)}, bf16[2,64,1024]{2,1,0:T(8,128)(2,1)S(1)}, u32[]{:S(2)}, u32[]{:S(2)}) collective-permute-start(bf16[2,64,1024]{2,1,0:T(8,128)(2,1)} %get-tuple-element.61), channel_id=1, source_target_pairs={{0,1},{1,2},{2,3},{3,4},{4,5},{5,6},{6,7},{7,8},{8,9},{9,10},{10,1... | collective-permute-start | bytes 786440 | tf_op jit(solution)/shard_map/ppermute | solution.py:23
  38.1 18.2 %collective-permute-start.4 = (bf16[2,2,64,1024]{3,2,0,1:T(8,128)(2,1)S(1)}, bf16[2,2,64,1024]{3,2,0,1:T(8,128)(2,1)}, u32[]{:S(2)}, u32[]{:S(2)}) collective-permute-start(bf16[2,2,64,1024]{3,2,0,1:T(8,128)(2,1)S(1)} %broadcast_select_fusion.4), channel_id=1, source_target_pairs={{0,4},{1,5},{2,6},{3,7},{4,0},{5,1},{6,2},{7,3},{8,12},{9,13},{10,... | collective-permute-start | bytes 1572872 | tf_op jit(solution)/shard_map/ppermute | solution.py:35
  58.2 15.0 %collective-permute-start.5 = (bf16[2,2,64,1024]{3,2,0,1:T(8,128)(2,1)}, bf16[2,2,64,1024]{3,2,0,1:T(8,128)(2,1)}, u32[]{:S(2)}, u32[]{:S(2)}) collective-permute-start(bf16[2,2,64,1024]{3,2,0,1:T(8,128)(2,1)} %broadcast_select_fusion.5), channel_id=1, source_target_pairs={{0,8},{1,9},{2,10},{3,11},{4,12},{5,13},{6,14},{7,15},{8,0},{9,1},... | collective-permute-start | bytes 1572872 | tf_op jit(solution)/shard_map/ppermute | solution.py:35
  62.9 12.5 %copy-start.6 = (bf16[2,64,1024]{1,2,0:T(8,128)(2,1)S(1)}, bf16[2,64,1024]{1,2,0:T(8,128)(2,1)}, u32[]{:S(2)}) copy-start(bf16[2,64,1024]{1,2,0:T(8,128)(2,1)} %copy.39) | copy-start | bytes 786436
  62.9 12.5 %copy-start.7 = (bf16[2,64,1024]{1,2,0:T(8,128)(2,1)S(1)}, bf16[2,64,1024]{1,2,0:T(8,128)(2,1)}, u32[]{:S(2)}) copy-start(bf16[2,64,1024]{1,2,0:T(8,128)(2,1)} %copy.38) | copy-start | bytes 786436
  74.6 23.3 %collective-permute-start.6 = (bf16[2,2,64,1024]{3,2,0,1:T(8,128)(2,1)S(1)}, bf16[2,2,64,1024]{3,2,0,1:T(8,128)(2,1)S(1)}, u32[]{:S(2)}, u32[]{:S(2)}) collective-permute-start(bf16[2,2,64,1024]{3,2,0,1:T(8,128)(2,1)S(1)} %broadcast_select_fusion.6), channel_id=1, source_target_pairs={{0,16},{1,17},{2,18},{3,19},{4,20},{5,21},{6,22},{7,23},{8,24},{9,... | collective-permute-start | bytes 1572872 | tf_op jit(solution)/shard_map/ppermute | solution.py:35
  112.7 4.1 %copy-start.10 = (bf16[2,64,16,64]{1,3,2,0:T(8,128)(2,1)S(1)}, bf16[2,64,16,64]{1,3,2,0:T(8,128)(2,1)}, u32[]{:S(2)}) copy-start(bf16[2,64,16,64]{1,3,2,0:T(8,128)(2,1)} %copy.44) | copy-start | bytes 786436
  116.8 8.5 %copy-start.1 = (bf16[1,2,512,1024]{2,3,1,0:T(8,128)(2,1)}, bf16[1,2,512,1024]{2,3,1,0:T(8,128)(2,1)S(1)}, u32[]{:S(2)}) copy-start(bf16[1,2,512,1024]{2,3,1,0:T(8,128)(2,1)S(1)} %get-tuple-element.39) | copy-start | bytes 6291460
  116.8 3.4 %copy-start.11 = (bf16[2,64,16,64]{1,3,2,0:T(8,128)(2,1)S(1)}, bf16[2,64,16,64]{1,3,2,0:T(8,128)(2,1)}, u32[]{:S(2)}) copy-start(bf16[2,64,16,64]{1,3,2,0:T(8,128)(2,1)} %copy.46) | copy-start | bytes 786436
  120.2 5.1 %copy-start.2 = (f32[2,16,64,512]{3,2,1,0:T(8,128)S(1)}, f32[2,16,64,512]{3,2,1,0:T(8,128)}, u32[]{:S(2)}) copy-start(f32[2,16,64,512]{3,2,1,0:T(8,128)} %get-tuple-element.77) | copy-start | bytes 12582916
  120.2 5.1 %copy-start.8 = (bf16[1,2,512,1024]{2,3,1,0:T(8,128)(2,1)S(1)}, bf16[1,2,512,1024]{2,3,1,0:T(8,128)(2,1)}, u32[]{:S(2)}) copy-start(bf16[1,2,512,1024]{2,3,1,0:T(8,128)(2,1)} %get-tuple-element.40) | copy-start | bytes 6291460
  167.4 64.7 %collective-permute-start.14 = (f32[2,2,64,1024]{3,2,0,1:T(8,128)}, f32[2,2,64,1024]{3,2,0,1:T(8,128)}, u32[]{:S(2)}, u32[]{:S(2)}) collective-permute-start(f32[2,2,64,1024]{3,2,0,1:T(8,128)} %select_add_fusion), channel_id=1, source_target_pairs={{0,4},{1,5},{2,6},{3,7},{4,0},{5,1},{6,2},{7,3},{8,12},{9,13},{10,... | collective-permute-start | bytes 3145736 | tf_op jit(solution)/shard_map/ppermute | solution.py:42
  169.1 62.9 %collective-permute-start.13 = (f32[2,2,64,1024]{3,2,0,1:T(8,128)}, f32[2,2,64,1024]{3,2,0,1:T(8,128)}, u32[]{:S(2)}, u32[]{:S(2)}) collective-permute-start(f32[2,2,64,1024]{3,2,0,1:T(8,128)} %select_add_fusion.1), channel_id=1, source_target_pairs={{0,8},{1,9},{2,10},{3,11},{4,12},{5,13},{6,14},{7,15},{8,0},{9,1},... | collective-permute-start | bytes 3145736 | tf_op jit(solution)/shard_map/ppermute | solution.py:42
  172.4 6.5 %copy-start = (f32[2,4,64,1024]{3,2,1,0:T(8,128)}, f32[2,4,64,1024]{3,2,1,0:T(8,128)S(1)}, u32[]{:S(2)}) copy-start(f32[2,4,64,1024]{3,2,1,0:T(8,128)S(1)} %pad_add_fusion) | copy-start | bytes 6291460
  172.4 4.8 %copy-start.3 = (f32[2,16,64,512]{3,2,1,0:T(8,128)S(1)}, f32[2,16,64,512]{3,2,1,0:T(8,128)}, u32[]{:S(2)}) copy-start(f32[2,16,64,512]{3,2,1,0:T(8,128)} %get-tuple-element.77) | copy-start | bytes 12582916
  172.5 4.8 %copy-start.9 = (bf16[1,2,512,1024]{2,3,1,0:T(8,128)(2,1)S(1)}, bf16[1,2,512,1024]{2,3,1,0:T(8,128)(2,1)}, u32[]{:S(2)}) copy-start(bf16[1,2,512,1024]{2,3,1,0:T(8,128)(2,1)} %get-tuple-element.40) | copy-start | bytes 6291460
  173.5 17.8 %collective-permute-start.10 = (f32[2,64,1024]{2,1,0:T(8,128)}, f32[2,64,1024]{2,1,0:T(8,128)}, u32[]{:S(2)}, u32[]{:S(2)}) collective-permute-start(f32[2,64,1024]{2,1,0:T(8,128)} %get-tuple-element.42), channel_id=1, source_target_pairs={{1,0},{2,1},{3,2},{4,3},{5,4},{6,5},{7,6},{8,7},{9,8},{10,9},{11,1... | collective-permute-start | bytes 1572872 | tf_op jit(solution)/shard_map/ppermute | solution.py:48
  177.2 54.8 %collective-permute-start.12 = (f32[2,2,64,1024]{3,2,0,1:T(8,128)}, f32[2,2,64,1024]{3,2,0,1:T(8,128)}, u32[]{:S(2)}, u32[]{:S(2)}) collective-permute-start(f32[2,2,64,1024]{3,2,0,1:T(8,128)} %select_add_fusion.2), channel_id=1, source_target_pairs={{0,16},{1,17},{2,18},{3,19},{4,20},{5,21},{6,22},{7,23},{8,24},{9,... | collective-permute-start | bytes 3145736 | tf_op jit(solution)/shard_map/ppermute | solution.py:42
  178.9 12.3 %slice-start = ((f32[2,4,64,1024]{3,2,1,0:T(8,128)}), f32[2,2,64,1024]{3,2,1,0:T(8,128)S(1)}, s32[]{:S(2)}) async-start(f32[2,4,64,1024]{3,2,1,0:T(8,128)} %copy-done), calls=%async_computation | async-start | bytes 2097152 | tf_op jit(solution)/shard_map/slice | solution.py:148
  183.4 47.5 %collective-permute-start.11 = (f32[2,64,1024]{2,1,0:T(8,128)}, f32[2,64,1024]{2,1,0:T(8,128)}, u32[]{:S(2)}, u32[]{:S(2)}) collective-permute-start(f32[2,64,1024]{2,1,0:T(8,128)} %get-tuple-element.41), channel_id=1, source_target_pairs={{0,1},{1,2},{2,3},{3,4},{4,5},{5,6},{6,7},{7,8},{8,9},{9,10},{10,1... | collective-permute-start | bytes 1572872 | tf_op jit(solution)/shard_map/ppermute | solution.py:48

commit v2 on v1

--- a/solution.py
+++ b/solution.py
@@ -29,13 +29,22 @@
 def from_root(blocks, axis, sources):
     size = lax.axis_size(axis)
     position = lax.axis_index(axis)
-    shape = (-1,) + (1,) * (blocks.ndim - 1)
-    for level in range(size.bit_length() - 1):
+    shape = (-1,) + (1,) * (blocks.ndim - 2)
+    core = position % 2
+    sibling = [(i, i ^ 1) for i in range(size)]
+    mine = jnp.where(core == 0, blocks[:, 0], blocks[:, 1])
+    theirs = jnp.where(core == 0, blocks[:, 1], blocks[:, 0])
+    received = lax.ppermute(theirs, axis, sibling)
+    carried = jnp.where((sources == (position ^ 1)).reshape(shape), received, mine)
+    for level in range(1, size.bit_length() - 1):
         step = 1 << level
-        received = lax.ppermute(blocks, axis, [(i, i ^ step) for i in range(size)])
+        received = lax.ppermute(carried, axis, [(i, i ^ step) for i in range(size)])
         partner_holds = ((position ^ step) >> level) == (sources >> level)
-        blocks = jnp.where(partner_holds.reshape(shape), received, blocks)
-    return blocks
+        carried = jnp.where(partner_holds.reshape(shape), received, carried)
+    other = lax.ppermute(carried, axis, sibling)
+    first = jnp.where(core == 0, carried, other)
+    second = jnp.where(core == 0, other, carried)
+    return jnp.stack([first, second], axis=1)
 
 
 def partner_2(array, axis, distance):

time: 237 us -> 216 us (0.911)
  waiting for transfers between devices: 94.5 us -> 77.1 us
  local copies, waits for them, and re-layouts: 71.4 us -> 68.7 us
    ppermute x5 -> x6, waiting for transfers between devices: 47.5 us -> 25.3 us  [the longest x4 24 us: from_root(): received = lax.ppermute(carried, axis, [(i, i ^ step) for i in range(size)])]
    ppermute x1, waiting for transfers between devices: 0.01 us -> 7.56 us  [padded_2(): after = lax.ppermute(first, axis, down)]
    ppermute x1, waiting for transfers between devices: 8.69 us -> 4.81 us  [padded_2(): before = lax.ppermute(last, axis, up)]
  transfers between devices with their start and end apart: 15 -> 16, of which waited for: 6 -> 8; matrix products, arithmetic and copies ran while one was open for 18% -> 17% of each run, Pallas kernels for 0% -> 0%
where the time goes in v2:
time: 216 us; the launch traced here: 214 us
  waiting for transfers between devices  77.1 us (36%)
  local copies, waits for them, and re-layouts  68.7 us (32%)
  other arithmetic  25.6 us (12%)
  starting transfers between devices  21.5 us (10%)
  matrix products  18.9 us (9%)
  between operations  2.42 us (1%)
    ppermute x2, waiting for transfers between devices, passed_along(): return lax.ppermute(array, axis, pairs)  39.3 us
    another operation x4, local copies, waits for them, and re-layouts, local(): jnp.stack([grad_key, grad_value])  27.9 us
    ppermute x4, waiting for transfers between devices, from_root(): received = lax.ppermute(carried, axis, [(i, i ^ step) for i in range(size)])  24 us
    concatenate x1, local copies, waits for them, and re-layouts, local(): every_key = jnp.concatenate([window, global_part] + random_parts, axis=2)  9.62 us
    ppermute x6, starting transfers between devices, partner_2(): lax.ppermute(array, axis, [(i, i ^ 1 << distance) for i in range(lax.axis...  8.8 us
    ppermute x1, waiting for transfers between devices, padded_2(): after = lax.ppermute(first, axis, down)  7.56 us
    dot_general x1, matrix products, attend_blocks(): jnp.einsum('jhqk,jqhd->jkhd', probs_low, grad_blocks, preferred_element_t...  5.06 us
    ppermute x1, waiting for transfers between devices, padded_2(): before = lax.ppermute(last, axis, up)  4.81 us
  transfers between devices with their start and end apart: 16, of which 8 were waited for; matrix products, arithmetic and copies ran while one was open for 17% of the time, Pallas kernels for 0%

profile of v2, /device:TPU:192, one launch (start us, length us, event | category | flops | bytes accessed | tf_op | source)
XLA Modules:
  0.0 214.1 jit_solution(10909087097648699077)
XLA Ops:
  0.7 2.0 pad_maximum_fusion.2
  2.6 1.5 collective-permute-start.8
  4.1 1.0 collective-permute-start.9
  5.1 0.7 and_select_fusion
  5.8 0.6 fusion.34
  7.7 2.2 %fusion.24 = (bf16[2,1,64,1024]{3,2,1,0:T(8,128)(2,1)S(1)}, bf16[2,64,1024]{2,1,0:T(8,128)(2,1)}, bf16[2,64,1024]{2,1,0:T(8,128)(2,1)}, bf16[2,1,64,1024]{3,2,1,0:T(8,128)(2,1)S(1)}) fusion(s32[]{:T(128)S(6)} %select_n.109, bf16[1,128,1024]{2,1,0:T(8,128)(2,1)} %bitcast.153, bf16[1,128,1024]{2,1,0:T(8,128)(2,1)} %bitcast.156, s32[]{:T(128)S(6)} %select_n.110), kind=kLoop, calls=%fused_computation.67 | loop fusion | flops 2097152 | bytes 1572872 | tf_op jit(solution)/shard_map/stack | solution.py:106
  9.8 4.2 %collective-permute-start.1 = (bf16[2,64,1024]{2,1,0:T(8,128)(2,1)}, bf16[2,64,1024]{2,1,0:T(8,128)(2,1)}, u32[]{:S(2)}, u32[]{:S(2)}) collective-permute-start(bf16[2,64,1024]{2,1,0:T(8,128)(2,1)} %get-tuple-element.64), channel_id=1, source_target_pairs={{1,0},{2,1},{3,2},{4,3},{5,4},{6,5},{7,6},{8,7},{9,8},{10,9},{11,1... | collective-permute-start | bytes 786440 | tf_op jit(solution)/shard_map/ppermute | solution.py:24
  14.1 1.9 collective-permute-start
  16.1 0.7 select_bitcast_fusion.2
  18.2 0.3 reshape.154
  18.6 1.3 copy.47
  19.9 0.3 reshape.155
  20.2 1.3 copy.49
  21.6 2.2 %collective-permute-start.10 = (bf16[2,128,1024]{2,1,0:T(8,128)(2,1)}, bf16[2,128,1024]{2,1,0:T(8,128)(2,1)}, u32[]{:S(2)}, u32[]{:S(2)}) collective-permute-start(bf16[2,128,1024]{2,1,0:T(8,128)(2,1)} %pad_maximum_fusion.2), channel_id=1, source_target_pairs={{0,4},{1,5},{2,6},{3,7},{4,0},{5,1},{6,2},{7,3},{8,12},{9,13},{10,... | collective-permute-start | bytes 1572872 | tf_op jit(solution)/shard_map/ppermute | solution.py:51
  23.9 7.6 %collective-permute-done.1 = bf16[2,64,1024]{2,1,0:T(8,128)(2,1)} collective-permute-done((bf16[2,64,1024]{2,1,0:T(8,128)(2,1)}, bf16[2,64,1024]{2,1,0:T(8,128)(2,1)}, u32[]{:S(2)}, u32[]{:S(2)}) %collective-permute-start.1) | collective-permute-done | bytes 262176 | tf_op jit(solution)/shard_map/ppermute | solution.py:24
  31.5 4.8 %collective-permute-done = bf16[2,64,1024]{2,1,0:T(8,128)(2,1)} collective-permute-done((bf16[2,64,1024]{2,1,0:T(8,128)(2,1)}, bf16[2,64,1024]{2,1,0:T(8,128)(2,1)}, u32[]{:S(2)}, u32[]{:S(2)}) %collective-permute-start) | collective-permute-done | bytes 262176 | tf_op jit(solution)/shard_map/ppermute | solution.py:23
  36.3 1.1 pad_maximum_fusion.1
  37.6 1.4 copy.58
  39.0 1.3 copy.59
  40.3 1.3 copy.60
  41.6 5.0 %collective-permute-done.3 = bf16[2,64,1024]{2,1,0:T(8,128)(2,1)S(1)} collective-permute-done((bf16[2,64,1024]{2,1,0:T(8,128)(2,1)S(1)}, bf16[2,64,1024]{2,1,0:T(8,128)(2,1)S(1)}, u32[]{:S(2)}, u32[]{:S(2)}) %collective-permute-start.3) | collective-permute-done | bytes 262176 | tf_op jit(solution)/shard_map/ppermute | solution.py:41
  48.1 1.1 slice_bitcast_fusion.10
  49.1 1.0 copy.42
  50.2 1.1 copy.41
  51.2 4.5 %collective-permute-done.4 = bf16[2,64,1024]{2,1,0:T(8,128)(2,1)} collective-permute-done((bf16[2,64,1024]{2,1,0:T(8,128)(2,1)S(1)}, bf16[2,64,1024]{2,1,0:T(8,128)(2,1)}, u32[]{:S(2)}, u32[]{:S(2)}) %collective-permute-start.4) | collective-permute-done | bytes 262176 | tf_op jit(solution)/shard_map/ppermute | solution.py:41
  55.8 1.0 broadcast_select_fusion.4
  57.1 6.3 %collective-permute-done.5 = bf16[2,64,1024]{2,1,0:T(8,128)(2,1)S(1)} collective-permute-done((bf16[2,64,1024]{2,1,0:T(8,128)(2,1)S(1)}, bf16[2,64,1024]{2,1,0:T(8,128)(2,1)S(1)}, u32[]{:S(2)}, u32[]{:S(2)}) %collective-permute-start.5) | collective-permute-done | bytes 262176 | tf_op jit(solution)/shard_map/ppermute | solution.py:41
  63.5 1.3 collective-permute-start.6
  65.0 8.1 %collective-permute-done.6 = bf16[2,64,1024]{2,1,0:T(8,128)(2,1)S(1)} collective-permute-done((bf16[2,64,1024]{2,1,0:T(8,128)(2,1)S(1)}, bf16[2,64,1024]{2,1,0:T(8,128)(2,1)S(1)}, u32[]{:S(2)}, u32[]{:S(2)}) %collective-permute-start.6) | collective-permute-done | bytes 262176 | tf_op jit(solution)/shard_map/ppermute | solution.py:41
  73.6 1.3 collective-permute-done.7
  75.0 0.9 pad_maximum_fusion.3
  75.9 2.0 copy.36
  77.9 2.3 %broadcast_in_dim.246 = bf16[2,2,128,1024]{2,3,1,0:T(8,128)(2,1)} broadcast(bf16[2,128,1024]{1,2,0:T(8,128)(2,1)} %copy.36), dimensions={0,2,3} | broadcast | bytes 1572864 | tf_op jit(solution)/shard_map/broadcast_in_dim | solution.py:114
  80.2 9.6 %concatenate.15 = bf16[2,2,512,1024]{2,3,1,0:T(8,128)(2,1)} concatenate(bf16[2,2,64,1024]{2,3,1,0:T(8,128)(2,1)} %copy.58, bf16[2,2,64,1024]{2,3,1,0:T(8,128)(2,1)} %copy.59, bf16[2,2,64,1024]{2,3,1,0:T(8,128)(2,1)} %copy.60, bf16[2,2,128,1024]{2,3,1,0:T(8,128)(2,1)} %broadcast_in_dim.246, bf16[2,2,64,1024]{2,3,1,0:T(8,128)(2,1)S(1)} %broadcast_select_fusion.2, ...), dimensions={2} | concatenate | bytes 8388608 | tf_op jit(solution)/shard_map/concatenate | solution.py:128
  89.8 4.1 %fusion.31 = (bf16[1,2,512,1024]{2,3,1,0:T(8,128)(2,1)S(1)}, bf16[1,2,512,1024]{2,3,1,0:T(8,128)(2,1)}) fusion(bf16[2,2,512,1024]{2,3,1,0:T(8,128)(2,1)} %concatenate.15), kind=kLoop, calls=%fused_computation.115 | loop fusion | bytes 8388608 | tf_op jit(solution)/shard_map/slice | solution.py:129
  93.9 3.4 %fusion.35 = (f32[2,16,64]{2,1,0:T(8,128)S(1)}, f32[2,16,64,512]{3,2,1,0:T(8,128)}) fusion(pred[2,512]{1,0:T(4,128)(4,1)S(1)} %add_add_fusion, bf16[2,64,16,64]{1,3,2,0:T(8,128)(2,1)S(1)} %copy-done.10, bf16[2,512,16,64]{1,3,2,0:T(8,128)(2,1)S(1)} %bitcast.149), kind=kOutput, calls=%fused_computation.119 | convolution fusion | flops 138412544 | bytes 6562816 | tf_op jit(solution)/shard_map/sub | solution.py:68
  97.3 5.1 %convolution_bitcast_fusion = f32[2,512,16,64]{1,3,2,0:T(8,128)} fusion(bf16[2,64,16,64]{1,3,2,0:T(8,128)(2,1)S(1)} %copy-done.11, f32[2,16,64,512]{3,2,1,0:T(8,128)} %get-tuple-element.79, f32[2,16,64]{2,1,0:T(8,128)S(1)} %get-tuple-element.78), kind=kOutput, calls=%fused_computation.11 | convolution fusion | flops 136314880 | bytes 8658944 | tf_op jit(solution)/shard_map/jhqk,jqhd->jkhd/dot_general | solution.py:86
  102.4 3.0 %fusion.1 = (f32[2,16,64]{2,1,0:T(8,128)S(1)}, f32[2,16,512,64]{2,3,1,0:T(8,128)}) fusion(f32[2,16,64,512]{3,2,1,0:T(8,128)S(1)} %copy-done.2, f32[2,16,64]{2,1,0:T(8,128)S(1)} %get-tuple-element.78, bf16[2,64,16,64]{1,3,2,0:T(8,128)(2,1)S(1)} %copy-done.11, bf16[2,512,16,64]{1,3,2,0:T(8,128)(2,1)S(1)} %bitcast.159), kind=kOutput, calls=%fused_computation.3 | convolution fusion | flops 137361408 | bytes 10764288 | tf_op jit(solution)/shard_map/jqhd,jkhd->jhqk/dot_general | solution.py:75
  105.4 7.1 %reshape.159 = f32[1,2,8,64,1024]{3,2,4,1,0:T(8,128)} reshape(f32[2,512,16,64]{1,3,2,0:T(8,128)} %convolution_bitcast_fusion) | data formatting | bytes 8388608 | tf_op jit(solution)/shard_map/stack | solution.py:149
  112.5 6.9 %copy.57 = f32[1,2,8,64,1024]{4,3,2,1,0:T(8,128)} copy(f32[1,2,8,64,1024]{3,2,4,1,0:T(8,128)} %reshape.159) | data formatting | bytes 8388608 | tf_op jit(solution)/shard_map/stack | solution.py:149
  119.4 3.9 %fusion.3 = bf16[2,16,64,512]{3,2,1,0:T(8,128)(2,1)S(1)} fusion(f32[2,16,512,64]{2,3,1,0:T(8,128)} %get-tuple-element.81, f32[2,16,64]{2,1,0:T(8,128)S(1)} %get-tuple-element.80, f32[2,16,64,512]{3,2,1,0:T(8,128)} %get-tuple-element.79, f32[2,16,64]{2,1,0:T(8,128)S(1)} %get-tuple-element.78), kind=kLoop, calls=%fused_computation.5 | loop fusion | flops 5242880 | bytes 10502144 | tf_op jit(solution)/shard_map/convert_element_type | solution.py:79
  123.3 2.6 %convolution_bitcast_fusion.1 = f32[2,512,16,64]{1,3,2,0:T(8,128)} fusion(bf16[2,64,16,64]{1,3,2,0:T(8,128)(2,1)S(1)} %copy-done.10, bf16[2,16,64,512]{3,2,1,0:T(8,128)(2,1)S(1)} %fusion.3), kind=kOutput, calls=%fused_computation.12 | convolution fusion | flops 134217728 | bytes 6553600 | tf_op jit(solution)/shard_map/jhqk,jqhd->jkhd/dot_general | solution.py:83
  125.9 7.1 %reshape.158 = f32[1,2,8,64,1024]{3,2,4,1,0:T(8,128)} reshape(f32[2,512,16,64]{1,3,2,0:T(8,128)} %convolution_bitcast_fusion.1) | data formatting | bytes 8388608 | tf_op jit(solution)/shard_map/stack | solution.py:149
  133.1 6.8 %copy.56 = f32[1,2,8,64,1024]{4,3,2,1,0:T(8,128)} copy(f32[1,2,8,64,1024]{3,2,4,1,0:T(8,128)} %reshape.158) | data formatting | bytes 8388608 | tf_op jit(solution)/shard_map/stack | solution.py:149
  139.9 3.4 %maximum_bitcast_fusion.1 = (f32[2,2,64,1024]{3,2,1,0:T(8,128)S(1)}, f32[2,2,64,1024]{3,2,1,0:T(8,128)S(1)}, f32[2,2,64,1024]{3,2,1,0:T(8,128)S(1)}, f32[2,2,64,...) fusion(f32[1,2,8,64,1024]{4,3,2,1,0:T(8,128)} %copy.57, ...), kind=kLoop, calls=%fused_computation.25 | loop fusion | flops 1572864 | bytes 14680064 | tf_op jit(solution)/shard_map/squeeze | solution.py:162
  143.3 1.2 select_add_fusion
  144.5 1.0 collective-permute-start.15
  145.7 1.2 select_add_fusion.1
  146.9 3.1 %collective-permute-start.14 = (f32[2,2,64,1024]{3,2,0,1:T(8,128)}, f32[2,2,64,1024]{3,2,0,1:T(8,128)}, u32[]{:S(2)}, u32[]{:S(2)}) collective-permute-start(f32[2,2,64,1024]{3,2,0,1:T(8,128)} %select_add_fusion.1), channel_id=1, source_target_pairs={{0,8},{1,9},{2,10},{3,11},{4,12},{5,13},{6,14},{7,15},{8,0},{9,1},... | collective-permute-start | bytes 3145736 | tf_op jit(solution)/shard_map/ppermute | solution.py:51
  150.2 1.1 slice_bitcast_fusion.6
  151.3 2.8 %collective-permute-start.11 = (f32[2,64,1024]{2,1,0:T(8,128)}, f32[2,64,1024]{2,1,0:T(8,128)}, u32[]{:S(2)}, u32[]{:S(2)}) collective-permute-start(f32[2,64,1024]{2,1,0:T(8,128)} %get-tuple-element.42), channel_id=1, source_target_pairs={{1,0},{2,1},{3,2},{4,3},{5,4},{6,5},{7,6},{8,7},{9,8},{10,9},{11,1... | collective-permute-start | bytes 1572872 | tf_op jit(solution)/shard_map/ppermute | solution.py:57
  154.2 1.3 select_add_fusion.2
  155.5 1.7 fusion.11
  157.2 2.3 %copy.44 = bf16[2,64,16,64]{3,2,1,0:T(8,128)(2,1)} copy(bf16[2,64,16,64]{1,3,2,0:T(8,128)(2,1)} %fusion.11) | data formatting | bytes 524288 | tf_op jit(solution)/shard_map/convert_element_type | solution.py:168
  159.5 2.1 convert_element_type.41
  161.6 1.9 collective-permute-start.12
  163.5 3.1 %fusion.12 = bf16[2,64,16,64]{1,3,2,0:T(8,128)(2,1)} fusion(bf16[2,512,16,64]{1,3,2,0:T(8,128)(2,1)} %bitcast.150, bf16[2,16,64,512]{3,2,1,0:T(8,128)(2,1)S(1)} %fusion.3), kind=kOutput, calls=%fused_computation.21 | convolution fusion | flops 134348800 | bytes 4456448 | tf_op jit(solution)/shard_map/jhqk,jkhd->jqhd/dot_general | solution.py:80
  166.6 1.5 copy.46
  168.1 1.1 convert_element_type.45
  169.2 1.3 fusion.18
  170.5 39.3 %collective-permute-done.12 = f32[2,64,1024]{2,1,0:T(8,128)} collective-permute-done((f32[2,64,1024]{2,1,0:T(8,128)}, f32[2,64,1024]{2,1,0:T(8,128)}, u32[]{:S(2)}, u32[]{:S(2)}) %collective-permute-start.12) | collective-permute-done | bytes 524320 | tf_op jit(solution)/shard_map/ppermute | solution.py:57
  209.9 1.2 fusion.16
  211.1 2.2 %add_convert_fusion = bf16[2,2,64,1024]{3,2,0,1:T(8,128)(2,1)S(1)} fusion(f32[2,2,64,1024]{3,2,0,1:T(8,128)} %collective-permute-done.15, f32[2,2,64,1024]{3,2,0,1:T(8,128)} %collective-permute-done.14, f32[2,2,64,1024]{3,2,0,1:T(8,128)S(1)} %fusion.16, f32[2,2,64,1024]{3,2,0,1:T(8,128)} %collective-permute-done.13), kind=kLoop, calls=%fused_computation.30 | loop fusion | flops 1048576 | bytes 4718592 | tf_op jit(solution)/shard_map/convert.1
  213.3 0.8 fusion.33
  (88 shorter events, 4.7 us)
Async XLA Ops:
  0.6 16.2 %copy-start.15 = (s32[2]{0:T(128)S(1)}, s32[2]{0:T(128)}, u32[]{:S(2)}) copy-start(s32[2]{0:T(128)} %param.15) | copy-start | bytes 28
  0.6 16.2 %copy-start.14 = (s32[2,3]{1,0:T(2,128)S(1)}, s32[2,3]{1,0:T(2,128)}, u32[]{:S(2)}) copy-start(s32[2,3]{1,0:T(2,128)} %param.14) | copy-start | bytes 76
  0.7 17.5 %copy-start.12 = (bf16[128,1024]{1,0:T(8,128)(2,1)S(1)}, bf16[128,1024]{1,0:T(8,128)(2,1)}, u32[]{:S(2)}) copy-start(bf16[128,1024]{1,0:T(8,128)(2,1)} %param.10) | copy-start | bytes 786436
  0.7 19.2 %copy-start.13 = (bf16[128,1024]{1,0:T(8,128)(2,1)S(1)}, bf16[128,1024]{1,0:T(8,128)(2,1)}, u32[]{:S(2)}) copy-start(bf16[128,1024]{1,0:T(8,128)(2,1)} %param.13) | copy-start | bytes 786436
  2.6 33.7 %copy-start.4 = (bf16[128,1024]{1,0:T(8,128)(2,1)S(1)}, bf16[128,1024]{1,0:T(8,128)(2,1)}, u32[]{:S(2)}) copy-start(bf16[128,1024]{1,0:T(8,128)(2,1)} %param.11) | copy-start | bytes 786436
  2.6 33.7 %copy-start.5 = (bf16[128,1024]{1,0:T(8,128)(2,1)S(1)}, bf16[128,1024]{1,0:T(8,128)(2,1)}, u32[]{:S(2)}) copy-start(bf16[128,1024]{1,0:T(8,128)(2,1)} %param.12) | copy-start | bytes 786436
  2.6 44.2 %collective-permute-start.8 = (bf16[2,128,1024]{2,1,0:T(8,128)(2,1)}, bf16[2,128,1024]{2,1,0:T(8,128)(2,1)S(1)}, u32[]{:S(2)}, u32[]{:S(2)}) collective-permute-start(bf16[2,128,1024]{2,1,0:T(8,128)(2,1)} %pad_maximum_fusion.2), channel_id=1, source_target_pairs={{0,16},{1,17},{2,18},{3,19},{4,20},{5,21},{6,22},{7,23},{8,24},{9,... | collective-permute-start | bytes 1572872 | tf_op jit(solution)/shard_map/ppermute | solution.py:51
  4.1 42.8 %collective-permute-start.9 = (bf16[2,128,1024]{2,1,0:T(8,128)(2,1)}, bf16[2,128,1024]{2,1,0:T(8,128)(2,1)S(1)}, u32[]{:S(2)}, u32[]{:S(2)}) collective-permute-start(bf16[2,128,1024]{2,1,0:T(8,128)(2,1)} %pad_maximum_fusion.2), channel_id=1, source_target_pairs={{0,8},{1,9},{2,10},{3,11},{4,12},{5,13},{6,14},{7,15},{8,0},{9,1},... | collective-permute-start | bytes 1572872 | tf_op jit(solution)/shard_map/ppermute | solution.py:51
  9.8 21.6 %collective-permute-start.1 = (bf16[2,64,1024]{2,1,0:T(8,128)(2,1)}, bf16[2,64,1024]{2,1,0:T(8,128)(2,1)}, u32[]{:S(2)}, u32[]{:S(2)}) collective-permute-start(bf16[2,64,1024]{2,1,0:T(8,128)(2,1)} %get-tuple-element.64), channel_id=1, source_target_pairs={{1,0},{2,1},{3,2},{4,3},{5,4},{6,5},{7,6},{8,7},{9,8},{10,9},{11,1... | collective-permute-start | bytes 786440 | tf_op jit(solution)/shard_map/ppermute | solution.py:24
  14.1 22.2 %collective-permute-start = (bf16[2,64,1024]{2,1,0:T(8,128)(2,1)}, bf16[2,64,1024]{2,1,0:T(8,128)(2,1)}, u32[]{:S(2)}, u32[]{:S(2)}) collective-permute-start(bf16[2,64,1024]{2,1,0:T(8,128)(2,1)} %get-tuple-element.63), channel_id=1, source_target_pairs={{0,1},{1,2},{2,3},{3,4},{4,5},{5,6},{6,7},{7,8},{8,9},{9,10},{10,1... | collective-permute-start | bytes 786440 | tf_op jit(solution)/shard_map/ppermute | solution.py:23
  16.8 4.8 %collective-permute-start.2 = (bf16[2,64,1024]{2,1,0:T(8,128)(2,1)}, bf16[2,64,1024]{2,1,0:T(8,128)(2,1)S(1)}, u32[]{:S(2)}, u32[]{:S(2)}) collective-permute-start(bf16[2,64,1024]{2,1,0:T(8,128)(2,1)} %select_bitcast_fusion.2), channel_id=1, source_target_pairs={{0,1},{1,0},{2,3},{3,2},{4,5},{5,4},{6,7},{7,6},{8,9},{9,8},{10,11... | collective-permute-start | bytes 786440 | tf_op jit(solution)/shard_map/ppermute | solution.py:37
  21.6 26.5 %collective-permute-start.10 = (bf16[2,128,1024]{2,1,0:T(8,128)(2,1)}, bf16[2,128,1024]{2,1,0:T(8,128)(2,1)}, u32[]{:S(2)}, u32[]{:S(2)}) collective-permute-start(bf16[2,128,1024]{2,1,0:T(8,128)(2,1)} %pad_maximum_fusion.2), channel_id=1, source_target_pairs={{0,4},{1,5},{2,6},{3,7},{4,0},{5,1},{6,2},{7,3},{8,12},{9,13},{10,... | collective-permute-start | bytes 1572872 | tf_op jit(solution)/shard_map/ppermute | solution.py:51
  31.5 15.1 %collective-permute-start.3 = (bf16[2,64,1024]{2,1,0:T(8,128)(2,1)S(1)}, bf16[2,64,1024]{2,1,0:T(8,128)(2,1)S(1)}, u32[]{:S(2)}, u32[]{:S(2)}) collective-permute-start(bf16[2,64,1024]{2,1,0:T(8,128)(2,1)S(1)} %bitcast_select_fusion), channel_id=1, source_target_pairs={{0,2},{1,3},{2,0},{3,1},{4,6},{5,7},{6,4},{7,5},{8,10},{9,11},{10,... | collective-permute-start | bytes 786440 | tf_op jit(solution)/shard_map/ppermute | solution.py:41
  46.7 9.1 %collective-permute-start.4 = (bf16[2,64,1024]{2,1,0:T(8,128)(2,1)S(1)}, bf16[2,64,1024]{2,1,0:T(8,128)(2,1)}, u32[]{:S(2)}, u32[]{:S(2)}) collective-permute-start(bf16[2,64,1024]{2,1,0:T(8,128)(2,1)S(1)} %broadcast_select_fusion.3), channel_id=1, source_target_pairs={{0,4},{1,5},{2,6},{3,7},{4,0},{5,1},{6,2},{7,3},{8,12},{9,13},{10,... | collective-permute-start | bytes 786440 | tf_op jit(solution)/shard_map/ppermute | solution.py:41
  51.2 22.2 %copy-start.6 = (bf16[2,64,1024]{1,2,0:T(8,128)(2,1)S(1)}, bf16[2,64,1024]{1,2,0:T(8,128)(2,1)}, u32[]{:S(2)}) copy-start(bf16[2,64,1024]{1,2,0:T(8,128)(2,1)} %copy.42) | copy-start | bytes 786436
  51.2 22.3 %copy-start.7 = (bf16[2,64,1024]{1,2,0:T(8,128)(2,1)S(1)}, bf16[2,64,1024]{1,2,0:T(8,128)(2,1)}, u32[]{:S(2)}) copy-start(bf16[2,64,1024]{1,2,0:T(8,128)(2,1)} %copy.41) | copy-start | bytes 786436
  56.8 6.6 %collective-permute-start.5 = (bf16[2,64,1024]{2,1,0:T(8,128)(2,1)S(1)}, bf16[2,64,1024]{2,1,0:T(8,128)(2,1)S(1)}, u32[]{:S(2)}, u32[]{:S(2)}) collective-permute-start(bf16[2,64,1024]{2,1,0:T(8,128)(2,1)S(1)} %broadcast_select_fusion.4), channel_id=1, source_target_pairs={{0,8},{1,9},{2,10},{3,11},{4,12},{5,13},{6,14},{7,15},{8,0},{9,1},... | collective-permute-start | bytes 786440 | tf_op jit(solution)/shard_map/ppermute | solution.py:41
  63.5 9.6 %collective-permute-start.6 = (bf16[2,64,1024]{2,1,0:T(8,128)(2,1)S(1)}, bf16[2,64,1024]{2,1,0:T(8,128)(2,1)S(1)}, u32[]{:S(2)}, u32[]{:S(2)}) collective-permute-start(bf16[2,64,1024]{2,1,0:T(8,128)(2,1)S(1)} %broadcast_select_fusion.5), channel_id=1, source_target_pairs={{0,16},{1,17},{2,18},{3,19},{4,20},{5,21},{6,22},{7,23},{8,24},{9,... | collective-permute-start | bytes 786440 | tf_op jit(solution)/shard_map/ppermute | solution.py:41
  73.2 1.8 collective-permute-start.7
  89.8 4.1 %copy-start.10 = (bf16[2,64,16,64]{1,3,2,0:T(8,128)(2,1)S(1)}, bf16[2,64,16,64]{1,3,2,0:T(8,128)(2,1)}, u32[]{:S(2)}) copy-start(bf16[2,64,16,64]{1,3,2,0:T(8,128)(2,1)} %copy.47) | copy-start | bytes 786436
  93.9 8.5 %copy-start.1 = (bf16[1,2,512,1024]{2,3,1,0:T(8,128)(2,1)}, bf16[1,2,512,1024]{2,3,1,0:T(8,128)(2,1)S(1)}, u32[]{:S(2)}) copy-start(bf16[1,2,512,1024]{2,3,1,0:T(8,128)(2,1)S(1)} %get-tuple-element.39) | copy-start | bytes 6291460
  93.9 3.4 %copy-start.11 = (bf16[2,64,16,64]{1,3,2,0:T(8,128)(2,1)S(1)}, bf16[2,64,16,64]{1,3,2,0:T(8,128)(2,1)}, u32[]{:S(2)}) copy-start(bf16[2,64,16,64]{1,3,2,0:T(8,128)(2,1)} %copy.49) | copy-start | bytes 786436
  97.3 5.1 %copy-start.2 = (f32[2,16,64,512]{3,2,1,0:T(8,128)S(1)}, f32[2,16,64,512]{3,2,1,0:T(8,128)}, u32[]{:S(2)}) copy-start(f32[2,16,64,512]{3,2,1,0:T(8,128)} %get-tuple-element.79) | copy-start | bytes 12582916
  97.3 5.1 %copy-start.8 = (bf16[1,2,512,1024]{2,3,1,0:T(8,128)(2,1)S(1)}, bf16[1,2,512,1024]{2,3,1,0:T(8,128)(2,1)}, u32[]{:S(2)}) copy-start(bf16[1,2,512,1024]{2,3,1,0:T(8,128)(2,1)} %get-tuple-element.40) | copy-start | bytes 6291460
  144.5 66.5 %collective-permute-start.15 = (f32[2,2,64,1024]{3,2,0,1:T(8,128)}, f32[2,2,64,1024]{3,2,0,1:T(8,128)}, u32[]{:S(2)}, u32[]{:S(2)}) collective-permute-start(f32[2,2,64,1024]{3,2,0,1:T(8,128)} %select_add_fusion), channel_id=1, source_target_pairs={{0,4},{1,5},{2,6},{3,7},{4,0},{5,1},{6,2},{7,3},{8,12},{9,13},{10,... | collective-permute-start | bytes 3145736 | tf_op jit(solution)/shard_map/ppermute | solution.py:51
  146.9 64.2 %collective-permute-start.14 = (f32[2,2,64,1024]{3,2,0,1:T(8,128)}, f32[2,2,64,1024]{3,2,0,1:T(8,128)}, u32[]{:S(2)}, u32[]{:S(2)}) collective-permute-start(f32[2,2,64,1024]{3,2,0,1:T(8,128)} %select_add_fusion.1), channel_id=1, source_target_pairs={{0,8},{1,9},{2,10},{3,11},{4,12},{5,13},{6,14},{7,15},{8,0},{9,1},... | collective-permute-start | bytes 3145736 | tf_op jit(solution)/shard_map/ppermute | solution.py:51
  150.2 7.0 %copy-start = (f32[2,4,64,1024]{3,2,1,0:T(8,128)}, f32[2,4,64,1024]{3,2,1,0:T(8,128)S(1)}, u32[]{:S(2)}) copy-start(f32[2,4,64,1024]{3,2,1,0:T(8,128)S(1)} %pad_add_fusion) | copy-start | bytes 6291460
  150.2 5.3 %copy-start.3 = (f32[2,16,64,512]{3,2,1,0:T(8,128)S(1)}, f32[2,16,64,512]{3,2,1,0:T(8,128)}, u32[]{:S(2)}) copy-start(f32[2,16,64,512]{3,2,1,0:T(8,128)} %get-tuple-element.79) | copy-start | bytes 12582916
  150.2 5.3 %copy-start.9 = (bf16[1,2,512,1024]{2,3,1,0:T(8,128)(2,1)S(1)}, bf16[1,2,512,1024]{2,3,1,0:T(8,128)(2,1)}, u32[]{:S(2)}) copy-start(bf16[1,2,512,1024]{2,3,1,0:T(8,128)(2,1)} %get-tuple-element.40) | copy-start | bytes 6291460
  151.3 18.0 %collective-permute-start.11 = (f32[2,64,1024]{2,1,0:T(8,128)}, f32[2,64,1024]{2,1,0:T(8,128)}, u32[]{:S(2)}, u32[]{:S(2)}) collective-permute-start(f32[2,64,1024]{2,1,0:T(8,128)} %get-tuple-element.42), channel_id=1, source_target_pairs={{1,0},{2,1},{3,2},{4,3},{5,4},{6,5},{7,6},{8,7},{9,8},{10,9},{11,1... | collective-permute-start | bytes 1572872 | tf_op jit(solution)/shard_map/ppermute | solution.py:57
  155.5 55.6 %collective-permute-start.13 = (f32[2,2,64,1024]{3,2,0,1:T(8,128)}, f32[2,2,64,1024]{3,2,0,1:T(8,128)}, u32[]{:S(2)}, u32[]{:S(2)}) collective-permute-start(f32[2,2,64,1024]{3,2,0,1:T(8,128)} %select_add_fusion.2), channel_id=1, source_target_pairs={{0,16},{1,17},{2,18},{3,19},{4,20},{5,21},{6,22},{7,23},{8,24},{9,... | collective-permute-start | bytes 3145736 | tf_op jit(solution)/shard_map/ppermute | solution.py:51
  157.2 12.0 %slice-start = ((f32[2,4,64,1024]{3,2,1,0:T(8,128)}), f32[2,2,64,1024]{3,2,1,0:T(8,128)S(1)}, s32[]{:S(2)}) async-start(f32[2,4,64,1024]{3,2,1,0:T(8,128)} %copy-done), calls=%async_computation | async-start | bytes 2097152 | tf_op jit(solution)/shard_map/slice | solution.py:157
  161.6 48.2 %collective-permute-start.12 = (f32[2,64,1024]{2,1,0:T(8,128)}, f32[2,64,1024]{2,1,0:T(8,128)}, u32[]{:S(2)}, u32[]{:S(2)}) collective-permute-start(f32[2,64,1024]{2,1,0:T(8,128)} %get-tuple-element.41), channel_id=1, source_target_pairs={{0,1},{1,2},{2,3},{3,4},{4,5},{5,6},{6,7},{7,8},{8,9},{9,10},{10,1... | collective-permute-start | bytes 1572872 | tf_op jit(solution)/shard_map/ppermute | solution.py:57

commit v3 on v2

--- a/solution.py
+++ b/solution.py
@@ -152,8 +152,9 @@
         + jnp.pad(split[:, :, 1], ((0, 0), (1, 1), (0, 0), (0, 0)))
         + jnp.pad(split[:, :, 2], ((0, 0), (2, 0), (0, 0), (0, 0)))
     )
-    from_right = passed_along(own_window[:, 0], "ctx", -1)
-    from_left = passed_along(own_window[:, -1], "ctx", 1)
+    low = jnp.bfloat16
+    from_right = passed_along(own_window[:, 0].astype(low), "ctx", -1).astype(jnp.float32)
+    from_left = passed_along(own_window[:, -1].astype(low), "ctx", 1).astype(jnp.float32)
     own_total = own_window[:, 1:-1]
     own_total = own_total.at[:, -1].add(from_right)
     own_total = own_total.at[:, 0].add(from_left)
@@ -164,7 +165,7 @@
             jnp.where(pickers[matching][None, j, :, None, None], terms[:, j : j + 1], 0.0)
             for j in range(block_count)
         )
-        own_total = own_total + partner_2(routed, "ctx", spread_bit)
+        own_total = own_total + partner_2(routed.astype(low), "ctx", spread_bit).astype(jnp.float32)
     attended_out = attended.reshape(tok_rows, width).astype(jnp.bfloat16)
     grad_queries = grad_query.reshape(tok_rows, width).astype(jnp.bfloat16)
     grad_keys = own_total[0].reshape(tok_rows, width).astype(jnp.bfloat16)

time: 216 us -> 194 us (0.90)
  the two profiles are of different devices: /device:TPU:192 before, /device:TPU:1 now
where the time goes in v3:
time: 194 us; the launch traced here: 192 us
  local copies, waits for them, and re-layouts  66.6 us (34%)
  waiting for transfers between devices  54.4 us (28%)
  starting transfers between devices  27.9 us (14%)
  other arithmetic  24.7 us (13%)
  matrix products  16.3 us (8%)
  between operations  2.41 us (1%)
    ppermute x4, waiting for transfers between devices, from_root(): received = lax.ppermute(carried, axis, [(i, i ^ step) for i in range(size)])  35 us
    another operation x4, local copies, waits for them, and re-layouts, local(): jnp.stack([grad_key, grad_value])  27.9 us
    ppermute x6, waiting for transfers between devices, partner_2(): lax.ppermute(array, axis, [(i, i ^ 1 << distance) for i in range(lax.axis...  18.4 us
    ppermute x6, starting transfers between devices, partner_2(): lax.ppermute(array, axis, [(i, i ^ 1 << distance) for i in range(lax.axis...  10.3 us
    concatenate x1, local copies, waits for them, and re-layouts, local(): every_key = jnp.concatenate([window, global_part] + random_parts, axis=2)  9.6 us
    ppermute x2, starting transfers between devices, passed_along(): return lax.ppermute(array, axis, pairs)  5.7 us
    unnamed x32, local copies, waits for them, and re-layouts  5.1 us
    broadcast_in_dim x2, local copies, waits for them, and re-layouts, local(): jnp.broadcast_to(fetched.reshape(2, 1, GLOBALS * BLOCK, width), (2, block...  4.29 us
  transfers between devices with their start and end apart: 16, of which 6 were waited for; matrix products, arithmetic and copies ran while one was open for 16% of the time, Pallas kernels for 0%

profile of v3, /device:TPU:1, one launch (start us, length us, event | category | flops | bytes accessed | tf_op | source)
XLA Modules:
  0.0 192.4 jit_solution(2514254078120396159)
XLA Ops:
  0.7 1.9 %pad_maximum_fusion.2 = bf16[2,128,1024]{2,1,0:T(8,128)(2,1)} fusion(bf16[1,128,1024]{2,1,0:T(8,128)(2,1)} %bitcast.157, bf16[1,128,1024]{2,1,0:T(8,128)(2,1)} %bitcast.154), kind=kLoop, calls=%fused_computation.43 | loop fusion | flops 262144 | bytes 1048576 | tf_op jit(solution)/shard_map/stack | solution.py:100
  2.6 3.8 %collective-permute-start.8 = (bf16[2,128,1024]{2,1,0:T(8,128)(2,1)}, bf16[2,128,1024]{2,1,0:T(8,128)(2,1)S(1)}, u32[]{:S(2)}, u32[]{:S(2)}) collective-permute-start(bf16[2,128,1024]{2,1,0:T(8,128)(2,1)} %pad_maximum_fusion.2), channel_id=1, source_target_pairs={{0,16},{1,17},{2,18},{3,19},{4,20},{5,21},{6,22},{7,23},{8,24},{9,... | collective-permute-start | bytes 1572872 | tf_op jit(solution)/shard_map/ppermute | solution.py:51
  6.4 1.6 collective-permute-start.9
  8.1 0.7 and_select_fusion
  8.7 0.6 fusion.35
  10.6 2.2 %fusion.24 = (bf16[2,1,64,1024]{3,2,1,0:T(8,128)(2,1)S(1)}, bf16[2,64,1024]{2,1,0:T(8,128)(2,1)}, bf16[2,64,1024]{2,1,0:T(8,128)(2,1)}, bf16[2,1,64,1024]{3,2,1,0:T(8,128)(2,1)S(1)}) fusion(s32[]{:T(128)S(6)} %select_n.109, bf16[1,128,1024]{2,1,0:T(8,128)(2,1)} %bitcast.155, bf16[1,128,1024]{2,1,0:T(8,128)(2,1)} %bitcast.158, s32[]{:T(128)S(6)} %select_n.110), kind=kLoop, calls=%fused_computation.65 | loop fusion | flops 2097152 | bytes 1572872 | tf_op jit(solution)/shard_map/stack | solution.py:106
  12.8 3.1 %collective-permute-start.1 = (bf16[2,64,1024]{2,1,0:T(8,128)(2,1)}, bf16[2,64,1024]{2,1,0:T(8,128)(2,1)}, u32[]{:S(2)}, u32[]{:S(2)}) collective-permute-start(bf16[2,64,1024]{2,1,0:T(8,128)(2,1)} %get-tuple-element.66), channel_id=1, source_target_pairs={{1,0},{2,1},{3,2},{4,3},{5,4},{6,5},{7,6},{8,7},{9,8},{10,9},{11,1... | collective-permute-start | bytes 786440 | tf_op jit(solution)/shard_map/ppermute | solution.py:24
  15.9 3.1 %collective-permute-start = (bf16[2,64,1024]{2,1,0:T(8,128)(2,1)}, bf16[2,64,1024]{2,1,0:T(8,128)(2,1)}, u32[]{:S(2)}, u32[]{:S(2)}) collective-permute-start(bf16[2,64,1024]{2,1,0:T(8,128)(2,1)} %get-tuple-element.65), channel_id=1, source_target_pairs={{0,1},{1,2},{2,3},{3,4},{4,5},{5,6},{6,7},{7,8},{8,9},{9,10},{10,1... | collective-permute-start | bytes 786440 | tf_op jit(solution)/shard_map/ppermute | solution.py:23
  19.1 0.7 select_bitcast_fusion.2
  21.6 1.3 copy.47
  23.3 1.3 copy.49
  24.6 2.6 %collective-permute-start.10 = (bf16[2,128,1024]{2,1,0:T(8,128)(2,1)}, bf16[2,128,1024]{2,1,0:T(8,128)(2,1)}, u32[]{:S(2)}, u32[]{:S(2)}) collective-permute-start(bf16[2,128,1024]{2,1,0:T(8,128)(2,1)} %pad_maximum_fusion.2), channel_id=1, source_target_pairs={{0,4},{1,5},{2,6},{3,7},{4,0},{5,1},{6,2},{7,3},{8,12},{9,13},{10,... | collective-permute-start | bytes 1572872 | tf_op jit(solution)/shard_map/ppermute | solution.py:51
  27.3 2.2 %collective-permute-start.3 = (bf16[2,64,1024]{2,1,0:T(8,128)(2,1)S(1)}, bf16[2,64,1024]{2,1,0:T(8,128)(2,1)S(1)}, u32[]{:S(2)}, u32[]{:S(2)}) collective-permute-start(bf16[2,64,1024]{2,1,0:T(8,128)(2,1)S(1)} %bitcast_select_fusion), channel_id=1, source_target_pairs={{0,2},{1,3},{2,0},{3,1},{4,6},{5,7},{6,4},{7,5},{8,10},{9,11},{10,... | collective-permute-start | bytes 786440 | tf_op jit(solution)/shard_map/ppermute | solution.py:41
  29.5 1.1 pad_maximum_fusion.1
  30.8 1.4 copy.58
  32.2 1.3 copy.59
  33.5 1.3 copy.60
  34.8 14.4 %collective-permute-done.3 = bf16[2,64,1024]{2,1,0:T(8,128)(2,1)S(1)} collective-permute-done((bf16[2,64,1024]{2,1,0:T(8,128)(2,1)S(1)}, bf16[2,64,1024]{2,1,0:T(8,128)(2,1)S(1)}, u32[]{:S(2)}, u32[]{:S(2)}) %collective-permute-start.3) | collective-permute-done | bytes 262176 | tf_op jit(solution)/shard_map/ppermute | solution.py:41
  50.7 1.1 slice_bitcast_fusion.10
  51.7 1.0 copy.42
  52.7 1.1 copy.41
  53.8 3.5 %collective-permute-done.4 = bf16[2,64,1024]{2,1,0:T(8,128)(2,1)} collective-permute-done((bf16[2,64,1024]{2,1,0:T(8,128)(2,1)S(1)}, bf16[2,64,1024]{2,1,0:T(8,128)(2,1)}, u32[]{:S(2)}, u32[]{:S(2)}) %collective-permute-start.4) | collective-permute-done | bytes 262176 | tf_op jit(solution)/shard_map/ppermute | solution.py:41
  57.3 1.0 broadcast_select_fusion.4
  58.3 0.5 collective-permute-start.5
  58.9 4.7 %collective-permute-done.5 = bf16[2,64,1024]{2,1,0:T(8,128)(2,1)S(1)} collective-permute-done((bf16[2,64,1024]{2,1,0:T(8,128)(2,1)S(1)}, bf16[2,64,1024]{2,1,0:T(8,128)(2,1)S(1)}, u32[]{:S(2)}, u32[]{:S(2)}) %collective-permute-start.5) | collective-permute-done | bytes 262176 | tf_op jit(solution)/shard_map/ppermute | solution.py:41
  63.7 1.1 collective-permute-start.6
  65.0 12.5 %collective-permute-done.6 = bf16[2,64,1024]{2,1,0:T(8,128)(2,1)S(1)} collective-permute-done((bf16[2,64,1024]{2,1,0:T(8,128)(2,1)S(1)}, bf16[2,64,1024]{2,1,0:T(8,128)(2,1)S(1)}, u32[]{:S(2)}, u32[]{:S(2)}) %collective-permute-start.6) | collective-permute-done | bytes 262176 | tf_op jit(solution)/shard_map/ppermute | solution.py:41
  77.5 1.9 collective-permute-start.7
  79.6 1.0 collective-permute-done.7
  80.6 0.8 pad_maximum_fusion.3
  81.5 2.0 %copy.36 = bf16[2,128,1024]{1,2,0:T(8,128)(2,1)} copy(bf16[2,128,1024]{2,1,0:T(8,128)(2,1)} %bitcast.160) | data formatting | bytes 1048576 | tf_op jit(solution)/shard_map/broadcast_in_dim | solution.py:114
  83.5 2.2 %broadcast_in_dim.246 = bf16[2,2,128,1024]{2,3,1,0:T(8,128)(2,1)} broadcast(bf16[2,128,1024]{1,2,0:T(8,128)(2,1)} %copy.36), dimensions={0,2,3} | broadcast | bytes 1572864 | tf_op jit(solution)/shard_map/broadcast_in_dim | solution.py:114
  85.8 9.6 %concatenate.15 = bf16[2,2,512,1024]{2,3,1,0:T(8,128)(2,1)} concatenate(bf16[2,2,64,1024]{2,3,1,0:T(8,128)(2,1)} %copy.58, bf16[2,2,64,1024]{2,3,1,0:T(8,128)(2,1)} %copy.59, bf16[2,2,64,1024]{2,3,1,0:T(8,128)(2,1)} %copy.60, bf16[2,2,128,1024]{2,3,1,0:T(8,128)(2,1)} %broadcast_in_dim.246, bf16[2,2,64,1024]{2,3,1,0:T(8,128)(2,1)S(1)} %broadcast_select_fusion.2, ...), dimensions={2} | concatenate | bytes 8388608 | tf_op jit(solution)/shard_map/concatenate | solution.py:128
  95.4 4.0 %fusion.32 = (bf16[1,2,512,1024]{2,3,1,0:T(8,128)(2,1)S(1)}, bf16[1,2,512,1024]{2,3,1,0:T(8,128)(2,1)}) fusion(bf16[2,2,512,1024]{2,3,1,0:T(8,128)(2,1)} %concatenate.15), kind=kLoop, calls=%fused_computation.116 | loop fusion | bytes 8388608 | tf_op jit(solution)/shard_map/slice | solution.py:129
  99.4 3.4 %fusion.36 = (f32[2,16,64]{2,1,0:T(8,128)S(1)}, f32[2,16,64,512]{3,2,1,0:T(8,128)}) fusion(pred[2,512]{1,0:T(4,128)(4,1)S(1)} %add_add_fusion, bf16[2,64,16,64]{1,3,2,0:T(8,128)(2,1)S(1)} %copy-done.8, bf16[2,512,16,64]{1,3,2,0:T(8,128)(2,1)S(1)} %bitcast.151), kind=kOutput, calls=%fused_computation.120 | convolution fusion | flops 138412544 | bytes 6562816 | tf_op jit(solution)/shard_map/sub | solution.py:68
  102.8 3.8 %fusion.11 = bf16[2,64,16,64]{1,3,2,0:T(8,128)(2,1)S(1)} fusion(bf16[2,512,16,64]{1,3,2,0:T(8,128)(2,1)} %bitcast.161, f32[2,16,64,512]{3,2,1,0:T(8,128)} %get-tuple-element.81, f32[2,16,64]{2,1,0:T(8,128)S(1)} %get-tuple-element.80), kind=kOutput, calls=%fused_computation.20 | convolution fusion | flops 136445952 | bytes 6561792 | tf_op jit(solution)/shard_map/jhqk,jkhd->jqhd/dot_general | solution.py:72
  106.8 0.7 copy-done.7
  107.5 3.0 %fusion.1 = (f32[2,16,64]{2,1,0:T(8,128)S(1)}, f32[2,16,512,64]{2,3,1,0:T(8,128)}) fusion(f32[2,16,64,512]{3,2,1,0:T(8,128)S(1)} %copy-done.2, f32[2,16,64]{2,1,0:T(8,128)S(1)} %get-tuple-element.80, bf16[2,64,16,64]{1,3,2,0:T(8,128)(2,1)S(1)} %copy-done.9, bf16[2,512,16,64]{1,3,2,0:T(8,128)(2,1)S(1)} %bitcast.162), kind=kOutput, calls=%fused_computation.3 | convolution fusion | flops 137361408 | bytes 10764288 | tf_op jit(solution)/shard_map/jqhd,jkhd->jhqk/dot_general | solution.py:75
  110.5 2.7 %convolution_bitcast_fusion = f32[2,512,16,64]{1,3,2,0:T(8,128)} fusion(bf16[2,64,16,64]{1,3,2,0:T(8,128)(2,1)S(1)} %copy-done.9, f32[2,16,64,512]{3,2,1,0:T(8,128)S(1)} %copy-done.2, f32[2,16,64]{2,1,0:T(8,128)S(1)} %get-tuple-element.80), kind=kOutput, calls=%fused_computation.11 | convolution fusion | flops 136314880 | bytes 8658944 | tf_op jit(solution)/shard_map/jhqk,jqhd->jkhd/dot_general | solution.py:86
  113.3 7.1 %reshape.165 = f32[1,2,8,64,1024]{3,2,4,1,0:T(8,128)} reshape(f32[2,512,16,64]{1,3,2,0:T(8,128)} %convolution_bitcast_fusion) | data formatting | bytes 8388608 | tf_op jit(solution)/shard_map/stack | solution.py:149
  120.4 6.8 %copy.57 = f32[1,2,8,64,1024]{4,3,2,1,0:T(8,128)} copy(f32[1,2,8,64,1024]{3,2,4,1,0:T(8,128)} %reshape.165) | data formatting | bytes 8388608 | tf_op jit(solution)/shard_map/stack | solution.py:149
  127.2 3.9 %fusion.3 = bf16[2,16,64,512]{3,2,1,0:T(8,128)(2,1)S(1)} fusion(f32[2,16,512,64]{2,3,1,0:T(8,128)} %get-tuple-element.83, f32[2,16,64]{2,1,0:T(8,128)S(1)} %get-tuple-element.82, f32[2,16,64,512]{3,2,1,0:T(8,128)} %get-tuple-element.81, f32[2,16,64]{2,1,0:T(8,128)S(1)} %get-tuple-element.80), kind=kLoop, calls=%fused_computation.5 | loop fusion | flops 5242880 | bytes 10502144 | tf_op jit(solution)/shard_map/convert_element_type | solution.py:79
  131.2 2.7 %convolution_bitcast_fusion.1 = f32[2,512,16,64]{1,3,2,0:T(8,128)} fusion(bf16[2,64,16,64]{1,3,2,0:T(8,128)(2,1)S(1)} %copy-done.8, bf16[2,16,64,512]{3,2,1,0:T(8,128)(2,1)S(1)} %fusion.3), kind=kOutput, calls=%fused_computation.12 | convolution fusion | flops 134217728 | bytes 6553600 | tf_op jit(solution)/shard_map/jhqk,jqhd->jkhd/dot_general | solution.py:83
  133.8 7.1 %reshape.164 = f32[1,2,8,64,1024]{3,2,4,1,0:T(8,128)} reshape(f32[2,512,16,64]{1,3,2,0:T(8,128)} %convolution_bitcast_fusion.1) | data formatting | bytes 8388608 | tf_op jit(solution)/shard_map/stack | solution.py:149
  140.9 6.8 %copy.56 = f32[1,2,8,64,1024]{4,3,2,1,0:T(8,128)} copy(f32[1,2,8,64,1024]{3,2,4,1,0:T(8,128)} %reshape.164) | data formatting | bytes 8388608 | tf_op jit(solution)/shard_map/stack | solution.py:149
  147.8 3.4 %maximum_bitcast_fusion.1 = (f32[2,2,64,1024]{3,2,1,0:T(8,128)S(1)}, f32[2,2,64,1024]{3,2,1,0:T(8,128)S(1)}, f32[2,2,64,1024]{3,2,1,0:T(8,128)S(1)}, f32[2,2,64,...) fusion(f32[1,2,8,64,1024]{4,3,2,1,0:T(8,128)} %copy.57, ...), kind=kLoop, calls=%fused_computation.25 | loop fusion | flops 1572864 | bytes 14680064 | tf_op jit(solution)/shard_map/squeeze | solution.py:163
  151.2 1.0 add_convert_fusion.1
  152.2 0.8 collective-permute-start.15
  153.1 1.0 add_convert_fusion.2
  154.1 1.7 fusion.31
  155.8 0.8 slice_bitcast_fusion.7
  156.6 2.6 %collective-permute-start.11 = (bf16[2,64,1024]{2,1,0:T(8,128)(2,1)}, bf16[2,64,1024]{2,1,0:T(8,128)(2,1)}, u32[]{:S(2)}, u32[]{:S(2)}) collective-permute-start(bf16[2,64,1024]{2,1,0:T(8,128)(2,1)} %get-tuple-element.46), channel_id=1, source_target_pairs={{1,0},{2,1},{3,2},{4,3},{5,4},{6,5},{7,6},{8,7},{9,8},{10,9},{11,1... | collective-permute-start | bytes 786440 | tf_op jit(solution)/shard_map/ppermute | solution.py:57
  159.2 3.1 %collective-permute-start.12 = (bf16[2,64,1024]{2,1,0:T(8,128)(2,1)}, bf16[2,64,1024]{2,1,0:T(8,128)(2,1)S(1)}, u32[]{:S(2)}, u32[]{:S(2)}) collective-permute-start(bf16[2,64,1024]{2,1,0:T(8,128)(2,1)} %get-tuple-element.45), channel_id=1, source_target_pairs={{0,1},{1,2},{2,3},{3,4},{4,5},{5,6},{6,7},{7,8},{8,9},{9,10},{10,1... | collective-permute-start | bytes 786440 | tf_op jit(solution)/shard_map/ppermute | solution.py:57
  162.4 1.0 add_convert_fusion.3
  163.4 1.5 collective-permute-start.13
  164.9 0.7 fusion.12
  165.6 0.4 copy.44
  166.1 1.1 convert_element_type.69
  167.6 1.1 convert_element_type.73
  168.6 1.3 slice.264
  170.1 1.2 fusion.18
  171.4 18.4 %collective-permute-done.13 = bf16[2,2,64,1024]{3,2,0,1:T(8,128)(2,1)} collective-permute-done((bf16[2,2,64,1024]{3,2,0,1:T(8,128)(2,1)}, bf16[2,2,64,1024]{3,2,0,1:T(8,128)(2,1)}, u32[]{:S(2)}, u32[]{:S(2)}) %collective-permute-start.13) | collective-permute-done | bytes 524320 | tf_op jit(solution)/shard_map/ppermute | solution.py:51
  189.8 1.7 add_convert_fusion
  191.5 0.8 fusion.34
  (83 shorter events, 5.7 us)
Async XLA Ops:
  0.6 19.2 %copy-start.13 = (s32[2]{0:T(128)S(1)}, s32[2]{0:T(128)}, u32[]{:S(2)}) copy-start(s32[2]{0:T(128)} %param.15) | copy-start | bytes 28
  0.6 19.3 %copy-start.12 = (s32[2,3]{1,0:T(2,128)S(1)}, s32[2,3]{1,0:T(2,128)}, u32[]{:S(2)}) copy-start(s32[2,3]{1,0:T(2,128)} %param.14) | copy-start | bytes 76
  0.7 20.6 %copy-start.10 = (bf16[128,1024]{1,0:T(8,128)(2,1)S(1)}, bf16[128,1024]{1,0:T(8,128)(2,1)}, u32[]{:S(2)}) copy-start(bf16[128,1024]{1,0:T(8,128)(2,1)} %param.10) | copy-start | bytes 786436
  0.7 22.2 %copy-start.11 = (bf16[128,1024]{1,0:T(8,128)(2,1)S(1)}, bf16[128,1024]{1,0:T(8,128)(2,1)}, u32[]{:S(2)}) copy-start(bf16[128,1024]{1,0:T(8,128)(2,1)} %param.13) | copy-start | bytes 786436
  2.6 26.9 %copy-start.3 = (bf16[128,1024]{1,0:T(8,128)(2,1)S(1)}, bf16[128,1024]{1,0:T(8,128)(2,1)}, u32[]{:S(2)}) copy-start(bf16[128,1024]{1,0:T(8,128)(2,1)} %param.11) | copy-start | bytes 786436
  2.6 26.9 %copy-start.4 = (bf16[128,1024]{1,0:T(8,128)(2,1)S(1)}, bf16[128,1024]{1,0:T(8,128)(2,1)}, u32[]{:S(2)}) copy-start(bf16[128,1024]{1,0:T(8,128)(2,1)} %param.12) | copy-start | bytes 786436
  2.6 46.8 %collective-permute-start.8 = (bf16[2,128,1024]{2,1,0:T(8,128)(2,1)}, bf16[2,128,1024]{2,1,0:T(8,128)(2,1)S(1)}, u32[]{:S(2)}, u32[]{:S(2)}) collective-permute-start(bf16[2,128,1024]{2,1,0:T(8,128)(2,1)} %pad_maximum_fusion.2), channel_id=1, source_target_pairs={{0,16},{1,17},{2,18},{3,19},{4,20},{5,21},{6,22},{7,23},{8,24},{9,... | collective-permute-start | bytes 1572872 | tf_op jit(solution)/shard_map/ppermute | solution.py:51
  6.4 43.1 %collective-permute-start.9 = (bf16[2,128,1024]{2,1,0:T(8,128)(2,1)}, bf16[2,128,1024]{2,1,0:T(8,128)(2,1)S(1)}, u32[]{:S(2)}, u32[]{:S(2)}) collective-permute-start(bf16[2,128,1024]{2,1,0:T(8,128)(2,1)} %pad_maximum_fusion.2), channel_id=1, source_target_pairs={{0,8},{1,9},{2,10},{3,11},{4,12},{5,13},{6,14},{7,15},{8,0},{9,1},... | collective-permute-start | bytes 1572872 | tf_op jit(solution)/shard_map/ppermute | solution.py:51
  12.8 14.5 %collective-permute-start.1 = (bf16[2,64,1024]{2,1,0:T(8,128)(2,1)}, bf16[2,64,1024]{2,1,0:T(8,128)(2,1)}, u32[]{:S(2)}, u32[]{:S(2)}) collective-permute-start(bf16[2,64,1024]{2,1,0:T(8,128)(2,1)} %get-tuple-element.66), channel_id=1, source_target_pairs={{1,0},{2,1},{3,2},{4,3},{5,4},{6,5},{7,6},{8,7},{9,8},{10,9},{11,1... | collective-permute-start | bytes 786440 | tf_op jit(solution)/shard_map/ppermute | solution.py:24
  15.9 13.6 %collective-permute-start = (bf16[2,64,1024]{2,1,0:T(8,128)(2,1)}, bf16[2,64,1024]{2,1,0:T(8,128)(2,1)}, u32[]{:S(2)}, u32[]{:S(2)}) collective-permute-start(bf16[2,64,1024]{2,1,0:T(8,128)(2,1)} %get-tuple-element.65), channel_id=1, source_target_pairs={{0,1},{1,2},{2,3},{3,4},{4,5},{5,6},{6,7},{7,8},{8,9},{9,10},{10,1... | collective-permute-start | bytes 786440 | tf_op jit(solution)/shard_map/ppermute | solution.py:23
  19.8 4.7 %collective-permute-start.2 = (bf16[2,64,1024]{2,1,0:T(8,128)(2,1)}, bf16[2,64,1024]{2,1,0:T(8,128)(2,1)S(1)}, u32[]{:S(2)}, u32[]{:S(2)}) collective-permute-start(bf16[2,64,1024]{2,1,0:T(8,128)(2,1)} %select_bitcast_fusion.2), channel_id=1, source_target_pairs={{0,1},{1,0},{2,3},{3,2},{4,5},{5,4},{6,7},{7,6},{8,9},{9,8},{10,11... | collective-permute-start | bytes 786440 | tf_op jit(solution)/shard_map/ppermute | solution.py:37
  24.6 26.1 %collective-permute-start.10 = (bf16[2,128,1024]{2,1,0:T(8,128)(2,1)}, bf16[2,128,1024]{2,1,0:T(8,128)(2,1)}, u32[]{:S(2)}, u32[]{:S(2)}) collective-permute-start(bf16[2,128,1024]{2,1,0:T(8,128)(2,1)} %pad_maximum_fusion.2), channel_id=1, source_target_pairs={{0,4},{1,5},{2,6},{3,7},{4,0},{5,1},{6,2},{7,3},{8,12},{9,13},{10,... | collective-permute-start | bytes 1572872 | tf_op jit(solution)/shard_map/ppermute | solution.py:51
  27.3 21.9 %collective-permute-start.3 = (bf16[2,64,1024]{2,1,0:T(8,128)(2,1)S(1)}, bf16[2,64,1024]{2,1,0:T(8,128)(2,1)S(1)}, u32[]{:S(2)}, u32[]{:S(2)}) collective-permute-start(bf16[2,64,1024]{2,1,0:T(8,128)(2,1)S(1)} %bitcast_select_fusion), channel_id=1, source_target_pairs={{0,2},{1,3},{2,0},{3,1},{4,6},{5,7},{6,4},{7,5},{8,10},{9,11},{10,... | collective-permute-start | bytes 786440 | tf_op jit(solution)/shard_map/ppermute | solution.py:41
  49.3 8.0 %collective-permute-start.4 = (bf16[2,64,1024]{2,1,0:T(8,128)(2,1)S(1)}, bf16[2,64,1024]{2,1,0:T(8,128)(2,1)}, u32[]{:S(2)}, u32[]{:S(2)}) collective-permute-start(bf16[2,64,1024]{2,1,0:T(8,128)(2,1)S(1)} %broadcast_select_fusion.3), channel_id=1, source_target_pairs={{0,4},{1,5},{2,6},{3,7},{4,0},{5,1},{6,2},{7,3},{8,12},{9,13},{10,... | collective-permute-start | bytes 786440 | tf_op jit(solution)/shard_map/ppermute | solution.py:41
  53.8 25.6 %copy-start.5 = (bf16[2,64,1024]{1,2,0:T(8,128)(2,1)S(1)}, bf16[2,64,1024]{1,2,0:T(8,128)(2,1)}, u32[]{:S(2)}) copy-start(bf16[2,64,1024]{1,2,0:T(8,128)(2,1)} %copy.42) | copy-start | bytes 786436
  53.8 25.6 %copy-start.6 = (bf16[2,64,1024]{1,2,0:T(8,128)(2,1)S(1)}, bf16[2,64,1024]{1,2,0:T(8,128)(2,1)}, u32[]{:S(2)}) copy-start(bf16[2,64,1024]{1,2,0:T(8,128)(2,1)} %copy.41) | copy-start | bytes 786436
  58.3 5.3 %collective-permute-start.5 = (bf16[2,64,1024]{2,1,0:T(8,128)(2,1)S(1)}, bf16[2,64,1024]{2,1,0:T(8,128)(2,1)S(1)}, u32[]{:S(2)}, u32[]{:S(2)}) collective-permute-start(bf16[2,64,1024]{2,1,0:T(8,128)(2,1)S(1)} %broadcast_select_fusion.4), channel_id=1, source_target_pairs={{0,8},{1,9},{2,10},{3,11},{4,12},{5,13},{6,14},{7,15},{8,0},{9,1},... | collective-permute-start | bytes 786440 | tf_op jit(solution)/shard_map/ppermute | solution.py:41
  63.7 13.7 %collective-permute-start.6 = (bf16[2,64,1024]{2,1,0:T(8,128)(2,1)S(1)}, bf16[2,64,1024]{2,1,0:T(8,128)(2,1)S(1)}, u32[]{:S(2)}, u32[]{:S(2)}) collective-permute-start(bf16[2,64,1024]{2,1,0:T(8,128)(2,1)S(1)} %broadcast_select_fusion.5), channel_id=1, source_target_pairs={{0,16},{1,17},{2,18},{3,19},{4,20},{5,21},{6,22},{7,23},{8,24},{9,... | collective-permute-start | bytes 786440 | tf_op jit(solution)/shard_map/ppermute | solution.py:41
  77.5 3.1 %collective-permute-start.7 = (bf16[2,64,1024]{2,1,0:T(8,128)(2,1)S(1)}, bf16[2,64,1024]{2,1,0:T(8,128)(2,1)S(1)}, u32[]{:S(2)}, u32[]{:S(2)}) collective-permute-start(bf16[2,64,1024]{2,1,0:T(8,128)(2,1)S(1)} %broadcast_select_fusion.6), channel_id=1, source_target_pairs={{0,1},{1,0},{2,3},{3,2},{4,5},{5,4},{6,7},{7,6},{8,9},{9,8},{10,11... | collective-permute-start | bytes 786440 | tf_op jit(solution)/shard_map/ppermute | solution.py:44
  95.4 4.0 %copy-start.8 = (bf16[2,64,16,64]{1,3,2,0:T(8,128)(2,1)S(1)}, bf16[2,64,16,64]{1,3,2,0:T(8,128)(2,1)}, u32[]{:S(2)}) copy-start(bf16[2,64,16,64]{1,3,2,0:T(8,128)(2,1)} %copy.47) | copy-start | bytes 786436
  99.4 7.2 %copy-start = (bf16[1,2,512,1024]{2,3,1,0:T(8,128)(2,1)}, bf16[1,2,512,1024]{2,3,1,0:T(8,128)(2,1)S(1)}, u32[]{:S(2)}) copy-start(bf16[1,2,512,1024]{2,3,1,0:T(8,128)(2,1)S(1)} %get-tuple-element.41) | copy-start | bytes 6291460
  102.8 4.0 %copy-start.2 = (f32[2,16,64,512]{3,2,1,0:T(8,128)S(1)}, f32[2,16,64,512]{3,2,1,0:T(8,128)}, u32[]{:S(2)}) copy-start(f32[2,16,64,512]{3,2,1,0:T(8,128)} %get-tuple-element.81) | copy-start | bytes 12582916
  102.8 4.7 %copy-start.7 = (bf16[1,2,512,1024]{2,3,1,0:T(8,128)(2,1)S(1)}, bf16[1,2,512,1024]{2,3,1,0:T(8,128)(2,1)}, u32[]{:S(2)}) copy-start(bf16[1,2,512,1024]{2,3,1,0:T(8,128)(2,1)} %get-tuple-element.42) | copy-start | bytes 6291460
  102.8 4.7 %copy-start.9 = (bf16[2,64,16,64]{1,3,2,0:T(8,128)(2,1)S(1)}, bf16[2,64,16,64]{1,3,2,0:T(8,128)(2,1)}, u32[]{:S(2)}) copy-start(bf16[2,64,16,64]{1,3,2,0:T(8,128)(2,1)} %copy.49) | copy-start | bytes 786436
  152.2 19.2 %collective-permute-start.15 = (bf16[2,2,64,1024]{3,2,0,1:T(8,128)(2,1)}, bf16[2,2,64,1024]{3,2,0,1:T(8,128)(2,1)}, u32[]{:S(2)}, u32[]{:S(2)}) collective-permute-start(bf16[2,2,64,1024]{3,2,0,1:T(8,128)(2,1)} %add_convert_fusion.1), channel_id=1, source_target_pairs={{0,4},{1,5},{2,6},{3,7},{4,0},{5,1},{6,2},{7,3},{8,12},{9,13},{10,... | collective-permute-start | bytes 1572872 | tf_op jit(solution)/shard_map/ppermute | solution.py:51
  154.1 17.3 %collective-permute-start.14 = (bf16[2,2,64,1024]{3,2,0,1:T(8,128)(2,1)}, bf16[2,2,64,1024]{3,2,0,1:T(8,128)(2,1)}, u32[]{:S(2)}, u32[]{:S(2)}) collective-permute-start(bf16[2,2,64,1024]{3,2,0,1:T(8,128)(2,1)} %add_convert_fusion.2), channel_id=1, source_target_pairs={{0,8},{1,9},{2,10},{3,11},{4,12},{5,13},{6,14},{7,15},{8,0},{9,1},... | collective-permute-start | bytes 1572872 | tf_op jit(solution)/shard_map/ppermute | solution.py:51
  154.1 10.8 %copy-start.1 = (bf16[1,2,512,1024]{2,3,1,0:T(8,128)(2,1)S(1)}, bf16[1,2,512,1024]{2,3,1,0:T(8,128)(2,1)}, u32[]{:S(2)}) copy-start(bf16[1,2,512,1024]{2,3,1,0:T(8,128)(2,1)} %copy-done) | copy-start | bytes 6291460
  156.6 13.4 %collective-permute-start.11 = (bf16[2,64,1024]{2,1,0:T(8,128)(2,1)}, bf16[2,64,1024]{2,1,0:T(8,128)(2,1)}, u32[]{:S(2)}, u32[]{:S(2)}) collective-permute-start(bf16[2,64,1024]{2,1,0:T(8,128)(2,1)} %get-tuple-element.46), channel_id=1, source_target_pairs={{1,0},{2,1},{3,2},{4,3},{5,4},{6,5},{7,6},{8,7},{9,8},{10,9},{11,1... | collective-permute-start | bytes 786440 | tf_op jit(solution)/shard_map/ppermute | solution.py:57
  159.2 12.1 %collective-permute-start.12 = (bf16[2,64,1024]{2,1,0:T(8,128)(2,1)}, bf16[2,64,1024]{2,1,0:T(8,128)(2,1)S(1)}, u32[]{:S(2)}, u32[]{:S(2)}) collective-permute-start(bf16[2,64,1024]{2,1,0:T(8,128)(2,1)} %get-tuple-element.45), channel_id=1, source_target_pairs={{0,1},{1,2},{2,3},{3,4},{4,5},{5,6},{6,7},{7,8},{8,9},{9,10},{10,1... | collective-permute-start | bytes 786440 | tf_op jit(solution)/shard_map/ppermute | solution.py:57
  163.4 26.4 %collective-permute-start.13 = (bf16[2,2,64,1024]{3,2,0,1:T(8,128)(2,1)}, bf16[2,2,64,1024]{3,2,0,1:T(8,128)(2,1)}, u32[]{:S(2)}, u32[]{:S(2)}) collective-permute-start(bf16[2,2,64,1024]{3,2,0,1:T(8,128)(2,1)} %add_convert_fusion.3), channel_id=1, source_target_pairs={{0,16},{1,17},{2,18},{3,19},{4,20},{5,21},{6,22},{7,23},{8,24},{9,... | collective-permute-start | bytes 1572872 | tf_op jit(solution)/shard_map/ppermute | solution.py:51

commit v4 on v3

v4 whole, which is shorter than its diff:
```python
import jax
import jax.numpy as jnp
from jax import lax
from jax.sharding import PartitionSpec as P
from jax.experimental import pallas as pl
from jax.experimental.pallas import tpu as pltpu

HEADS = 16
HEAD_DIM = 64
BLOCK = 64
RAND = 3
GLOBALS = 2


SCORE_FLOOR = -1e30


def padded_2(array, sides, width):
    for axis, dim in sides:
        size, length = (lax.axis_size(axis), array.shape[dim])
        up = [(i, (i + 1) % size) for i in range(size - 1)]
        down = [(j, i) for i, j in up]
        last = lax.slice_in_dim(array, length - width, length, axis=dim)
        first = lax.slice_in_dim(array, 0, width, axis=dim)
        before = lax.ppermute(last, axis, up)
        after = lax.ppermute(first, axis, down)
        array = jnp.concatenate([before, array, after], axis=dim)
    return array


def from_root(blocks, axis, sources):
    size = lax.axis_size(axis)
    position = lax.axis_index(axis)
    shape = (-1,) + (1,) * (blocks.ndim - 2)
    core = position % 2
    sibling = [(i, i ^ 1) for i in range(size)]
    mine = jnp.where(core == 0, blocks[:, 0], blocks[:, 1])
    theirs = jnp.where(core == 0, blocks[:, 1], blocks[:, 0])
    received = lax.ppermute(theirs, axis, sibling)
    carried = jnp.where((sources == (position ^ 1)).reshape(shape), received, mine)
    for level in range(1, size.bit_length() - 1):
        step = 1 << level
        received = lax.ppermute(carried, axis, [(i, i ^ step) for i in range(size)])
        partner_holds = ((position ^ step) >> level) == (sources >> level)
        carried = jnp.where(partner_holds.reshape(shape), received, carried)
    other = lax.ppermute(carried, axis, sibling)
    first = jnp.where(core == 0, carried, other)
    second = jnp.where(core == 0, other, carried)
    return jnp.stack([first, second], axis=1)


def partner_2(array, axis, distance):
    return lax.ppermute(array, axis, [(i, i ^ 1 << distance) for i in range(lax.axis_size(axis))])


def passed_along(array, axis, by):
    size = lax.axis_size(axis)
    pairs = [(i, i + by) for i in range(size) if 0 <= i + by < size]
    return lax.ppermute(array, axis, pairs)


LANES = 128


def attend_kernel(meta_ref, q_ref, g_ref, win_ref, glob_ref, *rest):
    partner_refs = rest[:RAND]
    att_ref, gq_ref, gwin_ref, gpart_ref = rest[RAND:]
    block_count = q_ref.shape[0] // BLOCK
    listed = 3 + GLOBALS + RAND
    scale_factor = HEAD_DIM ** (-0.5)
    gwin_ref[...] = jnp.zeros_like(gwin_ref)
    gpart_ref[...] = jnp.zeros_like(gpart_ref)
    lane = lax.broadcasted_iota(jnp.int32, (BLOCK, LANES), 1)
    col = lax.broadcasted_iota(jnp.int32, (BLOCK, listed * BLOCK), 1)
    nt = (((1,), (1,)), ((), ()))
    tn = (((0,), (0,)), ((), ()))
    base = (3 + GLOBALS) * BLOCK
    for j in range(block_count):
        rows = pl.ds(j * BLOCK, BLOCK)
        q = q_ref[rows, :]
        g = g_ref[rows, :]
        picks = [pl.multiple_of(meta_ref[j * RAND + r] * BLOCK, BLOCK) for r in range(RAND)]
        left_ok = meta_ref[block_count * RAND + j]
        right_ok = meta_ref[block_count * RAND + block_count + j]

        def gather(kv):
            parts = [win_ref[kv, pl.ds(j * BLOCK, 3 * BLOCK), :], glob_ref[kv]]
            for r in range(RAND):
                parts.append(partner_refs[r][kv, pl.ds(picks[r], BLOCK), :])
            return jnp.concatenate(parts, axis=0)

        k = gather(0)
        v = gather(1)
        invalid = ((col < BLOCK) & (left_ok == 0)) | (
            (col >= 2 * BLOCK) & (col < 3 * BLOCK) & (right_ok == 0)
        )
        att = jnp.zeros((BLOCK, LANES), jnp.float32)
        gq = jnp.zeros((BLOCK, LANES), jnp.float32)
        gk = jnp.zeros((listed * BLOCK, LANES), jnp.float32)
        gv = jnp.zeros((listed * BLOCK, LANES), jnp.float32)
        for h in range(LANES // HEAD_DIM):
            in_head = (lane >= h * HEAD_DIM) & (lane < (h + 1) * HEAD_DIM)
            qh = jnp.where(in_head, q, jnp.zeros_like(q))
            gh = jnp.where(in_head, g, jnp.zeros_like(g))
            scores = lax.dot_general(qh, k, nt, preferred_element_type=jnp.float32) * scale_factor
            scores = jnp.where(invalid, SCORE_FLOOR, scores)
            highest = jnp.max(scores, axis=-1, keepdims=True)
            raw_weights = jnp.exp(scores - highest)
            weight_total = jnp.sum(raw_weights, axis=-1, keepdims=True)
            probs = raw_weights / weight_total
            probs_low = probs.astype(jnp.bfloat16)
            att = jnp.where(
                in_head, jnp.dot(probs_low, v, preferred_element_type=jnp.float32), att
            )
            grad_probs = lax.dot_general(gh, v, nt, preferred_element_type=jnp.float32)
            inner = jnp.sum(probs * grad_probs, axis=-1, keepdims=True)
            grad_scores = (scale_factor * probs * (grad_probs - inner)).astype(jnp.bfloat16)
            gq = jnp.where(
                in_head, jnp.dot(grad_scores, k, preferred_element_type=jnp.float32), gq
            )
            gk = gk + lax.dot_general(grad_scores, qh, tn, preferred_element_type=jnp.float32)
            gv = gv + lax.dot_general(probs_low, gh, tn, preferred_element_type=jnp.float32)
        att_ref[rows, :] = att.astype(att_ref.dtype)
        gq_ref[rows, :] = gq.astype(gq_ref.dtype)
        window = pl.ds(j * BLOCK, 3 * BLOCK)
        gwin_ref[0, window, :] += gk[: 3 * BLOCK]
        gwin_ref[1, window, :] += gv[: 3 * BLOCK]
        for r in range(RAND):
            there = pl.ds(picks[r], BLOCK)
            gpart_ref[r, 0, there, :] += gk[base + r * BLOCK : base + (r + 1) * BLOCK]
            gpart_ref[r, 1, there, :] += gv[base + r * BLOCK : base + (r + 1) * BLOCK]


def attend(meta, queries, grad_out, padded, glob, partners):
    tok_rows, width = queries.shape
    framed = padded.shape[1]
    pairs = width // LANES
    row_spec = pl.BlockSpec((tok_rows, LANES), lambda p, m: (0, p))
    win_spec = pl.BlockSpec((2, framed, LANES), lambda p, m: (0, 0, p))
    glob_spec = pl.BlockSpec((2, glob.shape[1], LANES), lambda p, m: (0, 0, p))
    part_spec = pl.BlockSpec((2, tok_rows, LANES), lambda p, m: (0, 0, p))
    out_specs = [
        row_spec,
        row_spec,
        win_spec,
        pl.BlockSpec((RAND, 2, tok_rows, LANES), lambda p, m: (0, 0, 0, p)),
    ]
    out_shape = [
        jax.ShapeDtypeStruct((tok_rows, width), jnp.bfloat16),
        jax.ShapeDtypeStruct((tok_rows, width), jnp.bfloat16),
        jax.ShapeDtypeStruct((2, framed, width), jnp.float32),
        jax.ShapeDtypeStruct((RAND, 2, tok_rows, width), jnp.float32),
    ]
    return pl.pallas_call(
        attend_kernel,
        grid_spec=pltpu.PrefetchScalarGridSpec(
            num_scalar_prefetch=1,
            grid=(pairs,),
            in_specs=[row_spec, row_spec, win_spec, glob_spec] + [part_spec] * RAND,
            out_specs=out_specs,
        ),
        out_shape=out_shape,
        compiler_params=pltpu.CompilerParams(dimension_semantics=("arbitrary",)),
    )(meta, queries, grad_out, padded, glob, *partners)


def local(queries, keys, values, grad_out, rand_blocks, global_ids):
    tok_rows, width = queries.shape
    block_count = tok_rows // BLOCK
    ctx_count = lax.axis_size("ctx")
    position = lax.axis_index("ctx")
    top_bit = ctx_count.bit_length() - 1
    block_iota = jnp.arange(block_count, dtype=jnp.int32)
    stacked = jnp.stack([keys, values])
    padded = padded_2(stacked, (("ctx", 1),), BLOCK)
    owners = global_ids // block_count
    local_ids = global_ids % block_count
    own_pieces = jnp.stack(
        [
            lax.dynamic_slice_in_dim(stacked, local_ids[global_slot] * BLOCK, BLOCK, 1)
            for global_slot in range(GLOBALS)
        ],
        axis=1,
    )
    fetched = jnp.swapaxes(from_root(jnp.swapaxes(own_pieces, 0, 1), "ctx", owners), 0, 1)
    glob = fetched.reshape(2, GLOBALS * BLOCK, width)
    spread = [top_bit - 1 - matching for matching in range(RAND)]
    partners = [partner_2(stacked, "ctx", bit) for bit in spread]
    global_block = position * block_count + block_iota
    seq_blocks = block_count * ctx_count
    meta = jnp.concatenate(
        [
            rand_blocks.reshape(-1).astype(jnp.int32),
            (global_block > 0).astype(jnp.int32),
            (global_block < seq_blocks - 1).astype(jnp.int32),
        ]
    )
    attended_out, grad_queries, gwin, gpart = attend(
        meta, queries, grad_out, padded, glob, partners
    )
    low = jnp.bfloat16
    from_right = passed_along(gwin[:, :BLOCK].astype(low), "ctx", -1).astype(jnp.float32)
    from_left = passed_along(gwin[:, -BLOCK:].astype(low), "ctx", 1).astype(jnp.float32)
    own_total = gwin[:, BLOCK:-BLOCK]
    own_total = own_total.at[:, tok_rows - BLOCK :].add(from_right)
    own_total = own_total.at[:, :BLOCK].add(from_left)
    for matching in range(RAND):
        own_total = own_total + partner_2(gpart[matching].astype(low), "ctx", spread[matching]).astype(
            jnp.float32
        )
    grad_keys = own_total[0].astype(jnp.bfloat16)
    grad_values = own_total[1].astype(jnp.bfloat16)
    return (attended_out, grad_queries, grad_keys, grad_values)


def solution(mesh):
    placed = (
        P(("dp", "ctx"), None),
        P(("dp", "ctx"), None),
        P(("dp", "ctx"), None),
        P(("dp", "ctx"), None),
        P(("dp", "ctx"), None),
        P("dp"),
    )
    return jax.shard_map(
        local,
        mesh=mesh,
        in_specs=placed,
        out_specs=(
            P(("dp", "ctx"), None),
            P(("dp", "ctx"), None),
            P(("dp", "ctx"), None),
            P(("dp", "ctx"), None),
        ),
        check_vma=False,
    )
```

time: 194 us -> 142 us (0.73)
  the two profiles are of different devices: /device:TPU:1 before, /device:TPU:6 now
where the time goes in v4:
time: 142 us
  waiting for transfers between devices  75.2 us (53%)
  starting transfers between devices  27.6 us (19%)
  Pallas kernels  25.5 us (18%)
  other arithmetic  8.98 us (6%)
  local copies, waits for them, and re-layouts  2.62 us (2%)
  between operations  2.23 us (2%)
    ppermute x6, waiting for transfers between devices, partner_2(): lax.ppermute(array, axis, [(i, i ^ 1 << distance) for i in range(lax.axis...  39.7 us
    ppermute x4, waiting for transfers between devices, from_root(): received = lax.ppermute(carried, axis, [(i, i ^ step) for i in range(size)])  33.1 us
    pallas_call x1, Pallas kernels, attend(): pl.pallas_call(attend_kernel, grid_spec=pltpu.PrefetchScalarGridSpec(num_...  25.5 us
    ppermute x6, starting transfers between devices, partner_2(): lax.ppermute(array, axis, [(i, i ^ 1 << distance) for i in range(lax.axis...  11.1 us
    ppermute x4, starting transfers between devices, from_root(): received = lax.ppermute(carried, axis, [(i, i ^ step) for i in range(size)])  10.3 us
  transfers between devices with their start and end apart: 16, of which 9 were waited for; matrix products, arithmetic and copies ran while one was open for 3% of the time, Pallas kernels for 0%

profile of v4, /device:TPU:6, one launch (start us, length us, event | category | flops | bytes accessed | tf_op | source)
XLA Modules:
  0.0 142.2 jit_solution(12453481945373559816)
XLA Ops:
  0.6 0.0 copy-start.7
  0.6 0.7 and_select_fusion
  1.4 0.6 fusion.10
  3.3 1.4 fusion.6
  4.7 0.1 maximum_bitcast_fusion
  4.7 0.0 copy-start.2
  4.7 0.0 copy-start.3
  4.8 0.1 collective-permute-start.2
  4.9 0.0 copy-done.7
  4.9 1.5 %collective-permute-done.2 = bf16[2,64,1024]{2,1,0:T(8,128)(2,1)S(1)} collective-permute-done((bf16[2,64,1024]{2,1,0:T(8,128)(2,1)S(1)}, bf16[2,64,1024]{2,1,0:T(8,128)(2,1)S(1)}, u32[]{:S(2)}, u32[]{:S(2)}) %collective-permute-start.2) | collective-permute-done | bytes 262176 | tf_op jit(solution)/shard_map/ppermute | solution.py:39
  6.4 0.1 fusion.2
  6.5 1.7 %collective-permute-start.3 = (bf16[2,64,1024]{2,1,0:T(8,128)(2,1)S(1)}, bf16[2,64,1024]{2,1,0:T(8,128)(2,1)S(1)}, u32[]{:S(2)}, u32[]{:S(2)}) collective-permute-start(bf16[2,64,1024]{2,1,0:T(8,128)(2,1)S(1)} %fusion.2), channel_id=1, source_target_pairs={{0,2},{1,3},{2,0},{3,1},{4,6},{5,7},{6,4},{7,5},{8,10},{9,11},{10,... | collective-permute-start | bytes 786440 | tf_op jit(solution)/shard_map/ppermute | solution.py:43
  8.2 6.8 %collective-permute-done.3 = bf16[2,64,1024]{2,1,0:T(8,128)(2,1)S(1)} collective-permute-done((bf16[2,64,1024]{2,1,0:T(8,128)(2,1)S(1)}, bf16[2,64,1024]{2,1,0:T(8,128)(2,1)S(1)}, u32[]{:S(2)}, u32[]{:S(2)}) %collective-permute-start.3) | collective-permute-done | bytes 262176 | tf_op jit(solution)/shard_map/ppermute | solution.py:43
  14.9 0.1 broadcast_select_fusion
  15.0 3.3 %collective-permute-start.4 = (bf16[2,64,1024]{2,1,0:T(8,128)(2,1)S(1)}, bf16[2,64,1024]{2,1,0:T(8,128)(2,1)S(1)}, u32[]{:S(2)}, u32[]{:S(2)}) collective-permute-start(bf16[2,64,1024]{2,1,0:T(8,128)(2,1)S(1)} %broadcast_select_fusion), channel_id=1, source_target_pairs={{0,4},{1,5},{2,6},{3,7},{4,0},{5,1},{6,2},{7,3},{8,12},{9,13},{10,... | collective-permute-start | bytes 786440 | tf_op jit(solution)/shard_map/ppermute | solution.py:43
  18.3 5.8 %collective-permute-done.4 = bf16[2,64,1024]{2,1,0:T(8,128)(2,1)S(1)} collective-permute-done((bf16[2,64,1024]{2,1,0:T(8,128)(2,1)S(1)}, bf16[2,64,1024]{2,1,0:T(8,128)(2,1)S(1)}, u32[]{:S(2)}, u32[]{:S(2)}) %collective-permute-start.4) | collective-permute-done | bytes 262176 | tf_op jit(solution)/shard_map/ppermute | solution.py:43
  24.1 0.1 broadcast_select_fusion.1
  24.2 2.0 %collective-permute-start.5 = (bf16[2,64,1024]{2,1,0:T(8,128)(2,1)S(1)}, bf16[2,64,1024]{2,1,0:T(8,128)(2,1)S(1)}, u32[]{:S(2)}, u32[]{:S(2)}) collective-permute-start(bf16[2,64,1024]{2,1,0:T(8,128)(2,1)S(1)} %broadcast_select_fusion.1), channel_id=1, source_target_pairs={{0,8},{1,9},{2,10},{3,11},{4,12},{5,13},{6,14},{7,15},{8,0},{9,1},... | collective-permute-start | bytes 786440 | tf_op jit(solution)/shard_map/ppermute | solution.py:43
  26.2 4.9 %collective-permute-done.5 = bf16[2,64,1024]{2,1,0:T(8,128)(2,1)S(1)} collective-permute-done((bf16[2,64,1024]{2,1,0:T(8,128)(2,1)S(1)}, bf16[2,64,1024]{2,1,0:T(8,128)(2,1)S(1)}, u32[]{:S(2)}, u32[]{:S(2)}) %collective-permute-start.5) | collective-permute-done | bytes 262176 | tf_op jit(solution)/shard_map/ppermute | solution.py:43
  31.1 0.1 broadcast_select_fusion.2
  31.2 3.4 %collective-permute-start.6 = (bf16[2,64,1024]{2,1,0:T(8,128)(2,1)S(1)}, bf16[2,64,1024]{2,1,0:T(8,128)(2,1)S(1)}, u32[]{:S(2)}, u32[]{:S(2)}) collective-permute-start(bf16[2,64,1024]{2,1,0:T(8,128)(2,1)S(1)} %broadcast_select_fusion.2), channel_id=1, source_target_pairs={{0,16},{1,17},{2,18},{3,19},{4,20},{5,21},{6,22},{7,23},{8,24},{9,... | collective-permute-start | bytes 786440 | tf_op jit(solution)/shard_map/ppermute | solution.py:43
  34.6 0.0 copy-done.2
  34.6 0.0 copy-done.3
  34.6 0.1 pad_maximum_fusion.1
  34.6 3.3 %collective-permute-start.10 = (bf16[2,128,1024]{2,1,0:T(8,128)(2,1)S(1)}, bf16[2,128,1024]{2,1,0:T(8,128)(2,1)S(1)}, u32[]{:S(2)}, u32[]{:S(2)}) collective-permute-start(bf16[2,128,1024]{2,1,0:T(8,128)(2,1)S(1)} %pad_maximum_fusion.1), channel_id=1, source_target_pairs={{0,4},{1,5},{2,6},{3,7},{4,0},{5,1},{6,2},{7,3},{8,12},{9,13},{10,... | collective-permute-start | bytes 1572872 | tf_op jit(solution)/shard_map/ppermute | solution.py:53
  37.9 0.0 collective-permute-start.8
  38.0 2.0 %collective-permute-start = (bf16[2,64,1024]{2,1,0:T(8,128)(2,1)S(1)}, bf16[2,64,1024]{2,1,0:T(8,128)(2,1)}, u32[]{:S(2)}, u32[]{:S(2)}) collective-permute-start(bf16[2,64,1024]{2,1,0:T(8,128)(2,1)S(1)} %get-tuple-element.48), channel_id=1, source_target_pairs={{0,1},{1,2},{2,3},{3,4},{4,5},{5,6},{6,7},{7,8},{8,9},{9,10},{10,1... | collective-permute-start | bytes 786440 | tf_op jit(solution)/shard_map/ppermute | solution.py:25
  39.9 1.3 collective-permute-start.1
  41.2 15.6 %collective-permute-done.6 = bf16[2,64,1024]{2,1,0:T(8,128)(2,1)S(1)} collective-permute-done((bf16[2,64,1024]{2,1,0:T(8,128)(2,1)S(1)}, bf16[2,64,1024]{2,1,0:T(8,128)(2,1)S(1)}, u32[]{:S(2)}, u32[]{:S(2)}) %collective-permute-start.6) | collective-permute-done | bytes 262176 | tf_op jit(solution)/shard_map/ppermute | solution.py:43
  56.9 0.1 broadcast_select_fusion.3
  56.9 0.1 collective-permute-start.7
  57.1 0.0 copy-done.8
  57.1 0.1 reshape.97
  57.2 0.0 collective-permute-done
  57.2 0.0 collective-permute-start.9
  57.2 0.6 pad_add_fusion.meta_ref
  57.8 0.0 collective-permute-done.1
  57.8 2.1 %pad_maximum_fusion.win_ref = bf16[2,256,1024]{2,1,0:T(8,128)(2,1)} fusion(bf16[2,64,1024]{2,1,0:T(8,128)(2,1)} %collective-permute-done.1, bf16[1,128,1024]{2,1,0:T(8,128)(2,1)S(1)} %bitcast.48, bf16[1,128,1024]{2,1,0:T(8,128)(2,1)S(1)} %bitcast.45, bf16[2,64,1024]{2,1,0:T(8,128)(2,1)} %collective-permute-done), kind=kLoop, calls=%fused_computation | loop fusion | flops 4194304 | bytes 2097152 | tf_op jit(solution)/shard_map/concatenate | solution.py:27
  59.9 0.0 collective-permute-done.7
  59.9 0.9 pad_maximum_fusion.2
  60.8 0.0 collective-permute-done.10.rest_2_
  60.8 6.2 %collective-permute-done.8.rest_0_ = bf16[2,128,1024]{2,1,0:T(8,128)(2,1)S(1)} collective-permute-done((bf16[2,128,1024]{2,1,0:T(8,128)(2,1)S(1)}, bf16[2,128,1024]{2,1,0:T(8,128)(2,1)S(1)}, u32[]{:S(2)}, u32[]{:S(2)}) %collective-permute-start.8) | collective-permute-done | bytes 524320 | tf_op jit(solution)/shard_map/ppermute | solution.py:53
  67.0 11.5 %collective-permute-done.9.rest_1_ = bf16[2,128,1024]{2,1,0:T(8,128)(2,1)S(1)} collective-permute-done((bf16[2,128,1024]{2,1,0:T(8,128)(2,1)S(1)}, bf16[2,128,1024]{2,1,0:T(8,128)(2,1)S(1)}, u32[]{:S(2)}, u32[]{:S(2)}) %collective-permute-start.9) | collective-permute-done | bytes 524320 | tf_op jit(solution)/shard_map/ppermute | solution.py:53
  78.5 0.0 copy-done.4
  78.5 0.8 copy-done.6
  79.3 25.5 %shard_map.93 = (bf16[128,1024]{1,0:T(8,128)(2,1)}, bf16[128,1024]{1,0:T(8,128)(2,1)}, f32[2,256,1024]{2,1,0:T(8,128)}, f32[3,2,128,1024]{3,2,1,0:T(8,128)}) custom-call(s32[10]{0:T(128)} %pad_add_fusion.meta_ref, bf16[128,1024]{1,0:T(8,128)(2,1)} %q_ref.1, bf16[128,1024]{1,0:T(8,128)(2,1)} %g_ref.1, bf16[2,256,1024]{2,1,0:T(8,128)(2,1)} %pad_maximum_fusion.win_ref, ...), custom_call_target="tpu_custom_call" | custom-call | tf_op jit(solution)/shard_map/pallas_call | solution.py:154
  104.8 1.9 %convert.13 = bf16[2,256,1024]{2,1,0:T(8,128)(2,1)S(1)} convert(f32[2,256,1024]{2,1,0:T(8,128)} %get-tuple-element.34) | non-fusion elementwise | flops 524288 | bytes 3145728 | tf_op jit(solution)/shard_map/convert.6
  106.8 1.3 collective-permute-start.11
  108.1 0.2 convert.14
  108.3 0.1 slice_bitcast_fusion.2
  108.5 6.4 %collective-permute-start.13 = (bf16[2,128,1024]{2,1,0:T(8,128)(2,1)S(1)}, bf16[2,128,1024]{2,1,0:T(8,128)(2,1)S(1)}, u32[]{:S(2)}, u32[]{:S(2)}) collective-permute-start(bf16[2,128,1024]{2,1,0:T(8,128)(2,1)S(1)} %get-tuple-element.38), channel_id=1, source_target_pairs={{0,16},{1,17},{2,18},{3,19},{4,20},{5,21},{6,22},{7,23},{8,24},{9,... | collective-permute-start | bytes 1572872 | tf_op jit(solution)/shard_map/ppermute | solution.py:53
  114.8 0.0 collective-permute-start.15
  114.8 1.4 collective-permute-start.14
  116.2 1.5 %collective-permute-start.12 = (bf16[2,64,1024]{2,1,0:T(8,128)(2,1)S(1)}, bf16[2,64,1024]{2,1,0:T(8,128)(2,1)S(1)}, u32[]{:S(2)}, u32[]{:S(2)}) collective-permute-start(bf16[2,64,1024]{2,1,0:T(8,128)(2,1)S(1)} %get-tuple-element.41), channel_id=1, source_target_pairs={{0,1},{1,2},{2,3},{3,4},{4,5},{5,6},{6,7},{7,8},{8,9},{9,10},{10,1... | collective-permute-start | bytes 786440 | tf_op jit(solution)/shard_map/ppermute | solution.py:59
  117.7 0.1 slice.106
  117.8 0.0 collective-permute-done.11
  117.8 0.1 add_dynamic-update-slice_fusion
  117.9 0.9 collective-permute-done.12
  118.8 0.1 fusion
  118.9 22.1 %collective-permute-done.13 = bf16[2,128,1024]{2,1,0:T(8,128)(2,1)S(1)} collective-permute-done((bf16[2,128,1024]{2,1,0:T(8,128)(2,1)S(1)}, bf16[2,128,1024]{2,1,0:T(8,128)(2,1)S(1)}, u32[]{:S(2)}, u32[]{:S(2)}) %collective-permute-start.13) | collective-permute-done | bytes 524320 | tf_op jit(solution)/shard_map/ppermute | solution.py:53
  141.0 0.0 collective-permute-done.15
  141.0 0.0 collective-permute-done.14
  141.0 0.3 add_convert_fusion
  141.4 0.8 slice_bitcast_fusion.3
  (15 shorter events, 0.2 us)
Async XLA Ops:
  0.6 4.3 %copy-start.7 = (s32[2]{0:T(128)S(1)}, s32[2]{0:T(128)}, u32[]{:S(2)}) copy-start(s32[2]{0:T(128)} %param.15) | copy-start | bytes 28
  4.7 29.9 %copy-start.2 = (bf16[128,1024]{1,0:T(8,128)(2,1)S(1)}, bf16[128,1024]{1,0:T(8,128)(2,1)}, u32[]{:S(2)}) copy-start(bf16[128,1024]{1,0:T(8,128)(2,1)} %param.11) | copy-start | bytes 786436
  4.7 29.9 %copy-start.3 = (bf16[128,1024]{1,0:T(8,128)(2,1)S(1)}, bf16[128,1024]{1,0:T(8,128)(2,1)}, u32[]{:S(2)}) copy-start(bf16[128,1024]{1,0:T(8,128)(2,1)} %param.12) | copy-start | bytes 786436
  4.8 1.6 %collective-permute-start.2 = (bf16[2,64,1024]{2,1,0:T(8,128)(2,1)S(1)}, bf16[2,64,1024]{2,1,0:T(8,128)(2,1)S(1)}, u32[]{:S(2)}, u32[]{:S(2)}) collective-permute-start(bf16[2,64,1024]{2,1,0:T(8,128)(2,1)S(1)} %select_bitcast_fusion.2), channel_id=1, source_target_pairs={{0,1},{1,0},{2,3},{3,2},{4,5},{5,4},{6,7},{7,6},{8,9},{9,8},{10,11... | collective-permute-start | bytes 786440 | tf_op jit(solution)/shard_map/ppermute | solution.py:39
  6.5 8.4 %collective-permute-start.3 = (bf16[2,64,1024]{2,1,0:T(8,128)(2,1)S(1)}, bf16[2,64,1024]{2,1,0:T(8,128)(2,1)S(1)}, u32[]{:S(2)}, u32[]{:S(2)}) collective-permute-start(bf16[2,64,1024]{2,1,0:T(8,128)(2,1)S(1)} %fusion.2), channel_id=1, source_target_pairs={{0,2},{1,3},{2,0},{3,1},{4,6},{5,7},{6,4},{7,5},{8,10},{9,11},{10,... | collective-permute-start | bytes 786440 | tf_op jit(solution)/shard_map/ppermute | solution.py:43
  14.9 42.1 %copy-start.8 = (s32[2,3]{1,0:T(2,128)S(1)}, s32[2,3]{1,0:T(2,128)}, u32[]{:S(2)}) copy-start(s32[2,3]{1,0:T(2,128)} %param.14) | copy-start | bytes 76
  15.0 9.1 %collective-permute-start.4 = (bf16[2,64,1024]{2,1,0:T(8,128)(2,1)S(1)}, bf16[2,64,1024]{2,1,0:T(8,128)(2,1)S(1)}, u32[]{:S(2)}, u32[]{:S(2)}) collective-permute-start(bf16[2,64,1024]{2,1,0:T(8,128)(2,1)S(1)} %broadcast_select_fusion), channel_id=1, source_target_pairs={{0,4},{1,5},{2,6},{3,7},{4,0},{5,1},{6,2},{7,3},{8,12},{9,13},{10,... | collective-permute-start | bytes 786440 | tf_op jit(solution)/shard_map/ppermute | solution.py:43
  24.2 6.9 %collective-permute-start.5 = (bf16[2,64,1024]{2,1,0:T(8,128)(2,1)S(1)}, bf16[2,64,1024]{2,1,0:T(8,128)(2,1)S(1)}, u32[]{:S(2)}, u32[]{:S(2)}) collective-permute-start(bf16[2,64,1024]{2,1,0:T(8,128)(2,1)S(1)} %broadcast_select_fusion.1), channel_id=1, source_target_pairs={{0,8},{1,9},{2,10},{3,11},{4,12},{5,13},{6,14},{7,15},{8,0},{9,1},... | collective-permute-start | bytes 786440 | tf_op jit(solution)/shard_map/ppermute | solution.py:43
  31.2 25.6 %collective-permute-start.6 = (bf16[2,64,1024]{2,1,0:T(8,128)(2,1)S(1)}, bf16[2,64,1024]{2,1,0:T(8,128)(2,1)S(1)}, u32[]{:S(2)}, u32[]{:S(2)}) collective-permute-start(bf16[2,64,1024]{2,1,0:T(8,128)(2,1)S(1)} %broadcast_select_fusion.2), channel_id=1, source_target_pairs={{0,16},{1,17},{2,18},{3,19},{4,20},{5,21},{6,22},{7,23},{8,24},{9,... | collective-permute-start | bytes 786440 | tf_op jit(solution)/shard_map/ppermute | solution.py:43
  34.6 26.1 %collective-permute-start.10 = (bf16[2,128,1024]{2,1,0:T(8,128)(2,1)S(1)}, bf16[2,128,1024]{2,1,0:T(8,128)(2,1)S(1)}, u32[]{:S(2)}, u32[]{:S(2)}) collective-permute-start(bf16[2,128,1024]{2,1,0:T(8,128)(2,1)S(1)} %pad_maximum_fusion.1), channel_id=1, source_target_pairs={{0,4},{1,5},{2,6},{3,7},{4,0},{5,1},{6,2},{7,3},{8,12},{9,13},{10,... | collective-permute-start | bytes 1572872 | tf_op jit(solution)/shard_map/ppermute | solution.py:53
  37.9 29.1 %collective-permute-start.8 = (bf16[2,128,1024]{2,1,0:T(8,128)(2,1)S(1)}, bf16[2,128,1024]{2,1,0:T(8,128)(2,1)S(1)}, u32[]{:S(2)}, u32[]{:S(2)}) collective-permute-start(bf16[2,128,1024]{2,1,0:T(8,128)(2,1)S(1)} %pad_maximum_fusion.1), channel_id=1, source_target_pairs={{0,16},{1,17},{2,18},{3,19},{4,20},{5,21},{6,22},{7,23},{8,24},{9,... | collective-permute-start | bytes 1572872 | tf_op jit(solution)/shard_map/ppermute | solution.py:53
  38.0 19.2 %collective-permute-start = (bf16[2,64,1024]{2,1,0:T(8,128)(2,1)S(1)}, bf16[2,64,1024]{2,1,0:T(8,128)(2,1)}, u32[]{:S(2)}, u32[]{:S(2)}) collective-permute-start(bf16[2,64,1024]{2,1,0:T(8,128)(2,1)S(1)} %get-tuple-element.48), channel_id=1, source_target_pairs={{0,1},{1,2},{2,3},{3,4},{4,5},{5,6},{6,7},{7,8},{8,9},{9,10},{10,1... | collective-permute-start | bytes 786440 | tf_op jit(solution)/shard_map/ppermute | solution.py:25
  39.9 17.8 %collective-permute-start.1 = (bf16[2,64,1024]{2,1,0:T(8,128)(2,1)S(1)}, bf16[2,64,1024]{2,1,0:T(8,128)(2,1)}, u32[]{:S(2)}, u32[]{:S(2)}) collective-permute-start(bf16[2,64,1024]{2,1,0:T(8,128)(2,1)S(1)} %get-tuple-element.49), channel_id=1, source_target_pairs={{1,0},{2,1},{3,2},{4,3},{5,4},{6,5},{7,6},{8,7},{9,8},{10,9},{11,1... | collective-permute-start | bytes 786440 | tf_op jit(solution)/shard_map/ppermute | solution.py:26
  56.9 2.9 %collective-permute-start.7 = (bf16[2,64,1024]{2,1,0:T(8,128)(2,1)S(1)}, bf16[2,64,1024]{2,1,0:T(8,128)(2,1)S(1)}, u32[]{:S(2)}, u32[]{:S(2)}) collective-permute-start(bf16[2,64,1024]{2,1,0:T(8,128)(2,1)S(1)} %broadcast_select_fusion.3), channel_id=1, source_target_pairs={{0,1},{1,0},{2,3},{3,2},{4,5},{5,4},{6,7},{7,6},{8,9},{9,8},{10,11... | collective-permute-start | bytes 786440 | tf_op jit(solution)/shard_map/ppermute | solution.py:46
  57.2 21.3 %collective-permute-start.9 = (bf16[2,128,1024]{2,1,0:T(8,128)(2,1)S(1)}, bf16[2,128,1024]{2,1,0:T(8,128)(2,1)S(1)}, u32[]{:S(2)}, u32[]{:S(2)}) collective-permute-start(bf16[2,128,1024]{2,1,0:T(8,128)(2,1)S(1)} %pad_maximum_fusion.1), channel_id=1, source_target_pairs={{0,8},{1,9},{2,10},{3,11},{4,12},{5,13},{6,14},{7,15},{8,0},{9,1},... | collective-permute-start | bytes 1572872 | tf_op jit(solution)/shard_map/ppermute | solution.py:53
  60.8 17.7 %copy-start.4 = (bf16[2,128,1024]{2,1,0:T(8,128)(2,1)}, bf16[2,128,1024]{2,1,0:T(8,128)(2,1)S(1)}, u32[]{:S(2)}) copy-start(bf16[2,128,1024]{2,1,0:T(8,128)(2,1)S(1)} %collective-permute-done.10.rest_2_) | copy-start | bytes 1572868
  67.0 11.5 %copy-start.5 = (bf16[2,128,1024]{2,1,0:T(8,128)(2,1)}, bf16[2,128,1024]{2,1,0:T(8,128)(2,1)S(1)}, u32[]{:S(2)}) copy-start(bf16[2,128,1024]{2,1,0:T(8,128)(2,1)S(1)} %collective-permute-done.8.rest_0_) | copy-start | bytes 1572868
  78.5 0.8 copy-start.6
  104.8 3.3 %copy-start.1 = (f32[3,2,128,1024]{3,2,1,0:T(8,128)S(1)}, f32[3,2,128,1024]{3,2,1,0:T(8,128)}, u32[]{:S(2)}) copy-start(f32[3,2,128,1024]{3,2,1,0:T(8,128)} %get-tuple-element.35) | copy-start | bytes 9437188
  106.8 11.1 %collective-permute-start.11 = (bf16[2,64,1024]{2,1,0:T(8,128)(2,1)S(1)}, bf16[2,64,1024]{2,1,0:T(8,128)(2,1)S(1)}, u32[]{:S(2)}, u32[]{:S(2)}) collective-permute-start(bf16[2,64,1024]{2,1,0:T(8,128)(2,1)S(1)} %get-tuple-element.42), channel_id=1, source_target_pairs={{1,0},{2,1},{3,2},{4,3},{5,4},{6,5},{7,6},{8,7},{9,8},{10,9},{11,1... | collective-permute-start | bytes 786440 | tf_op jit(solution)/shard_map/ppermute | solution.py:59
  108.3 9.4 %copy-start = (f32[2,256,1024]{2,1,0:T(8,128)S(1)}, f32[2,256,1024]{2,1,0:T(8,128)}, u32[]{:S(2)}) copy-start(f32[2,256,1024]{2,1,0:T(8,128)} %get-tuple-element.34) | copy-start | bytes 6291460
  108.5 32.6 %collective-permute-start.13 = (bf16[2,128,1024]{2,1,0:T(8,128)(2,1)S(1)}, bf16[2,128,1024]{2,1,0:T(8,128)(2,1)S(1)}, u32[]{:S(2)}, u32[]{:S(2)}) collective-permute-start(bf16[2,128,1024]{2,1,0:T(8,128)(2,1)S(1)} %get-tuple-element.38), channel_id=1, source_target_pairs={{0,16},{1,17},{2,18},{3,19},{4,20},{5,21},{6,22},{7,23},{8,24},{9,... | collective-permute-start | bytes 1572872 | tf_op jit(solution)/shard_map/ppermute | solution.py:53
  114.8 26.2 %collective-permute-start.15 = (bf16[2,128,1024]{2,1,0:T(8,128)(2,1)S(1)}, bf16[2,128,1024]{2,1,0:T(8,128)(2,1)S(1)}, u32[]{:S(2)}, u32[]{:S(2)}) collective-permute-start(bf16[2,128,1024]{2,1,0:T(8,128)(2,1)S(1)} %get-tuple-element.39), channel_id=1, source_target_pairs={{0,4},{1,5},{2,6},{3,7},{4,0},{5,1},{6,2},{7,3},{8,12},{9,13},{10,... | collective-permute-start | bytes 1572872 | tf_op jit(solution)/shard_map/ppermute | solution.py:53
  114.8 26.2 %collective-permute-start.14 = (bf16[2,128,1024]{2,1,0:T(8,128)(2,1)S(1)}, bf16[2,128,1024]{2,1,0:T(8,128)(2,1)S(1)}, u32[]{:S(2)}, u32[]{:S(2)}) collective-permute-start(bf16[2,128,1024]{2,1,0:T(8,128)(2,1)S(1)} %get-tuple-element.40), channel_id=1, source_target_pairs={{0,8},{1,9},{2,10},{3,11},{4,12},{5,13},{6,14},{7,15},{8,0},{9,1},... | collective-permute-start | bytes 1572872 | tf_op jit(solution)/shard_map/ppermute | solution.py:53
  116.2 2.6 %collective-permute-start.12 = (bf16[2,64,1024]{2,1,0:T(8,128)(2,1)S(1)}, bf16[2,64,1024]{2,1,0:T(8,128)(2,1)S(1)}, u32[]{:S(2)}, u32[]{:S(2)}) collective-permute-start(bf16[2,64,1024]{2,1,0:T(8,128)(2,1)S(1)} %get-tuple-element.41), channel_id=1, source_target_pairs={{0,1},{1,2},{2,3},{3,4},{4,5},{5,6},{6,7},{7,8},{8,9},{9,10},{10,1... | collective-permute-start | bytes 786440 | tf_op jit(solution)/shard_map/ppermute | solution.py:59

commit v5 on v4

--- a/solution.py
+++ b/solution.py
@@ -28,21 +28,28 @@
     return array
 
 
-def from_root(blocks, axis, sources):
+def from_root(blocks, axis, sources, mask):
     size = lax.axis_size(axis)
     position = lax.axis_index(axis)
     shape = (-1,) + (1,) * (blocks.ndim - 2)
     core = position % 2
     sibling = [(i, i ^ 1) for i in range(size)]
+
+    def holds(partner):
+        return (((sources ^ partner) & ~mask) == 0).reshape(shape)
+
     mine = jnp.where(core == 0, blocks[:, 0], blocks[:, 1])
     theirs = jnp.where(core == 0, blocks[:, 1], blocks[:, 0])
     received = lax.ppermute(theirs, axis, sibling)
-    carried = jnp.where((sources == (position ^ 1)).reshape(shape), received, mine)
+    carried = jnp.where(holds(position ^ 1), received, mine)
+    mask = mask | 1
     for level in range(1, size.bit_length() - 1):
         step = 1 << level
+        if mask & step:
+            continue
         received = lax.ppermute(carried, axis, [(i, i ^ step) for i in range(size)])
-        partner_holds = ((position ^ step) >> level) == (sources >> level)
-        carried = jnp.where(partner_holds.reshape(shape), received, carried)
+        carried = jnp.where(holds(position ^ step), received, carried)
+        mask = mask | step
     other = lax.ppermute(carried, axis, sibling)
     first = jnp.where(core == 0, carried, other)
     second = jnp.where(core == 0, other, carried)
@@ -71,7 +78,8 @@
     gwin_ref[...] = jnp.zeros_like(gwin_ref)
     gpart_ref[...] = jnp.zeros_like(gpart_ref)
     lane = lax.broadcasted_iota(jnp.int32, (BLOCK, LANES), 1)
-    col = lax.broadcasted_iota(jnp.int32, (BLOCK, listed * BLOCK), 1)
+    per_pair = LANES // HEAD_DIM
+    col = lax.broadcasted_iota(jnp.int32, (per_pair * BLOCK, listed * BLOCK), 1)
     nt = (((1,), (1,)), ((), ()))
     tn = (((0,), (0,)), ((), ()))
     base = (3 + GLOBALS) * BLOCK
@@ -94,32 +102,28 @@
         invalid = ((col < BLOCK) & (left_ok == 0)) | (
             (col >= 2 * BLOCK) & (col < 3 * BLOCK) & (right_ok == 0)
         )
-        att = jnp.zeros((BLOCK, LANES), jnp.float32)
-        gq = jnp.zeros((BLOCK, LANES), jnp.float32)
-        gk = jnp.zeros((listed * BLOCK, LANES), jnp.float32)
-        gv = jnp.zeros((listed * BLOCK, LANES), jnp.float32)
-        for h in range(LANES // HEAD_DIM):
-            in_head = (lane >= h * HEAD_DIM) & (lane < (h + 1) * HEAD_DIM)
-            qh = jnp.where(in_head, q, jnp.zeros_like(q))
-            gh = jnp.where(in_head, g, jnp.zeros_like(g))
-            scores = lax.dot_general(qh, k, nt, preferred_element_type=jnp.float32) * scale_factor
-            scores = jnp.where(invalid, SCORE_FLOOR, scores)
-            highest = jnp.max(scores, axis=-1, keepdims=True)
-            raw_weights = jnp.exp(scores - highest)
-            weight_total = jnp.sum(raw_weights, axis=-1, keepdims=True)
-            probs = raw_weights / weight_total
-            probs_low = probs.astype(jnp.bfloat16)
-            att = jnp.where(
-                in_head, jnp.dot(probs_low, v, preferred_element_type=jnp.float32), att
-            )
-            grad_probs = lax.dot_general(gh, v, nt, preferred_element_type=jnp.float32)
-            inner = jnp.sum(probs * grad_probs, axis=-1, keepdims=True)
-            grad_scores = (scale_factor * probs * (grad_probs - inner)).astype(jnp.bfloat16)
-            gq = jnp.where(
-                in_head, jnp.dot(grad_scores, k, preferred_element_type=jnp.float32), gq
-            )
-            gk = gk + lax.dot_general(grad_scores, qh, tn, preferred_element_type=jnp.float32)
-            gv = gv + lax.dot_general(probs_low, gh, tn, preferred_element_type=jnp.float32)
+        heads = [(lane >= h * HEAD_DIM) & (lane < (h + 1) * HEAD_DIM) for h in range(per_pair)]
+        qm = jnp.concatenate([jnp.where(m, q, jnp.zeros_like(q)) for m in heads], axis=0)
+        gm = jnp.concatenate([jnp.where(m, g, jnp.zeros_like(g)) for m in heads], axis=0)
+        scores = lax.dot_general(qm, k, nt, preferred_element_type=jnp.float32) * scale_factor
+        scores = jnp.where(invalid, SCORE_FLOOR, scores)
+        highest = jnp.max(scores, axis=-1, keepdims=True)
+        raw_weights = jnp.exp(scores - highest)
+        weight_total = jnp.sum(raw_weights, axis=-1, keepdims=True)
+        probs = raw_weights / weight_total
+        probs_low = probs.astype(jnp.bfloat16)
+        grad_probs = lax.dot_general(gm, v, nt, preferred_element_type=jnp.float32)
+        inner = jnp.sum(probs * grad_probs, axis=-1, keepdims=True)
+        grad_scores = (scale_factor * probs * (grad_probs - inner)).astype(jnp.bfloat16)
+        att_all = jnp.dot(probs_low, v, preferred_element_type=jnp.float32)
+        gq_all = jnp.dot(grad_scores, k, preferred_element_type=jnp.float32)
+        att = att_all[:BLOCK]
+        gq = gq_all[:BLOCK]
+        for h in range(1, per_pair):
+            att = jnp.where(heads[h], att_all[h * BLOCK : (h + 1) * BLOCK], att)
+            gq = jnp.where(heads[h], gq_all[h * BLOCK : (h + 1) * BLOCK], gq)
+        gk = lax.dot_general(grad_scores, qm, tn, preferred_element_type=jnp.float32)
+        gv = lax.dot_general(probs_low, gm, tn, preferred_element_type=jnp.float32)
         att_ref[rows, :] = att.astype(att_ref.dtype)
         gq_ref[rows, :] = gq.astype(gq_ref.dtype)
         window = pl.ds(j * BLOCK, 3 * BLOCK)
@@ -175,17 +179,18 @@
     padded = padded_2(stacked, (("ctx", 1),), BLOCK)
     owners = global_ids // block_count
     local_ids = global_ids % block_count
-    own_pieces = jnp.stack(
-        [
-            lax.dynamic_slice_in_dim(stacked, local_ids[global_slot] * BLOCK, BLOCK, 1)
-            for global_slot in range(GLOBALS)
-        ],
-        axis=1,
-    )
-    fetched = jnp.swapaxes(from_root(jnp.swapaxes(own_pieces, 0, 1), "ctx", owners), 0, 1)
-    glob = fetched.reshape(2, GLOBALS * BLOCK, width)
     spread = [top_bit - 1 - matching for matching in range(RAND)]
     partners = [partner_2(stacked, "ctx", bit) for bit in spread]
+    first_step = 1 << spread[0]
+    candidates = []
+    for global_slot in range(GLOBALS):
+        start = local_ids[global_slot] * BLOCK
+        own_piece = lax.dynamic_slice_in_dim(stacked, start, BLOCK, 1)
+        far_piece = lax.dynamic_slice_in_dim(partners[0], start, BLOCK, 1)
+        from_far = owners[global_slot] == (position ^ first_step)
+        candidates.append(jnp.where(from_far, far_piece, own_piece))
+    fetched = from_root(jnp.stack(candidates), "ctx", owners, first_step)
+    glob = jnp.swapaxes(fetched, 0, 1).reshape(2, GLOBALS * BLOCK, width)
     global_block = position * block_count + block_iota
     seq_blocks = block_count * ctx_count
     meta = jnp.concatenate(

time: 142 us -> 124 us (0.87)
  the two profiles are of different devices: /device:TPU:6 before, /device:TPU:192 now
where the time goes in v5:
time: 124 us; the launch traced here: 122 us
  waiting for transfers between devices  57.5 us (46%)
  starting transfers between devices  33.9 us (27%)
  Pallas kernels  13.2 us (11%)
  other arithmetic  10.8 us (9%)
  between operations  3.55 us (3%)
  local copies, waits for them, and re-layouts  3.42 us (3%)
    ppermute x2, waiting for transfers between devices, passed_along(): return lax.ppermute(array, axis, pairs)  20.6 us
    ppermute x6, waiting for transfers between devices, partner_2(): lax.ppermute(array, axis, [(i, i ^ 1 << distance) for i in range(lax.axis...  19.3 us
    pallas_call x1, Pallas kernels, attend(): pl.pallas_call(attend_kernel, grid_spec=pltpu.PrefetchScalarGridSpec(num_...  13.2 us
    ppermute x3, waiting for transfers between devices, from_root(): received = lax.ppermute(carried, axis, [(i, i ^ step) for i in range(size)])  12.6 us
    ppermute x6, starting transfers between devices, partner_2(): lax.ppermute(array, axis, [(i, i ^ 1 << distance) for i in range(lax.axis...  10.4 us
    ppermute x3, starting transfers between devices, from_root(): received = lax.ppermute(carried, axis, [(i, i ^ step) for i in range(size)])  7.98 us
    ppermute x2, starting transfers between devices, passed_along(): return lax.ppermute(array, axis, pairs)  7.62 us
    ppermute x1, starting transfers between devices, padded_2(): after = lax.ppermute(first, axis, down)  5.75 us
  transfers between devices with their start and end apart: 15, of which 7 were waited for; matrix products, arithmetic and copies ran while one was open for 6% of the time, Pallas kernels for 0%

profile of v5, /device:TPU:192, one launch (start us, length us, event | category | flops | bytes accessed | tf_op | source)
XLA Modules:
  0.0 122.3 jit_solution(5767832698573160303)
XLA Ops:
  0.6 1.1 pad_maximum_fusion.1
  1.7 1.5 %collective-permute-start.2 = (bf16[2,128,1024]{2,1,0:T(8,128)(2,1)S(1)}, bf16[2,128,1024]{2,1,0:T(8,128)(2,1)S(1)}, u32[]{:S(2)}, u32[]{:S(2)}) collective-permute-start(bf16[2,128,1024]{2,1,0:T(8,128)(2,1)S(1)} %pad_maximum_fusion.1), channel_id=1, source_target_pairs={{0,16},{1,17},{2,18},{3,19},{4,20},{5,21},{6,22},{7,23},{8,24},{9,... | collective-permute-start | bytes 1572872 | tf_op jit(solution)/shard_map/ppermute | solution.py:60
  3.3 0.7 and_select_fusion
  3.9 0.6 fusion.15
  5.8 0.7 and_compare_fusion.3
  6.5 0.6 fusion.14
  8.4 17.3 %collective-permute-done.2.rest_0_ = bf16[2,128,1024]{2,1,0:T(8,128)(2,1)S(1)} collective-permute-done((bf16[2,128,1024]{2,1,0:T(8,128)(2,1)S(1)}, bf16[2,128,1024]{2,1,0:T(8,128)(2,1)S(1)}, u32[]{:S(2)}, u32[]{:S(2)}) %collective-permute-start.2) | collective-permute-done | bytes 524320 | tf_op jit(solution)/shard_map/ppermute | solution.py:60
  25.7 1.7 %fusion.8 = (bf16[1,2,64,1024]{3,2,1,0:T(8,128)(2,1)S(1)}, bf16[1,2,64,1024]{3,2,1,0:T(8,128)(2,1)S(1)}, bf16[2,64,1024]{2,1,0:T(8,128)(2,1)S(1)}, bf16[2,64,1024]{2,1,0:T(8,128)(2,1)S(1)}) fusion(s32[]{:T(128)S(6)} %select_n.85, bf16[1,128,1024]{2,1,0:T(8,128)(2,1)} %bitcast.48, bf16[1,128,1024]{2,1,0:T(8,128)(2,1)} %bitcast.51, ...), kind=kLoop, calls=%fused_computation.28 | loop fusion | flops 2359296 | bytes 2097162 | tf_op jit(solution)/shard_map/stack | solution.py:192
  27.4 0.0 copy-start.7
  27.4 0.0 copy-start.2
  27.4 0.0 copy-start.3
  27.5 0.1 collective-permute-start.3
  27.6 1.5 %collective-permute-done.3 = bf16[2,64,1024]{2,1,0:T(8,128)(2,1)S(1)} collective-permute-done((bf16[2,64,1024]{2,1,0:T(8,128)(2,1)S(1)}, bf16[2,64,1024]{2,1,0:T(8,128)(2,1)S(1)}, u32[]{:S(2)}, u32[]{:S(2)}) %collective-permute-start.3) | collective-permute-done | bytes 262176 | tf_op jit(solution)/shard_map/ppermute | solution.py:43
  29.1 0.1 fusion.2
  29.2 1.7 %collective-permute-start.4 = (bf16[2,64,1024]{2,1,0:T(8,128)(2,1)S(1)}, bf16[2,64,1024]{2,1,0:T(8,128)(2,1)S(1)}, u32[]{:S(2)}, u32[]{:S(2)}) collective-permute-start(bf16[2,64,1024]{2,1,0:T(8,128)(2,1)S(1)} %fusion.2), channel_id=1, source_target_pairs={{0,2},{1,3},{2,0},{3,1},{4,6},{5,7},{6,4},{7,5},{8,10},{9,11},{10,... | collective-permute-start | bytes 786440 | tf_op jit(solution)/shard_map/ppermute | solution.py:50
  30.9 6.8 %collective-permute-done.4 = bf16[2,64,1024]{2,1,0:T(8,128)(2,1)S(1)} collective-permute-done((bf16[2,64,1024]{2,1,0:T(8,128)(2,1)S(1)}, bf16[2,64,1024]{2,1,0:T(8,128)(2,1)S(1)}, u32[]{:S(2)}, u32[]{:S(2)}) %collective-permute-start.4) | collective-permute-done | bytes 262176 | tf_op jit(solution)/shard_map/ppermute | solution.py:50
  37.6 0.1 broadcast_select_fusion
  37.7 0.0 copy-done.4
  37.8 3.3 %collective-permute-start.5 = (bf16[2,64,1024]{2,1,0:T(8,128)(2,1)S(1)}, bf16[2,64,1024]{2,1,0:T(8,128)(2,1)S(1)}, u32[]{:S(2)}, u32[]{:S(2)}) collective-permute-start(bf16[2,64,1024]{2,1,0:T(8,128)(2,1)S(1)} %broadcast_select_fusion), channel_id=1, source_target_pairs={{0,4},{1,5},{2,6},{3,7},{4,0},{5,1},{6,2},{7,3},{8,12},{9,13},{10,... | collective-permute-start | bytes 786440 | tf_op jit(solution)/shard_map/ppermute | solution.py:50
  41.0 5.8 %collective-permute-done.5 = bf16[2,64,1024]{2,1,0:T(8,128)(2,1)S(1)} collective-permute-done((bf16[2,64,1024]{2,1,0:T(8,128)(2,1)S(1)}, bf16[2,64,1024]{2,1,0:T(8,128)(2,1)S(1)}, u32[]{:S(2)}, u32[]{:S(2)}) %collective-permute-start.5) | collective-permute-done | bytes 262176 | tf_op jit(solution)/shard_map/ppermute | solution.py:50
  46.8 0.1 broadcast_select_fusion.1
  46.9 3.0 %collective-permute-start.6 = (bf16[2,64,1024]{2,1,0:T(8,128)(2,1)S(1)}, bf16[2,64,1024]{2,1,0:T(8,128)(2,1)S(1)}, u32[]{:S(2)}, u32[]{:S(2)}) collective-permute-start(bf16[2,64,1024]{2,1,0:T(8,128)(2,1)S(1)} %broadcast_select_fusion.1), channel_id=1, source_target_pairs={{0,8},{1,9},{2,10},{3,11},{4,12},{5,13},{6,14},{7,15},{8,0},{9,1},... | collective-permute-start | bytes 786440 | tf_op jit(solution)/shard_map/ppermute | solution.py:50
  50.0 3.2 %collective-permute-start.9 = (bf16[2,128,1024]{2,1,0:T(8,128)(2,1)S(1)}, bf16[2,128,1024]{2,1,0:T(8,128)(2,1)S(1)}, u32[]{:S(2)}, u32[]{:S(2)}) collective-permute-start(bf16[2,128,1024]{2,1,0:T(8,128)(2,1)S(1)} %pad_maximum_fusion.1), channel_id=1, source_target_pairs={{0,4},{1,5},{2,6},{3,7},{4,0},{5,1},{6,2},{7,3},{8,12},{9,13},{10,... | collective-permute-start | bytes 1572872 | tf_op jit(solution)/shard_map/ppermute | solution.py:60
  53.2 0.1 collective-permute-start.8
  53.3 1.9 %collective-permute-start = (bf16[2,64,1024]{2,1,0:T(8,128)(2,1)S(1)}, bf16[2,64,1024]{2,1,0:T(8,128)(2,1)}, u32[]{:S(2)}, u32[]{:S(2)}) collective-permute-start(bf16[2,64,1024]{2,1,0:T(8,128)(2,1)S(1)} %get-tuple-element.49), channel_id=1, source_target_pairs={{0,1},{1,2},{2,3},{3,4},{4,5},{5,6},{6,7},{7,8},{8,9},{9,10},{10,1... | collective-permute-start | bytes 786440 | tf_op jit(solution)/shard_map/ppermute | solution.py:25
  55.2 5.8 %collective-permute-start.1 = (bf16[2,64,1024]{2,1,0:T(8,128)(2,1)S(1)}, bf16[2,64,1024]{2,1,0:T(8,128)(2,1)}, u32[]{:S(2)}, u32[]{:S(2)}) collective-permute-start(bf16[2,64,1024]{2,1,0:T(8,128)(2,1)S(1)} %get-tuple-element.50), channel_id=1, source_target_pairs={{1,0},{2,1},{3,2},{4,3},{5,4},{6,5},{7,6},{8,7},{9,8},{10,9},{11,1... | collective-permute-start | bytes 786440 | tf_op jit(solution)/shard_map/ppermute | solution.py:26
  60.9 0.0 collective-permute-done.6
  60.9 0.1 broadcast_select_fusion.2
  61.0 0.1 collective-permute-start.7
  61.2 0.0 copy-done.7
  61.2 0.1 reshape.95
  61.3 0.6 pad_add_fusion.meta_ref
  61.8 3.6 %collective-permute-done = bf16[2,64,1024]{2,1,0:T(8,128)(2,1)} collective-permute-done((bf16[2,64,1024]{2,1,0:T(8,128)(2,1)S(1)}, bf16[2,64,1024]{2,1,0:T(8,128)(2,1)}, u32[]{:S(2)}, u32[]{:S(2)}) %collective-permute-start) | collective-permute-done | bytes 262176 | tf_op jit(solution)/shard_map/ppermute | solution.py:25
  65.4 0.0 collective-permute-done.1
  65.4 0.0 copy-done.2
  65.4 0.0 copy-done.3
  65.4 2.1 %pad_maximum_fusion.win_ref = bf16[2,256,1024]{2,1,0:T(8,128)(2,1)} fusion(bf16[2,64,1024]{2,1,0:T(8,128)(2,1)} %collective-permute-done.1, bf16[1,128,1024]{2,1,0:T(8,128)(2,1)S(1)} %bitcast.52, bf16[1,128,1024]{2,1,0:T(8,128)(2,1)S(1)} %bitcast.49, bf16[2,64,1024]{2,1,0:T(8,128)(2,1)} %collective-permute-done), kind=kLoop, calls=%fused_computation | loop fusion | flops 4194304 | bytes 2097152 | tf_op jit(solution)/shard_map/concatenate | solution.py:27
  67.5 0.0 collective-permute-done.7
  67.6 0.8 pad_maximum_fusion.2
  68.4 0.0 collective-permute-done.9.rest_2_
  68.4 0.0 collective-permute-done.8.rest_1_
  68.4 0.0 copy-start.6
  68.4 0.8 copy-done.5
  69.3 0.2 copy-done.6
  69.5 13.2 %shard_map.93 = (bf16[128,1024]{1,0:T(8,128)(2,1)}, bf16[128,1024]{1,0:T(8,128)(2,1)}, f32[2,256,1024]{2,1,0:T(8,128)}, f32[3,2,128,1024]{3,2,1,0:T(8,128)}) custom-call(s32[10]{0:T(128)} %pad_add_fusion.meta_ref, bf16[128,1024]{1,0:T(8,128)(2,1)} %q_ref.1, bf16[128,1024]{1,0:T(8,128)(2,1)} %g_ref.1, bf16[2,256,1024]{2,1,0:T(8,128)(2,1)} %pad_maximum_fusion.win_ref, ...), custom_call_target="tpu_custom_call" | custom-call | tf_op jit(solution)/shard_map/pallas_call | solution.py:158
  82.7 1.9 %convert.13 = bf16[2,256,1024]{2,1,0:T(8,128)(2,1)S(1)} convert(f32[2,256,1024]{2,1,0:T(8,128)} %get-tuple-element.34) | non-fusion elementwise | flops 524288 | bytes 3145728 | tf_op jit(solution)/shard_map/convert.6
  84.6 5.7 %collective-permute-start.10 = (bf16[2,64,1024]{2,1,0:T(8,128)(2,1)S(1)}, bf16[2,64,1024]{2,1,0:T(8,128)(2,1)S(1)}, u32[]{:S(2)}, u32[]{:S(2)}) collective-permute-start(bf16[2,64,1024]{2,1,0:T(8,128)(2,1)S(1)} %get-tuple-element.42), channel_id=1, source_target_pairs={{1,0},{2,1},{3,2},{4,3},{5,4},{6,5},{7,6},{8,7},{9,8},{10,9},{11,1... | collective-permute-start | bytes 786440 | tf_op jit(solution)/shard_map/ppermute | solution.py:66
  90.3 0.0 copy-done.1
  90.3 0.2 convert.14
  90.6 0.1 slice_bitcast_fusion.2
  90.7 0.1 collective-permute-start.12
  90.8 1.3 %collective-permute-start.14 = (bf16[2,128,1024]{2,1,0:T(8,128)(2,1)S(1)}, bf16[2,128,1024]{2,1,0:T(8,128)(2,1)S(1)}, u32[]{:S(2)}, u32[]{:S(2)}) collective-permute-start(bf16[2,128,1024]{2,1,0:T(8,128)(2,1)S(1)} %get-tuple-element.39), channel_id=1, source_target_pairs={{0,4},{1,5},{2,6},{3,7},{4,0},{5,1},{6,2},{7,3},{8,12},{9,13},{10,... | collective-permute-start | bytes 1572872 | tf_op jit(solution)/shard_map/ppermute | solution.py:60
  92.1 4.2 %collective-permute-start.13 = (bf16[2,128,1024]{2,1,0:T(8,128)(2,1)S(1)}, bf16[2,128,1024]{2,1,0:T(8,128)(2,1)S(1)}, u32[]{:S(2)}, u32[]{:S(2)}) collective-permute-start(bf16[2,128,1024]{2,1,0:T(8,128)(2,1)S(1)} %get-tuple-element.40), channel_id=1, source_target_pairs={{0,8},{1,9},{2,10},{3,11},{4,12},{5,13},{6,14},{7,15},{8,0},{9,1},... | collective-permute-start | bytes 1572872 | tf_op jit(solution)/shard_map/ppermute | solution.py:60
  96.3 1.9 %collective-permute-start.11 = (bf16[2,64,1024]{2,1,0:T(8,128)(2,1)S(1)}, bf16[2,64,1024]{2,1,0:T(8,128)(2,1)S(1)}, u32[]{:S(2)}, u32[]{:S(2)}) collective-permute-start(bf16[2,64,1024]{2,1,0:T(8,128)(2,1)S(1)} %get-tuple-element.41), channel_id=1, source_target_pairs={{0,1},{1,2},{2,3},{3,4},{4,5},{5,6},{6,7},{7,8},{8,9},{9,10},{10,1... | collective-permute-start | bytes 786440 | tf_op jit(solution)/shard_map/ppermute | solution.py:66
  98.3 0.1 slice.114
  98.4 0.0 collective-permute-done.10
  98.4 0.1 add_dynamic-update-slice_fusion
  98.5 20.6 %collective-permute-done.11 = bf16[2,64,1024]{2,1,0:T(8,128)(2,1)S(1)} collective-permute-done((bf16[2,64,1024]{2,1,0:T(8,128)(2,1)S(1)}, bf16[2,64,1024]{2,1,0:T(8,128)(2,1)S(1)}, u32[]{:S(2)}, u32[]{:S(2)}) %collective-permute-start.11) | collective-permute-done | bytes 262176 | tf_op jit(solution)/shard_map/ppermute | solution.py:66
  119.1 0.1 fusion
  119.2 0.0 collective-permute-done.12
  119.2 0.0 collective-permute-done.14
  119.2 2.0 %collective-permute-done.13 = bf16[2,128,1024]{2,1,0:T(8,128)(2,1)S(1)} collective-permute-done((bf16[2,128,1024]{2,1,0:T(8,128)(2,1)S(1)}, bf16[2,128,1024]{2,1,0:T(8,128)(2,1)S(1)}, u32[]{:S(2)}, u32[]{:S(2)}) %collective-permute-start.13) | collective-permute-done | bytes 524320 | tf_op jit(solution)/shard_map/ppermute | solution.py:60
  121.2 0.3 add_convert_fusion
  121.5 0.8 slice_bitcast_fusion.3
  (10 shorter events, 0.1 us)
Async XLA Ops:
  1.7 24.0 %collective-permute-start.2 = (bf16[2,128,1024]{2,1,0:T(8,128)(2,1)S(1)}, bf16[2,128,1024]{2,1,0:T(8,128)(2,1)S(1)}, u32[]{:S(2)}, u32[]{:S(2)}) collective-permute-start(bf16[2,128,1024]{2,1,0:T(8,128)(2,1)S(1)} %pad_maximum_fusion.1), channel_id=1, source_target_pairs={{0,16},{1,17},{2,18},{3,19},{4,20},{5,21},{6,22},{7,23},{8,24},{9,... | collective-permute-start | bytes 1572872 | tf_op jit(solution)/shard_map/ppermute | solution.py:60
  25.7 12.1 %copy-start.4 = (bf16[2,128,1024]{2,1,0:T(8,128)(2,1)}, bf16[2,128,1024]{2,1,0:T(8,128)(2,1)S(1)}, u32[]{:S(2)}) copy-start(bf16[2,128,1024]{2,1,0:T(8,128)(2,1)S(1)} %collective-permute-done.2.rest_0_) | copy-start | bytes 1572868
  27.4 33.8 %copy-start.7 = (s32[2,3]{1,0:T(2,128)S(1)}, s32[2,3]{1,0:T(2,128)}, u32[]{:S(2)}) copy-start(s32[2,3]{1,0:T(2,128)} %param.14) | copy-start | bytes 76
  27.4 38.0 %copy-start.2 = (bf16[128,1024]{1,0:T(8,128)(2,1)S(1)}, bf16[128,1024]{1,0:T(8,128)(2,1)}, u32[]{:S(2)}) copy-start(bf16[128,1024]{1,0:T(8,128)(2,1)} %param.11) | copy-start | bytes 786436
  27.4 38.0 %copy-start.3 = (bf16[128,1024]{1,0:T(8,128)(2,1)S(1)}, bf16[128,1024]{1,0:T(8,128)(2,1)}, u32[]{:S(2)}) copy-start(bf16[128,1024]{1,0:T(8,128)(2,1)} %param.12) | copy-start | bytes 786436
  27.5 1.6 %collective-permute-start.3 = (bf16[2,64,1024]{2,1,0:T(8,128)(2,1)S(1)}, bf16[2,64,1024]{2,1,0:T(8,128)(2,1)S(1)}, u32[]{:S(2)}, u32[]{:S(2)}) collective-permute-start(bf16[2,64,1024]{2,1,0:T(8,128)(2,1)S(1)} %fusion.12), channel_id=1, source_target_pairs={{0,1},{1,0},{2,3},{3,2},{4,5},{5,4},{6,7},{7,6},{8,9},{9,8},{10,11... | collective-permute-start | bytes 786440 | tf_op jit(solution)/shard_map/ppermute | solution.py:43
  29.2 8.4 %collective-permute-start.4 = (bf16[2,64,1024]{2,1,0:T(8,128)(2,1)S(1)}, bf16[2,64,1024]{2,1,0:T(8,128)(2,1)S(1)}, u32[]{:S(2)}, u32[]{:S(2)}) collective-permute-start(bf16[2,64,1024]{2,1,0:T(8,128)(2,1)S(1)} %fusion.2), channel_id=1, source_target_pairs={{0,2},{1,3},{2,0},{3,1},{4,6},{5,7},{6,4},{7,5},{8,10},{9,11},{10,... | collective-permute-start | bytes 786440 | tf_op jit(solution)/shard_map/ppermute | solution.py:50
  37.8 9.1 %collective-permute-start.5 = (bf16[2,64,1024]{2,1,0:T(8,128)(2,1)S(1)}, bf16[2,64,1024]{2,1,0:T(8,128)(2,1)S(1)}, u32[]{:S(2)}, u32[]{:S(2)}) collective-permute-start(bf16[2,64,1024]{2,1,0:T(8,128)(2,1)S(1)} %broadcast_select_fusion), channel_id=1, source_target_pairs={{0,4},{1,5},{2,6},{3,7},{4,0},{5,1},{6,2},{7,3},{8,12},{9,13},{10,... | collective-permute-start | bytes 786440 | tf_op jit(solution)/shard_map/ppermute | solution.py:50
  46.9 14.0 %collective-permute-start.6 = (bf16[2,64,1024]{2,1,0:T(8,128)(2,1)S(1)}, bf16[2,64,1024]{2,1,0:T(8,128)(2,1)S(1)}, u32[]{:S(2)}, u32[]{:S(2)}) collective-permute-start(bf16[2,64,1024]{2,1,0:T(8,128)(2,1)S(1)} %broadcast_select_fusion.1), channel_id=1, source_target_pairs={{0,8},{1,9},{2,10},{3,11},{4,12},{5,13},{6,14},{7,15},{8,0},{9,1},... | collective-permute-start | bytes 786440 | tf_op jit(solution)/shard_map/ppermute | solution.py:50
  50.0 18.5 %collective-permute-start.9 = (bf16[2,128,1024]{2,1,0:T(8,128)(2,1)S(1)}, bf16[2,128,1024]{2,1,0:T(8,128)(2,1)S(1)}, u32[]{:S(2)}, u32[]{:S(2)}) collective-permute-start(bf16[2,128,1024]{2,1,0:T(8,128)(2,1)S(1)} %pad_maximum_fusion.1), channel_id=1, source_target_pairs={{0,4},{1,5},{2,6},{3,7},{4,0},{5,1},{6,2},{7,3},{8,12},{9,13},{10,... | collective-permute-start | bytes 1572872 | tf_op jit(solution)/shard_map/ppermute | solution.py:60
  53.2 15.3 %collective-permute-start.8 = (bf16[2,128,1024]{2,1,0:T(8,128)(2,1)S(1)}, bf16[2,128,1024]{2,1,0:T(8,128)(2,1)S(1)}, u32[]{:S(2)}, u32[]{:S(2)}) collective-permute-start(bf16[2,128,1024]{2,1,0:T(8,128)(2,1)S(1)} %pad_maximum_fusion.1), channel_id=1, source_target_pairs={{0,8},{1,9},{2,10},{3,11},{4,12},{5,13},{6,14},{7,15},{8,0},{9,1},... | collective-permute-start | bytes 1572872 | tf_op jit(solution)/shard_map/ppermute | solution.py:60
  53.3 12.2 %collective-permute-start = (bf16[2,64,1024]{2,1,0:T(8,128)(2,1)S(1)}, bf16[2,64,1024]{2,1,0:T(8,128)(2,1)}, u32[]{:S(2)}, u32[]{:S(2)}) collective-permute-start(bf16[2,64,1024]{2,1,0:T(8,128)(2,1)S(1)} %get-tuple-element.49), channel_id=1, source_target_pairs={{0,1},{1,2},{2,3},{3,4},{4,5},{5,6},{6,7},{7,8},{8,9},{9,10},{10,1... | collective-permute-start | bytes 786440 | tf_op jit(solution)/shard_map/ppermute | solution.py:25
  55.2 10.3 %collective-permute-start.1 = (bf16[2,64,1024]{2,1,0:T(8,128)(2,1)S(1)}, bf16[2,64,1024]{2,1,0:T(8,128)(2,1)}, u32[]{:S(2)}, u32[]{:S(2)}) collective-permute-start(bf16[2,64,1024]{2,1,0:T(8,128)(2,1)S(1)} %get-tuple-element.50), channel_id=1, source_target_pairs={{1,0},{2,1},{3,2},{4,3},{5,4},{6,5},{7,6},{8,7},{9,8},{10,9},{11,1... | collective-permute-start | bytes 786440 | tf_op jit(solution)/shard_map/ppermute | solution.py:26
  61.0 6.5 %collective-permute-start.7 = (bf16[2,64,1024]{2,1,0:T(8,128)(2,1)S(1)}, bf16[2,64,1024]{2,1,0:T(8,128)(2,1)S(1)}, u32[]{:S(2)}, u32[]{:S(2)}) collective-permute-start(bf16[2,64,1024]{2,1,0:T(8,128)(2,1)S(1)} %broadcast_select_fusion.2), channel_id=1, source_target_pairs={{0,1},{1,0},{2,3},{3,2},{4,5},{5,4},{6,7},{7,6},{8,9},{9,8},{10,11... | collective-permute-start | bytes 786440 | tf_op jit(solution)/shard_map/ppermute | solution.py:53
  68.4 0.9 copy-start.5
  68.4 1.1 copy-start.6
  82.7 7.7 %copy-start.1 = (f32[3,2,128,1024]{3,2,1,0:T(8,128)S(1)}, f32[3,2,128,1024]{3,2,1,0:T(8,128)}, u32[]{:S(2)}) copy-start(f32[3,2,128,1024]{3,2,1,0:T(8,128)} %get-tuple-element.35) | copy-start | bytes 9437188
  84.6 13.8 %collective-permute-start.10 = (bf16[2,64,1024]{2,1,0:T(8,128)(2,1)S(1)}, bf16[2,64,1024]{2,1,0:T(8,128)(2,1)S(1)}, u32[]{:S(2)}, u32[]{:S(2)}) collective-permute-start(bf16[2,64,1024]{2,1,0:T(8,128)(2,1)S(1)} %get-tuple-element.42), channel_id=1, source_target_pairs={{1,0},{2,1},{3,2},{4,3},{5,4},{6,5},{7,6},{8,7},{9,8},{10,9},{11,1... | collective-permute-start | bytes 786440 | tf_op jit(solution)/shard_map/ppermute | solution.py:66
  90.6 7.7 %copy-start = (f32[2,256,1024]{2,1,0:T(8,128)S(1)}, f32[2,256,1024]{2,1,0:T(8,128)}, u32[]{:S(2)}) copy-start(f32[2,256,1024]{2,1,0:T(8,128)} %get-tuple-element.34) | copy-start | bytes 6291460
  90.7 28.4 %collective-permute-start.12 = (bf16[2,128,1024]{2,1,0:T(8,128)(2,1)S(1)}, bf16[2,128,1024]{2,1,0:T(8,128)(2,1)S(1)}, u32[]{:S(2)}, u32[]{:S(2)}) collective-permute-start(bf16[2,128,1024]{2,1,0:T(8,128)(2,1)S(1)} %get-tuple-element.38), channel_id=1, source_target_pairs={{0,16},{1,17},{2,18},{3,19},{4,20},{5,21},{6,22},{7,23},{8,24},{9,... | collective-permute-start | bytes 1572872 | tf_op jit(solution)/shard_map/ppermute | solution.py:60
  90.8 28.4 %collective-permute-start.14 = (bf16[2,128,1024]{2,1,0:T(8,128)(2,1)S(1)}, bf16[2,128,1024]{2,1,0:T(8,128)(2,1)S(1)}, u32[]{:S(2)}, u32[]{:S(2)}) collective-permute-start(bf16[2,128,1024]{2,1,0:T(8,128)(2,1)S(1)} %get-tuple-element.39), channel_id=1, source_target_pairs={{0,4},{1,5},{2,6},{3,7},{4,0},{5,1},{6,2},{7,3},{8,12},{9,13},{10,... | collective-permute-start | bytes 1572872 | tf_op jit(solution)/shard_map/ppermute | solution.py:60
  92.1 29.0 %collective-permute-start.13 = (bf16[2,128,1024]{2,1,0:T(8,128)(2,1)S(1)}, bf16[2,128,1024]{2,1,0:T(8,128)(2,1)S(1)}, u32[]{:S(2)}, u32[]{:S(2)}) collective-permute-start(bf16[2,128,1024]{2,1,0:T(8,128)(2,1)S(1)} %get-tuple-element.40), channel_id=1, source_target_pairs={{0,8},{1,9},{2,10},{3,11},{4,12},{5,13},{6,14},{7,15},{8,0},{9,1},... | collective-permute-start | bytes 1572872 | tf_op jit(solution)/shard_map/ppermute | solution.py:60
  96.3 22.7 %collective-permute-start.11 = (bf16[2,64,1024]{2,1,0:T(8,128)(2,1)S(1)}, bf16[2,64,1024]{2,1,0:T(8,128)(2,1)S(1)}, u32[]{:S(2)}, u32[]{:S(2)}) collective-permute-start(bf16[2,64,1024]{2,1,0:T(8,128)(2,1)S(1)} %get-tuple-element.41), channel_id=1, source_target_pairs={{0,1},{1,2},{2,3},{3,4},{4,5},{5,6},{6,7},{7,8},{8,9},{9,10},{10,1... | collective-permute-start | bytes 786440 | tf_op jit(solution)/shard_map/ppermute | solution.py:66

commit v6 on v5

--- a/solution.py
+++ b/solution.py
@@ -5,7 +5,6 @@
 from jax.experimental import pallas as pl
 from jax.experimental.pallas import tpu as pltpu
 
-HEADS = 16
 HEAD_DIM = 64
 BLOCK = 64
 RAND = 3
@@ -168,7 +167,7 @@
     )(meta, queries, grad_out, padded, glob, *partners)
 
 
-def local(queries, keys, values, grad_out, rand_blocks, global_ids):
+def local_body(queries, keys, values, grad_out, rand_blocks, global_ids):
     tok_rows, width = queries.shape
     block_count = tok_rows // BLOCK
     ctx_count = lax.axis_size("ctx")
@@ -180,7 +179,9 @@
     owners = global_ids // block_count
     local_ids = global_ids % block_count
     spread = [top_bit - 1 - matching for matching in range(RAND)]
-    partners = [partner_2(stacked, "ctx", bit) for bit in spread]
+    partners = []
+    for bit in spread:
+        partners.append(partner_2(stacked, "ctx", bit))
     first_step = 1 << spread[0]
     candidates = []
     for global_slot in range(GLOBALS):
@@ -228,7 +229,7 @@
         P("dp"),
     )
     return jax.shard_map(
-        local,
+        local_body,
         mesh=mesh,
         in_specs=placed,
         out_specs=(

time: 124 us -> 124 us (level)
  no operation moved by 1% of the time
where the time goes in v6:
time: 124 us; the launch traced here: 122 us
  waiting for transfers between devices  57.5 us (46%)
  starting transfers between devices  33.9 us (27%)
  Pallas kernels  13.2 us (11%)
  other arithmetic  10.8 us (9%)
  between operations  3.55 us (3%)
  local copies, waits for them, and re-layouts  3.42 us (3%)
    ppermute x2, waiting for transfers between devices, passed_along(): return lax.ppermute(array, axis, pairs)  20.6 us
    ppermute x6, waiting for transfers between devices, partner_2(): lax.ppermute(array, axis, [(i, i ^ 1 << distance) for i in range(lax.axis...  19.3 us
    pallas_call x1, Pallas kernels, attend(): pl.pallas_call(attend_kernel, grid_spec=pltpu.PrefetchScalarGridSpec(num_...  13.2 us
    ppermute x3, waiting for transfers between devices, from_root(): received = lax.ppermute(carried, axis, [(i, i ^ step) for i in range(size)])  12.6 us
    ppermute x6, starting transfers between devices, partner_2(): lax.ppermute(array, axis, [(i, i ^ 1 << distance) for i in range(lax.axis...  10.4 us
    ppermute x3, starting transfers between devices, from_root(): received = lax.ppermute(carried, axis, [(i, i ^ step) for i in range(size)])  7.98 us
    ppermute x2, starting transfers between devices, passed_along(): return lax.ppermute(array, axis, pairs)  7.62 us
    ppermute x1, starting transfers between devices, padded_2(): after = lax.ppermute(first, axis, down)  5.75 us
  transfers between devices with their start and end apart: 15, of which 7 were waited for; matrix products, arithmetic and copies ran while one was open for 6% of the time, Pallas kernels for 0%

profile of v6, /device:TPU:192, one launch (start us, length us, event | category | flops | bytes accessed | tf_op | source)
XLA Modules:
  0.0 122.3 jit_solution(5767832698573160303)
XLA Ops:
  0.6 1.1 pad_maximum_fusion.1
  1.7 1.5 %collective-permute-start.2 = (bf16[2,128,1024]{2,1,0:T(8,128)(2,1)S(1)}, bf16[2,128,1024]{2,1,0:T(8,128)(2,1)S(1)}, u32[]{:S(2)}, u32[]{:S(2)}) collective-permute-start(bf16[2,128,1024]{2,1,0:T(8,128)(2,1)S(1)} %pad_maximum_fusion.1), channel_id=1, source_target_pairs={{0,16},{1,17},{2,18},{3,19},{4,20},{5,21},{6,22},{7,23},{8,24},{9,... | collective-permute-start | bytes 1572872 | tf_op jit(solution)/shard_map/ppermute | solution.py:59
  3.3 0.7 and_select_fusion
  3.9 0.6 fusion.15
  5.8 0.7 and_compare_fusion.3
  6.5 0.6 fusion.14
  8.4 17.3 %collective-permute-done.2.rest_0_ = bf16[2,128,1024]{2,1,0:T(8,128)(2,1)S(1)} collective-permute-done((bf16[2,128,1024]{2,1,0:T(8,128)(2,1)S(1)}, bf16[2,128,1024]{2,1,0:T(8,128)(2,1)S(1)}, u32[]{:S(2)}, u32[]{:S(2)}) %collective-permute-start.2) | collective-permute-done | bytes 524320 | tf_op jit(solution)/shard_map/ppermute | solution.py:59
  25.7 1.7 %fusion.8 = (bf16[1,2,64,1024]{3,2,1,0:T(8,128)(2,1)S(1)}, bf16[1,2,64,1024]{3,2,1,0:T(8,128)(2,1)S(1)}, bf16[2,64,1024]{2,1,0:T(8,128)(2,1)S(1)}, bf16[2,64,1024]{2,1,0:T(8,128)(2,1)S(1)}) fusion(s32[]{:T(128)S(6)} %select_n.85, bf16[1,128,1024]{2,1,0:T(8,128)(2,1)} %bitcast.48, bf16[1,128,1024]{2,1,0:T(8,128)(2,1)} %bitcast.51, ...), kind=kLoop, calls=%fused_computation.28 | loop fusion | flops 2359296 | bytes 2097162 | tf_op jit(solution)/shard_map/stack | solution.py:193
  27.4 0.0 copy-start.7
  27.4 0.0 copy-start.2
  27.4 0.0 copy-start.3
  27.5 0.1 collective-permute-start.3
  27.6 1.5 %collective-permute-done.3 = bf16[2,64,1024]{2,1,0:T(8,128)(2,1)S(1)} collective-permute-done((bf16[2,64,1024]{2,1,0:T(8,128)(2,1)S(1)}, bf16[2,64,1024]{2,1,0:T(8,128)(2,1)S(1)}, u32[]{:S(2)}, u32[]{:S(2)}) %collective-permute-start.3) | collective-permute-done | bytes 262176 | tf_op jit(solution)/shard_map/ppermute | solution.py:42
  29.1 0.1 fusion.2
  29.2 1.7 %collective-permute-start.4 = (bf16[2,64,1024]{2,1,0:T(8,128)(2,1)S(1)}, bf16[2,64,1024]{2,1,0:T(8,128)(2,1)S(1)}, u32[]{:S(2)}, u32[]{:S(2)}) collective-permute-start(bf16[2,64,1024]{2,1,0:T(8,128)(2,1)S(1)} %fusion.2), channel_id=1, source_target_pairs={{0,2},{1,3},{2,0},{3,1},{4,6},{5,7},{6,4},{7,5},{8,10},{9,11},{10,... | collective-permute-start | bytes 786440 | tf_op jit(solution)/shard_map/ppermute | solution.py:49
  30.9 6.8 %collective-permute-done.4 = bf16[2,64,1024]{2,1,0:T(8,128)(2,1)S(1)} collective-permute-done((bf16[2,64,1024]{2,1,0:T(8,128)(2,1)S(1)}, bf16[2,64,1024]{2,1,0:T(8,128)(2,1)S(1)}, u32[]{:S(2)}, u32[]{:S(2)}) %collective-permute-start.4) | collective-permute-done | bytes 262176 | tf_op jit(solution)/shard_map/ppermute | solution.py:49
  37.6 0.1 broadcast_select_fusion
  37.7 0.0 copy-done.4
  37.8 3.3 %collective-permute-start.5 = (bf16[2,64,1024]{2,1,0:T(8,128)(2,1)S(1)}, bf16[2,64,1024]{2,1,0:T(8,128)(2,1)S(1)}, u32[]{:S(2)}, u32[]{:S(2)}) collective-permute-start(bf16[2,64,1024]{2,1,0:T(8,128)(2,1)S(1)} %broadcast_select_fusion), channel_id=1, source_target_pairs={{0,4},{1,5},{2,6},{3,7},{4,0},{5,1},{6,2},{7,3},{8,12},{9,13},{10,... | collective-permute-start | bytes 786440 | tf_op jit(solution)/shard_map/ppermute | solution.py:49
  41.0 5.8 %collective-permute-done.5 = bf16[2,64,1024]{2,1,0:T(8,128)(2,1)S(1)} collective-permute-done((bf16[2,64,1024]{2,1,0:T(8,128)(2,1)S(1)}, bf16[2,64,1024]{2,1,0:T(8,128)(2,1)S(1)}, u32[]{:S(2)}, u32[]{:S(2)}) %collective-permute-start.5) | collective-permute-done | bytes 262176 | tf_op jit(solution)/shard_map/ppermute | solution.py:49
  46.8 0.1 broadcast_select_fusion.1
  46.9 3.0 %collective-permute-start.6 = (bf16[2,64,1024]{2,1,0:T(8,128)(2,1)S(1)}, bf16[2,64,1024]{2,1,0:T(8,128)(2,1)S(1)}, u32[]{:S(2)}, u32[]{:S(2)}) collective-permute-start(bf16[2,64,1024]{2,1,0:T(8,128)(2,1)S(1)} %broadcast_select_fusion.1), channel_id=1, source_target_pairs={{0,8},{1,9},{2,10},{3,11},{4,12},{5,13},{6,14},{7,15},{8,0},{9,1},... | collective-permute-start | bytes 786440 | tf_op jit(solution)/shard_map/ppermute | solution.py:49
  50.0 3.2 %collective-permute-start.9 = (bf16[2,128,1024]{2,1,0:T(8,128)(2,1)S(1)}, bf16[2,128,1024]{2,1,0:T(8,128)(2,1)S(1)}, u32[]{:S(2)}, u32[]{:S(2)}) collective-permute-start(bf16[2,128,1024]{2,1,0:T(8,128)(2,1)S(1)} %pad_maximum_fusion.1), channel_id=1, source_target_pairs={{0,4},{1,5},{2,6},{3,7},{4,0},{5,1},{6,2},{7,3},{8,12},{9,13},{10,... | collective-permute-start | bytes 1572872 | tf_op jit(solution)/shard_map/ppermute | solution.py:59
  53.2 0.1 collective-permute-start.8
  53.3 1.9 %collective-permute-start = (bf16[2,64,1024]{2,1,0:T(8,128)(2,1)S(1)}, bf16[2,64,1024]{2,1,0:T(8,128)(2,1)}, u32[]{:S(2)}, u32[]{:S(2)}) collective-permute-start(bf16[2,64,1024]{2,1,0:T(8,128)(2,1)S(1)} %get-tuple-element.49), channel_id=1, source_target_pairs={{0,1},{1,2},{2,3},{3,4},{4,5},{5,6},{6,7},{7,8},{8,9},{9,10},{10,1... | collective-permute-start | bytes 786440 | tf_op jit(solution)/shard_map/ppermute | solution.py:24
  55.2 5.8 %collective-permute-start.1 = (bf16[2,64,1024]{2,1,0:T(8,128)(2,1)S(1)}, bf16[2,64,1024]{2,1,0:T(8,128)(2,1)}, u32[]{:S(2)}, u32[]{:S(2)}) collective-permute-start(bf16[2,64,1024]{2,1,0:T(8,128)(2,1)S(1)} %get-tuple-element.50), channel_id=1, source_target_pairs={{1,0},{2,1},{3,2},{4,3},{5,4},{6,5},{7,6},{8,7},{9,8},{10,9},{11,1... | collective-permute-start | bytes 786440 | tf_op jit(solution)/shard_map/ppermute | solution.py:25
  60.9 0.0 collective-permute-done.6
  60.9 0.1 broadcast_select_fusion.2
  61.0 0.1 collective-permute-start.7
  61.2 0.0 copy-done.7
  61.2 0.1 reshape.95
  61.3 0.6 pad_add_fusion.meta_ref
  61.8 3.6 %collective-permute-done = bf16[2,64,1024]{2,1,0:T(8,128)(2,1)} collective-permute-done((bf16[2,64,1024]{2,1,0:T(8,128)(2,1)S(1)}, bf16[2,64,1024]{2,1,0:T(8,128)(2,1)}, u32[]{:S(2)}, u32[]{:S(2)}) %collective-permute-start) | collective-permute-done | bytes 262176 | tf_op jit(solution)/shard_map/ppermute | solution.py:24
  65.4 0.0 collective-permute-done.1
  65.4 0.0 copy-done.2
  65.4 2.1 %pad_maximum_fusion.win_ref = bf16[2,256,1024]{2,1,0:T(8,128)(2,1)} fusion(bf16[2,64,1024]{2,1,0:T(8,128)(2,1)} %collective-permute-done.1, bf16[1,128,1024]{2,1,0:T(8,128)(2,1)S(1)} %bitcast.52, bf16[1,128,1024]{2,1,0:T(8,128)(2,1)S(1)} %bitcast.49, bf16[2,64,1024]{2,1,0:T(8,128)(2,1)} %collective-permute-done), kind=kLoop, calls=%fused_computation | loop fusion | flops 4194304 | bytes 2097152 | tf_op jit(solution)/shard_map/concatenate | solution.py:26
  67.5 0.0 collective-permute-done.7
  67.6 0.8 pad_maximum_fusion.2
  68.4 0.0 collective-permute-done.9.rest_2_
  68.4 0.0 collective-permute-done.8.rest_1_
  68.4 0.8 copy-done.5
  69.3 0.2 copy-done.6
  69.5 13.2 %shard_map.93 = (bf16[128,1024]{1,0:T(8,128)(2,1)}, bf16[128,1024]{1,0:T(8,128)(2,1)}, f32[2,256,1024]{2,1,0:T(8,128)}, f32[3,2,128,1024]{3,2,1,0:T(8,128)}) custom-call(s32[10]{0:T(128)} %pad_add_fusion.meta_ref, bf16[128,1024]{1,0:T(8,128)(2,1)} %q_ref.1, bf16[128,1024]{1,0:T(8,128)(2,1)} %g_ref.1, bf16[2,256,1024]{2,1,0:T(8,128)(2,1)} %pad_maximum_fusion.win_ref, ...), custom_call_target="tpu_custom_call" | custom-call | tf_op jit(solution)/shard_map/pallas_call | solution.py:157
  82.7 1.9 %convert.13 = bf16[2,256,1024]{2,1,0:T(8,128)(2,1)S(1)} convert(f32[2,256,1024]{2,1,0:T(8,128)} %get-tuple-element.34) | non-fusion elementwise | flops 524288 | bytes 3145728 | tf_op jit(solution)/shard_map/convert.6
  84.6 5.7 %collective-permute-start.10 = (bf16[2,64,1024]{2,1,0:T(8,128)(2,1)S(1)}, bf16[2,64,1024]{2,1,0:T(8,128)(2,1)S(1)}, u32[]{:S(2)}, u32[]{:S(2)}) collective-permute-start(bf16[2,64,1024]{2,1,0:T(8,128)(2,1)S(1)} %get-tuple-element.42), channel_id=1, source_target_pairs={{1,0},{2,1},{3,2},{4,3},{5,4},{6,5},{7,6},{8,7},{9,8},{10,9},{11,1... | collective-permute-start | bytes 786440 | tf_op jit(solution)/shard_map/ppermute | solution.py:65
  90.3 0.0 copy-done.1
  90.3 0.2 convert.14
  90.6 0.0 copy-start
  90.6 0.1 slice_bitcast_fusion.2
  90.7 0.1 collective-permute-start.12
  90.8 1.3 %collective-permute-start.14 = (bf16[2,128,1024]{2,1,0:T(8,128)(2,1)S(1)}, bf16[2,128,1024]{2,1,0:T(8,128)(2,1)S(1)}, u32[]{:S(2)}, u32[]{:S(2)}) collective-permute-start(bf16[2,128,1024]{2,1,0:T(8,128)(2,1)S(1)} %get-tuple-element.39), channel_id=1, source_target_pairs={{0,4},{1,5},{2,6},{3,7},{4,0},{5,1},{6,2},{7,3},{8,12},{9,13},{10,... | collective-permute-start | bytes 1572872 | tf_op jit(solution)/shard_map/ppermute | solution.py:59
  92.1 4.2 %collective-permute-start.13 = (bf16[2,128,1024]{2,1,0:T(8,128)(2,1)S(1)}, bf16[2,128,1024]{2,1,0:T(8,128)(2,1)S(1)}, u32[]{:S(2)}, u32[]{:S(2)}) collective-permute-start(bf16[2,128,1024]{2,1,0:T(8,128)(2,1)S(1)} %get-tuple-element.40), channel_id=1, source_target_pairs={{0,8},{1,9},{2,10},{3,11},{4,12},{5,13},{6,14},{7,15},{8,0},{9,1},... | collective-permute-start | bytes 1572872 | tf_op jit(solution)/shard_map/ppermute | solution.py:59
  96.3 1.9 %collective-permute-start.11 = (bf16[2,64,1024]{2,1,0:T(8,128)(2,1)S(1)}, bf16[2,64,1024]{2,1,0:T(8,128)(2,1)S(1)}, u32[]{:S(2)}, u32[]{:S(2)}) collective-permute-start(bf16[2,64,1024]{2,1,0:T(8,128)(2,1)S(1)} %get-tuple-element.41), channel_id=1, source_target_pairs={{0,1},{1,2},{2,3},{3,4},{4,5},{5,6},{6,7},{7,8},{8,9},{9,10},{10,1... | collective-permute-start | bytes 786440 | tf_op jit(solution)/shard_map/ppermute | solution.py:65
  98.2 0.0 copy-done
  98.3 0.1 slice.114
  98.4 0.0 collective-permute-done.10
  98.4 0.1 add_dynamic-update-slice_fusion
  98.5 20.6 %collective-permute-done.11 = bf16[2,64,1024]{2,1,0:T(8,128)(2,1)S(1)} collective-permute-done((bf16[2,64,1024]{2,1,0:T(8,128)(2,1)S(1)}, bf16[2,64,1024]{2,1,0:T(8,128)(2,1)S(1)}, u32[]{:S(2)}, u32[]{:S(2)}) %collective-permute-start.11) | collective-permute-done | bytes 262176 | tf_op jit(solution)/shard_map/ppermute | solution.py:65
  119.1 0.1 fusion
  119.2 0.0 collective-permute-done.12
  119.2 0.0 collective-permute-done.14
  119.2 2.0 %collective-permute-done.13 = bf16[2,128,1024]{2,1,0:T(8,128)(2,1)S(1)} collective-permute-done((bf16[2,128,1024]{2,1,0:T(8,128)(2,1)S(1)}, bf16[2,128,1024]{2,1,0:T(8,128)(2,1)S(1)}, u32[]{:S(2)}, u32[]{:S(2)}) %collective-permute-start.13) | collective-permute-done | bytes 524320 | tf_op jit(solution)/shard_map/ppermute | solution.py:59
  121.2 0.3 add_convert_fusion
  121.5 0.8 slice_bitcast_fusion.3
  (10 shorter events, 0.1 us)
Async XLA Ops:
  1.7 24.0 %collective-permute-start.2 = (bf16[2,128,1024]{2,1,0:T(8,128)(2,1)S(1)}, bf16[2,128,1024]{2,1,0:T(8,128)(2,1)S(1)}, u32[]{:S(2)}, u32[]{:S(2)}) collective-permute-start(bf16[2,128,1024]{2,1,0:T(8,128)(2,1)S(1)} %pad_maximum_fusion.1), channel_id=1, source_target_pairs={{0,16},{1,17},{2,18},{3,19},{4,20},{5,21},{6,22},{7,23},{8,24},{9,... | collective-permute-start | bytes 1572872 | tf_op jit(solution)/shard_map/ppermute | solution.py:59
  25.7 12.1 %copy-start.4 = (bf16[2,128,1024]{2,1,0:T(8,128)(2,1)}, bf16[2,128,1024]{2,1,0:T(8,128)(2,1)S(1)}, u32[]{:S(2)}) copy-start(bf16[2,128,1024]{2,1,0:T(8,128)(2,1)S(1)} %collective-permute-done.2.rest_0_) | copy-start | bytes 1572868
  27.4 33.8 %copy-start.7 = (s32[2,3]{1,0:T(2,128)S(1)}, s32[2,3]{1,0:T(2,128)}, u32[]{:S(2)}) copy-start(s32[2,3]{1,0:T(2,128)} %param.14) | copy-start | bytes 76
  27.4 38.0 %copy-start.2 = (bf16[128,1024]{1,0:T(8,128)(2,1)S(1)}, bf16[128,1024]{1,0:T(8,128)(2,1)}, u32[]{:S(2)}) copy-start(bf16[128,1024]{1,0:T(8,128)(2,1)} %param.11) | copy-start | bytes 786436
  27.4 38.0 %copy-start.3 = (bf16[128,1024]{1,0:T(8,128)(2,1)S(1)}, bf16[128,1024]{1,0:T(8,128)(2,1)}, u32[]{:S(2)}) copy-start(bf16[128,1024]{1,0:T(8,128)(2,1)} %param.12) | copy-start | bytes 786436
  27.5 1.6 %collective-permute-start.3 = (bf16[2,64,1024]{2,1,0:T(8,128)(2,1)S(1)}, bf16[2,64,1024]{2,1,0:T(8,128)(2,1)S(1)}, u32[]{:S(2)}, u32[]{:S(2)}) collective-permute-start(bf16[2,64,1024]{2,1,0:T(8,128)(2,1)S(1)} %fusion.12), channel_id=1, source_target_pairs={{0,1},{1,0},{2,3},{3,2},{4,5},{5,4},{6,7},{7,6},{8,9},{9,8},{10,11... | collective-permute-start | bytes 786440 | tf_op jit(solution)/shard_map/ppermute | solution.py:42
  29.2 8.4 %collective-permute-start.4 = (bf16[2,64,1024]{2,1,0:T(8,128)(2,1)S(1)}, bf16[2,64,1024]{2,1,0:T(8,128)(2,1)S(1)}, u32[]{:S(2)}, u32[]{:S(2)}) collective-permute-start(bf16[2,64,1024]{2,1,0:T(8,128)(2,1)S(1)} %fusion.2), channel_id=1, source_target_pairs={{0,2},{1,3},{2,0},{3,1},{4,6},{5,7},{6,4},{7,5},{8,10},{9,11},{10,... | collective-permute-start | bytes 786440 | tf_op jit(solution)/shard_map/ppermute | solution.py:49
  37.8 9.1 %collective-permute-start.5 = (bf16[2,64,1024]{2,1,0:T(8,128)(2,1)S(1)}, bf16[2,64,1024]{2,1,0:T(8,128)(2,1)S(1)}, u32[]{:S(2)}, u32[]{:S(2)}) collective-permute-start(bf16[2,64,1024]{2,1,0:T(8,128)(2,1)S(1)} %broadcast_select_fusion), channel_id=1, source_target_pairs={{0,4},{1,5},{2,6},{3,7},{4,0},{5,1},{6,2},{7,3},{8,12},{9,13},{10,... | collective-permute-start | bytes 786440 | tf_op jit(solution)/shard_map/ppermute | solution.py:49
  46.9 14.0 %collective-permute-start.6 = (bf16[2,64,1024]{2,1,0:T(8,128)(2,1)S(1)}, bf16[2,64,1024]{2,1,0:T(8,128)(2,1)S(1)}, u32[]{:S(2)}, u32[]{:S(2)}) collective-permute-start(bf16[2,64,1024]{2,1,0:T(8,128)(2,1)S(1)} %broadcast_select_fusion.1), channel_id=1, source_target_pairs={{0,8},{1,9},{2,10},{3,11},{4,12},{5,13},{6,14},{7,15},{8,0},{9,1},... | collective-permute-start | bytes 786440 | tf_op jit(solution)/shard_map/ppermute | solution.py:49
  50.0 18.5 %collective-permute-start.9 = (bf16[2,128,1024]{2,1,0:T(8,128)(2,1)S(1)}, bf16[2,128,1024]{2,1,0:T(8,128)(2,1)S(1)}, u32[]{:S(2)}, u32[]{:S(2)}) collective-permute-start(bf16[2,128,1024]{2,1,0:T(8,128)(2,1)S(1)} %pad_maximum_fusion.1), channel_id=1, source_target_pairs={{0,4},{1,5},{2,6},{3,7},{4,0},{5,1},{6,2},{7,3},{8,12},{9,13},{10,... | collective-permute-start | bytes 1572872 | tf_op jit(solution)/shard_map/ppermute | solution.py:59
  53.2 15.3 %collective-permute-start.8 = (bf16[2,128,1024]{2,1,0:T(8,128)(2,1)S(1)}, bf16[2,128,1024]{2,1,0:T(8,128)(2,1)S(1)}, u32[]{:S(2)}, u32[]{:S(2)}) collective-permute-start(bf16[2,128,1024]{2,1,0:T(8,128)(2,1)S(1)} %pad_maximum_fusion.1), channel_id=1, source_target_pairs={{0,8},{1,9},{2,10},{3,11},{4,12},{5,13},{6,14},{7,15},{8,0},{9,1},... | collective-permute-start | bytes 1572872 | tf_op jit(solution)/shard_map/ppermute | solution.py:59
  53.3 12.2 %collective-permute-start = (bf16[2,64,1024]{2,1,0:T(8,128)(2,1)S(1)}, bf16[2,64,1024]{2,1,0:T(8,128)(2,1)}, u32[]{:S(2)}, u32[]{:S(2)}) collective-permute-start(bf16[2,64,1024]{2,1,0:T(8,128)(2,1)S(1)} %get-tuple-element.49), channel_id=1, source_target_pairs={{0,1},{1,2},{2,3},{3,4},{4,5},{5,6},{6,7},{7,8},{8,9},{9,10},{10,1... | collective-permute-start | bytes 786440 | tf_op jit(solution)/shard_map/ppermute | solution.py:24
  55.2 10.3 %collective-permute-start.1 = (bf16[2,64,1024]{2,1,0:T(8,128)(2,1)S(1)}, bf16[2,64,1024]{2,1,0:T(8,128)(2,1)}, u32[]{:S(2)}, u32[]{:S(2)}) collective-permute-start(bf16[2,64,1024]{2,1,0:T(8,128)(2,1)S(1)} %get-tuple-element.50), channel_id=1, source_target_pairs={{1,0},{2,1},{3,2},{4,3},{5,4},{6,5},{7,6},{8,7},{9,8},{10,9},{11,1... | collective-permute-start | bytes 786440 | tf_op jit(solution)/shard_map/ppermute | solution.py:25
  61.0 6.5 %collective-permute-start.7 = (bf16[2,64,1024]{2,1,0:T(8,128)(2,1)S(1)}, bf16[2,64,1024]{2,1,0:T(8,128)(2,1)S(1)}, u32[]{:S(2)}, u32[]{:S(2)}) collective-permute-start(bf16[2,64,1024]{2,1,0:T(8,128)(2,1)S(1)} %broadcast_select_fusion.2), channel_id=1, source_target_pairs={{0,1},{1,0},{2,3},{3,2},{4,5},{5,4},{6,7},{7,6},{8,9},{9,8},{10,11... | collective-permute-start | bytes 786440 | tf_op jit(solution)/shard_map/ppermute | solution.py:52
  68.4 0.9 copy-start.5
  68.4 1.1 copy-start.6
  82.7 7.7 %copy-start.1 = (f32[3,2,128,1024]{3,2,1,0:T(8,128)S(1)}, f32[3,2,128,1024]{3,2,1,0:T(8,128)}, u32[]{:S(2)}) copy-start(f32[3,2,128,1024]{3,2,1,0:T(8,128)} %get-tuple-element.35) | copy-start | bytes 9437188
  84.6 13.8 %collective-permute-start.10 = (bf16[2,64,1024]{2,1,0:T(8,128)(2,1)S(1)}, bf16[2,64,1024]{2,1,0:T(8,128)(2,1)S(1)}, u32[]{:S(2)}, u32[]{:S(2)}) collective-permute-start(bf16[2,64,1024]{2,1,0:T(8,128)(2,1)S(1)} %get-tuple-element.42), channel_id=1, source_target_pairs={{1,0},{2,1},{3,2},{4,3},{5,4},{6,5},{7,6},{8,7},{9,8},{10,9},{11,1... | collective-permute-start | bytes 786440 | tf_op jit(solution)/shard_map/ppermute | solution.py:65
  90.6 7.7 %copy-start = (f32[2,256,1024]{2,1,0:T(8,128)S(1)}, f32[2,256,1024]{2,1,0:T(8,128)}, u32[]{:S(2)}) copy-start(f32[2,256,1024]{2,1,0:T(8,128)} %get-tuple-element.34) | copy-start | bytes 6291460
  90.7 28.4 %collective-permute-start.12 = (bf16[2,128,1024]{2,1,0:T(8,128)(2,1)S(1)}, bf16[2,128,1024]{2,1,0:T(8,128)(2,1)S(1)}, u32[]{:S(2)}, u32[]{:S(2)}) collective-permute-start(bf16[2,128,1024]{2,1,0:T(8,128)(2,1)S(1)} %get-tuple-element.38), channel_id=1, source_target_pairs={{0,16},{1,17},{2,18},{3,19},{4,20},{5,21},{6,22},{7,23},{8,24},{9,... | collective-permute-start | bytes 1572872 | tf_op jit(solution)/shard_map/ppermute | solution.py:59
  90.8 28.4 %collective-permute-start.14 = (bf16[2,128,1024]{2,1,0:T(8,128)(2,1)S(1)}, bf16[2,128,1024]{2,1,0:T(8,128)(2,1)S(1)}, u32[]{:S(2)}, u32[]{:S(2)}) collective-permute-start(bf16[2,128,1024]{2,1,0:T(8,128)(2,1)S(1)} %get-tuple-element.39), channel_id=1, source_target_pairs={{0,4},{1,5},{2,6},{3,7},{4,0},{5,1},{6,2},{7,3},{8,12},{9,13},{10,... | collective-permute-start | bytes 1572872 | tf_op jit(solution)/shard_map/ppermute | solution.py:59
  92.1 29.0 %collective-permute-start.13 = (bf16[2,128,1024]{2,1,0:T(8,128)(2,1)S(1)}, bf16[2,128,1024]{2,1,0:T(8,128)(2,1)S(1)}, u32[]{:S(2)}, u32[]{:S(2)}) collective-permute-start(bf16[2,128,1024]{2,1,0:T(8,128)(2,1)S(1)} %get-tuple-element.40), channel_id=1, source_target_pairs={{0,8},{1,9},{2,10},{3,11},{4,12},{5,13},{6,14},{7,15},{8,0},{9,1},... | collective-permute-start | bytes 1572872 | tf_op jit(solution)/shard_map/ppermute | solution.py:59
  96.3 22.7 %collective-permute-start.11 = (bf16[2,64,1024]{2,1,0:T(8,128)(2,1)S(1)}, bf16[2,64,1024]{2,1,0:T(8,128)(2,1)S(1)}, u32[]{:S(2)}, u32[]{:S(2)}) collective-permute-start(bf16[2,64,1024]{2,1,0:T(8,128)(2,1)S(1)} %get-tuple-element.41), channel_id=1, source_target_pairs={{0,1},{1,2},{2,3},{3,4},{4,5},{5,6},{6,7},{7,8},{8,9},{9,10},{10,1... | collective-permute-start | bytes 786440 | tf_op jit(solution)/shard_map/ppermute | solution.py:65

commit v7 on v6

--- a/solution.py
+++ b/solution.py
@@ -182,15 +182,11 @@
     partners = []
     for bit in spread:
         partners.append(partner_2(stacked, "ctx", bit))
-    first_step = 1 << spread[0]
-    candidates = []
-    for global_slot in range(GLOBALS):
-        start = local_ids[global_slot] * BLOCK
-        own_piece = lax.dynamic_slice_in_dim(stacked, start, BLOCK, 1)
-        far_piece = lax.dynamic_slice_in_dim(partners[0], start, BLOCK, 1)
-        from_far = owners[global_slot] == (position ^ first_step)
-        candidates.append(jnp.where(from_far, far_piece, own_piece))
-    fetched = from_root(jnp.stack(candidates), "ctx", owners, first_step)
+    candidates = [
+        lax.dynamic_slice_in_dim(stacked, local_ids[global_slot] * BLOCK, BLOCK, 1)
+        for global_slot in range(GLOBALS)
+    ]
+    fetched = from_root(jnp.stack(candidates), "ctx", owners, 0)
     glob = jnp.swapaxes(fetched, 0, 1).reshape(2, GLOBALS * BLOCK, width)
     global_block = position * block_count + block_iota
     seq_blocks = block_count * ctx_count

time: 124 us -> 130 us (1.048)
  the two profiles are of different devices: /device:TPU:192 before, /device:TPU:2 now
where the time goes in v7:
time: 130 us
  waiting for transfers between devices  75.2 us (58%)
  starting transfers between devices  27.6 us (21%)
  Pallas kernels  13.2 us (10%)
  other arithmetic  8.99 us (7%)
  local copies, waits for them, and re-layouts  2.62 us (2%)
  between operations  2.22 us (2%)
    ppermute x6, waiting for transfers between devices, partner_2(): lax.ppermute(array, axis, [(i, i ^ 1 << distance) for i in range(lax.axis...  39.7 us
    ppermute x4, waiting for transfers between devices, from_root(): received = lax.ppermute(carried, axis, [(i, i ^ step) for i in range(size)])  33.1 us
    pallas_call x1, Pallas kernels, attend(): pl.pallas_call(attend_kernel, grid_spec=pltpu.PrefetchScalarGridSpec(num_...  13.2 us
    ppermute x6, starting transfers between devices, partner_2(): lax.ppermute(array, axis, [(i, i ^ 1 << distance) for i in range(lax.axis...  11.1 us
    ppermute x4, starting transfers between devices, from_root(): received = lax.ppermute(carried, axis, [(i, i ^ step) for i in range(size)])  10.3 us
    ppermute x2, starting transfers between devices, passed_along(): return lax.ppermute(array, axis, pairs)  2.76 us
  transfers between devices with their start and end apart: 16, of which 9 were waited for; matrix products, arithmetic and copies ran while one was open for 3% of the time, Pallas kernels for 0%

profile of v7, /device:TPU:2, one launch (start us, length us, event | category | flops | bytes accessed | tf_op | source)
XLA Modules:
  0.0 129.9 jit_solution(16969828191781222032)
XLA Ops:
  0.6 0.0 copy-start.7
  0.6 0.7 and_select_fusion
  1.4 0.6 fusion.11
  3.3 1.4 %fusion.7 = (bf16[1,2,64,1024]{3,2,0,1:T(8,128)(2,1)S(1)}, bf16[2,64,1024]{2,1,0:T(8,128)(2,1)S(1)}, bf16[2,64,1024]{2,1,0:T(8,128)(2,1)S(1)}, bf16[1,2,64,1024]{3,2,0,1:T(8,128)(2,1)S(1)}) fusion(s32[]{:T(128)S(6)} %select_n.73, bf16[1,128,1024]{2,1,0:T(8,128)(2,1)} %bitcast.41, bf16[1,128,1024]{2,1,0:T(8,128)(2,1)} %bitcast.44, s32[]{:T(128)S(6)} %select_n.74), kind=kLoop, calls=%fused_computation.27 | loop fusion | flops 2097152 | bytes 1572872 | tf_op jit(solution)/shard_map/stack | solution.py:189
  4.7 0.0 copy-start.2
  4.7 0.0 copy-start.3
  4.8 0.1 collective-permute-start.2
  4.9 0.0 copy-done.7
  4.9 1.5 %collective-permute-done.2 = bf16[2,64,1024]{2,1,0:T(8,128)(2,1)S(1)} collective-permute-done((bf16[2,64,1024]{2,1,0:T(8,128)(2,1)S(1)}, bf16[2,64,1024]{2,1,0:T(8,128)(2,1)S(1)}, u32[]{:S(2)}, u32[]{:S(2)}) %collective-permute-start.2) | collective-permute-done | bytes 262176 | tf_op jit(solution)/shard_map/ppermute | solution.py:42
  6.4 0.1 fusion.2
  6.5 1.7 %collective-permute-start.3 = (bf16[2,64,1024]{2,1,0:T(8,128)(2,1)S(1)}, bf16[2,64,1024]{2,1,0:T(8,128)(2,1)S(1)}, u32[]{:S(2)}, u32[]{:S(2)}) collective-permute-start(bf16[2,64,1024]{2,1,0:T(8,128)(2,1)S(1)} %fusion.2), channel_id=1, source_target_pairs={{0,2},{1,3},{2,0},{3,1},{4,6},{5,7},{6,4},{7,5},{8,10},{9,11},{10,... | collective-permute-start | bytes 786440 | tf_op jit(solution)/shard_map/ppermute | solution.py:49
  8.2 6.8 %collective-permute-done.3 = bf16[2,64,1024]{2,1,0:T(8,128)(2,1)S(1)} collective-permute-done((bf16[2,64,1024]{2,1,0:T(8,128)(2,1)S(1)}, bf16[2,64,1024]{2,1,0:T(8,128)(2,1)S(1)}, u32[]{:S(2)}, u32[]{:S(2)}) %collective-permute-start.3) | collective-permute-done | bytes 262176 | tf_op jit(solution)/shard_map/ppermute | solution.py:49
  14.9 0.1 broadcast_select_fusion
  15.0 3.3 %collective-permute-start.4 = (bf16[2,64,1024]{2,1,0:T(8,128)(2,1)S(1)}, bf16[2,64,1024]{2,1,0:T(8,128)(2,1)S(1)}, u32[]{:S(2)}, u32[]{:S(2)}) collective-permute-start(bf16[2,64,1024]{2,1,0:T(8,128)(2,1)S(1)} %broadcast_select_fusion), channel_id=1, source_target_pairs={{0,4},{1,5},{2,6},{3,7},{4,0},{5,1},{6,2},{7,3},{8,12},{9,13},{10,... | collective-permute-start | bytes 786440 | tf_op jit(solution)/shard_map/ppermute | solution.py:49
  18.3 5.8 %collective-permute-done.4 = bf16[2,64,1024]{2,1,0:T(8,128)(2,1)S(1)} collective-permute-done((bf16[2,64,1024]{2,1,0:T(8,128)(2,1)S(1)}, bf16[2,64,1024]{2,1,0:T(8,128)(2,1)S(1)}, u32[]{:S(2)}, u32[]{:S(2)}) %collective-permute-start.4) | collective-permute-done | bytes 262176 | tf_op jit(solution)/shard_map/ppermute | solution.py:49
  24.1 0.1 broadcast_select_fusion.1
  24.2 2.0 %collective-permute-start.5 = (bf16[2,64,1024]{2,1,0:T(8,128)(2,1)S(1)}, bf16[2,64,1024]{2,1,0:T(8,128)(2,1)S(1)}, u32[]{:S(2)}, u32[]{:S(2)}) collective-permute-start(bf16[2,64,1024]{2,1,0:T(8,128)(2,1)S(1)} %broadcast_select_fusion.1), channel_id=1, source_target_pairs={{0,8},{1,9},{2,10},{3,11},{4,12},{5,13},{6,14},{7,15},{8,0},{9,1},... | collective-permute-start | bytes 786440 | tf_op jit(solution)/shard_map/ppermute | solution.py:49
  26.2 4.9 %collective-permute-done.5 = bf16[2,64,1024]{2,1,0:T(8,128)(2,1)S(1)} collective-permute-done((bf16[2,64,1024]{2,1,0:T(8,128)(2,1)S(1)}, bf16[2,64,1024]{2,1,0:T(8,128)(2,1)S(1)}, u32[]{:S(2)}, u32[]{:S(2)}) %collective-permute-start.5) | collective-permute-done | bytes 262176 | tf_op jit(solution)/shard_map/ppermute | solution.py:49
  31.1 0.1 broadcast_select_fusion.2
  31.2 3.4 %collective-permute-start.6 = (bf16[2,64,1024]{2,1,0:T(8,128)(2,1)S(1)}, bf16[2,64,1024]{2,1,0:T(8,128)(2,1)S(1)}, u32[]{:S(2)}, u32[]{:S(2)}) collective-permute-start(bf16[2,64,1024]{2,1,0:T(8,128)(2,1)S(1)} %broadcast_select_fusion.2), channel_id=1, source_target_pairs={{0,16},{1,17},{2,18},{3,19},{4,20},{5,21},{6,22},{7,23},{8,24},{9,... | collective-permute-start | bytes 786440 | tf_op jit(solution)/shard_map/ppermute | solution.py:49
  34.6 0.0 copy-done.2
  34.6 0.0 copy-done.3
  34.6 0.1 pad_maximum_fusion.1
  34.6 3.3 %collective-permute-start.10 = (bf16[2,128,1024]{2,1,0:T(8,128)(2,1)S(1)}, bf16[2,128,1024]{2,1,0:T(8,128)(2,1)S(1)}, u32[]{:S(2)}, u32[]{:S(2)}) collective-permute-start(bf16[2,128,1024]{2,1,0:T(8,128)(2,1)S(1)} %pad_maximum_fusion.1), channel_id=1, source_target_pairs={{0,4},{1,5},{2,6},{3,7},{4,0},{5,1},{6,2},{7,3},{8,12},{9,13},{10,... | collective-permute-start | bytes 1572872 | tf_op jit(solution)/shard_map/ppermute | solution.py:59
  37.9 0.0 collective-permute-start.8
  38.0 2.0 %collective-permute-start = (bf16[2,64,1024]{2,1,0:T(8,128)(2,1)S(1)}, bf16[2,64,1024]{2,1,0:T(8,128)(2,1)}, u32[]{:S(2)}, u32[]{:S(2)}) collective-permute-start(bf16[2,64,1024]{2,1,0:T(8,128)(2,1)S(1)} %get-tuple-element.48), channel_id=1, source_target_pairs={{0,1},{1,2},{2,3},{3,4},{4,5},{5,6},{6,7},{7,8},{8,9},{9,10},{10,1... | collective-permute-start | bytes 786440 | tf_op jit(solution)/shard_map/ppermute | solution.py:24
  40.0 1.3 collective-permute-start.1
  41.2 15.6 %collective-permute-done.6 = bf16[2,64,1024]{2,1,0:T(8,128)(2,1)S(1)} collective-permute-done((bf16[2,64,1024]{2,1,0:T(8,128)(2,1)S(1)}, bf16[2,64,1024]{2,1,0:T(8,128)(2,1)S(1)}, u32[]{:S(2)}, u32[]{:S(2)}) %collective-permute-start.6) | collective-permute-done | bytes 262176 | tf_op jit(solution)/shard_map/ppermute | solution.py:49
  56.9 0.1 broadcast_select_fusion.3
  57.0 0.1 collective-permute-start.7
  57.1 0.0 copy-done.8
  57.1 0.1 reshape.97
  57.2 0.0 collective-permute-done
  57.2 0.0 collective-permute-start.9
  57.2 0.6 pad_add_fusion.meta_ref
  57.8 0.0 collective-permute-done.1
  57.8 2.1 %pad_maximum_fusion.win_ref = bf16[2,256,1024]{2,1,0:T(8,128)(2,1)} fusion(bf16[2,64,1024]{2,1,0:T(8,128)(2,1)} %collective-permute-done.1, bf16[1,128,1024]{2,1,0:T(8,128)(2,1)S(1)} %bitcast.46, bf16[1,128,1024]{2,1,0:T(8,128)(2,1)S(1)} %bitcast.43, bf16[2,64,1024]{2,1,0:T(8,128)(2,1)} %collective-permute-done), kind=kLoop, calls=%fused_computation | loop fusion | flops 4194304 | bytes 2097152 | tf_op jit(solution)/shard_map/concatenate | solution.py:26
  59.9 0.0 collective-permute-done.7
  59.9 0.9 pad_maximum_fusion.2
  60.8 0.0 collective-permute-done.10.rest_2_
  60.8 6.2 %collective-permute-done.8.rest_0_ = bf16[2,128,1024]{2,1,0:T(8,128)(2,1)S(1)} collective-permute-done((bf16[2,128,1024]{2,1,0:T(8,128)(2,1)S(1)}, bf16[2,128,1024]{2,1,0:T(8,128)(2,1)S(1)}, u32[]{:S(2)}, u32[]{:S(2)}) %collective-permute-start.8) | collective-permute-done | bytes 524320 | tf_op jit(solution)/shard_map/ppermute | solution.py:59
  67.0 11.5 %collective-permute-done.9.rest_1_ = bf16[2,128,1024]{2,1,0:T(8,128)(2,1)S(1)} collective-permute-done((bf16[2,128,1024]{2,1,0:T(8,128)(2,1)S(1)}, bf16[2,128,1024]{2,1,0:T(8,128)(2,1)S(1)}, u32[]{:S(2)}, u32[]{:S(2)}) %collective-permute-start.9) | collective-permute-done | bytes 524320 | tf_op jit(solution)/shard_map/ppermute | solution.py:59
  78.5 0.0 copy-done.4
  78.5 0.8 copy-done.6
  79.3 13.2 %shard_map.93 = (bf16[128,1024]{1,0:T(8,128)(2,1)}, bf16[128,1024]{1,0:T(8,128)(2,1)}, f32[2,256,1024]{2,1,0:T(8,128)}, f32[3,2,128,1024]{3,2,1,0:T(8,128)}) custom-call(s32[10]{0:T(128)} %pad_add_fusion.meta_ref, bf16[128,1024]{1,0:T(8,128)(2,1)} %q_ref.1, bf16[128,1024]{1,0:T(8,128)(2,1)} %g_ref.1, bf16[2,256,1024]{2,1,0:T(8,128)(2,1)} %pad_maximum_fusion.win_ref, ...), custom_call_target="tpu_custom_call" | custom-call | tf_op jit(solution)/shard_map/pallas_call | solution.py:157
  92.5 1.9 %convert.13 = bf16[2,256,1024]{2,1,0:T(8,128)(2,1)S(1)} convert(f32[2,256,1024]{2,1,0:T(8,128)} %get-tuple-element.34) | non-fusion elementwise | flops 524288 | bytes 3145728 | tf_op jit(solution)/shard_map/convert.6
  94.4 1.3 collective-permute-start.11
  95.7 0.0 copy-done.1
  95.7 0.2 convert.14
  96.0 0.1 slice_bitcast_fusion.2
  96.1 6.4 %collective-permute-start.13 = (bf16[2,128,1024]{2,1,0:T(8,128)(2,1)S(1)}, bf16[2,128,1024]{2,1,0:T(8,128)(2,1)S(1)}, u32[]{:S(2)}, u32[]{:S(2)}) collective-permute-start(bf16[2,128,1024]{2,1,0:T(8,128)(2,1)S(1)} %get-tuple-element.38), channel_id=1, source_target_pairs={{0,16},{1,17},{2,18},{3,19},{4,20},{5,21},{6,22},{7,23},{8,24},{9,... | collective-permute-start | bytes 1572872 | tf_op jit(solution)/shard_map/ppermute | solution.py:59
  102.5 0.0 collective-permute-start.15
  102.5 1.4 %collective-permute-start.14 = (bf16[2,128,1024]{2,1,0:T(8,128)(2,1)S(1)}, bf16[2,128,1024]{2,1,0:T(8,128)(2,1)S(1)}, u32[]{:S(2)}, u32[]{:S(2)}) collective-permute-start(bf16[2,128,1024]{2,1,0:T(8,128)(2,1)S(1)} %get-tuple-element.40), channel_id=1, source_target_pairs={{0,8},{1,9},{2,10},{3,11},{4,12},{5,13},{6,14},{7,15},{8,0},{9,1},... | collective-permute-start | bytes 1572872 | tf_op jit(solution)/shard_map/ppermute | solution.py:59
  103.9 1.5 %collective-permute-start.12 = (bf16[2,64,1024]{2,1,0:T(8,128)(2,1)S(1)}, bf16[2,64,1024]{2,1,0:T(8,128)(2,1)S(1)}, u32[]{:S(2)}, u32[]{:S(2)}) collective-permute-start(bf16[2,64,1024]{2,1,0:T(8,128)(2,1)S(1)} %get-tuple-element.41), channel_id=1, source_target_pairs={{0,1},{1,2},{2,3},{3,4},{4,5},{5,6},{6,7},{7,8},{8,9},{9,10},{10,1... | collective-permute-start | bytes 786440 | tf_op jit(solution)/shard_map/ppermute | solution.py:65
  105.4 0.1 slice.106
  105.5 0.0 collective-permute-done.11
  105.5 0.1 add_dynamic-update-slice_fusion
  105.6 0.9 collective-permute-done.12
  106.5 0.1 fusion
  106.6 22.1 %collective-permute-done.13 = bf16[2,128,1024]{2,1,0:T(8,128)(2,1)S(1)} collective-permute-done((bf16[2,128,1024]{2,1,0:T(8,128)(2,1)S(1)}, bf16[2,128,1024]{2,1,0:T(8,128)(2,1)S(1)}, u32[]{:S(2)}, u32[]{:S(2)}) %collective-permute-start.13) | collective-permute-done | bytes 524320 | tf_op jit(solution)/shard_map/ppermute | solution.py:59
  128.7 0.0 collective-permute-done.15
  128.7 0.0 collective-permute-done.14
  128.7 0.3 add_convert_fusion
  129.0 0.8 slice_bitcast_fusion.3
  (14 shorter events, 0.2 us)
Async XLA Ops:
  0.6 4.3 %copy-start.7 = (s32[2]{0:T(128)S(1)}, s32[2]{0:T(128)}, u32[]{:S(2)}) copy-start(s32[2]{0:T(128)} %param.15) | copy-start | bytes 28
  4.7 29.9 %copy-start.2 = (bf16[128,1024]{1,0:T(8,128)(2,1)S(1)}, bf16[128,1024]{1,0:T(8,128)(2,1)}, u32[]{:S(2)}) copy-start(bf16[128,1024]{1,0:T(8,128)(2,1)} %param.11) | copy-start | bytes 786436
  4.7 29.9 %copy-start.3 = (bf16[128,1024]{1,0:T(8,128)(2,1)S(1)}, bf16[128,1024]{1,0:T(8,128)(2,1)}, u32[]{:S(2)}) copy-start(bf16[128,1024]{1,0:T(8,128)(2,1)} %param.12) | copy-start | bytes 786436
  4.8 1.6 %collective-permute-start.2 = (bf16[2,64,1024]{2,1,0:T(8,128)(2,1)S(1)}, bf16[2,64,1024]{2,1,0:T(8,128)(2,1)S(1)}, u32[]{:S(2)}, u32[]{:S(2)}) collective-permute-start(bf16[2,64,1024]{2,1,0:T(8,128)(2,1)S(1)} %select_bitcast_fusion.2), channel_id=1, source_target_pairs={{0,1},{1,0},{2,3},{3,2},{4,5},{5,4},{6,7},{7,6},{8,9},{9,8},{10,11... | collective-permute-start | bytes 786440 | tf_op jit(solution)/shard_map/ppermute | solution.py:42
  6.5 8.4 %collective-permute-start.3 = (bf16[2,64,1024]{2,1,0:T(8,128)(2,1)S(1)}, bf16[2,64,1024]{2,1,0:T(8,128)(2,1)S(1)}, u32[]{:S(2)}, u32[]{:S(2)}) collective-permute-start(bf16[2,64,1024]{2,1,0:T(8,128)(2,1)S(1)} %fusion.2), channel_id=1, source_target_pairs={{0,2},{1,3},{2,0},{3,1},{4,6},{5,7},{6,4},{7,5},{8,10},{9,11},{10,... | collective-permute-start | bytes 786440 | tf_op jit(solution)/shard_map/ppermute | solution.py:49
  14.9 42.1 %copy-start.8 = (s32[2,3]{1,0:T(2,128)S(1)}, s32[2,3]{1,0:T(2,128)}, u32[]{:S(2)}) copy-start(s32[2,3]{1,0:T(2,128)} %param.14) | copy-start | bytes 76
  15.0 9.1 %collective-permute-start.4 = (bf16[2,64,1024]{2,1,0:T(8,128)(2,1)S(1)}, bf16[2,64,1024]{2,1,0:T(8,128)(2,1)S(1)}, u32[]{:S(2)}, u32[]{:S(2)}) collective-permute-start(bf16[2,64,1024]{2,1,0:T(8,128)(2,1)S(1)} %broadcast_select_fusion), channel_id=1, source_target_pairs={{0,4},{1,5},{2,6},{3,7},{4,0},{5,1},{6,2},{7,3},{8,12},{9,13},{10,... | collective-permute-start | bytes 786440 | tf_op jit(solution)/shard_map/ppermute | solution.py:49
  24.2 6.9 %collective-permute-start.5 = (bf16[2,64,1024]{2,1,0:T(8,128)(2,1)S(1)}, bf16[2,64,1024]{2,1,0:T(8,128)(2,1)S(1)}, u32[]{:S(2)}, u32[]{:S(2)}) collective-permute-start(bf16[2,64,1024]{2,1,0:T(8,128)(2,1)S(1)} %broadcast_select_fusion.1), channel_id=1, source_target_pairs={{0,8},{1,9},{2,10},{3,11},{4,12},{5,13},{6,14},{7,15},{8,0},{9,1},... | collective-permute-start | bytes 786440 | tf_op jit(solution)/shard_map/ppermute | solution.py:49
  31.2 25.6 %collective-permute-start.6 = (bf16[2,64,1024]{2,1,0:T(8,128)(2,1)S(1)}, bf16[2,64,1024]{2,1,0:T(8,128)(2,1)S(1)}, u32[]{:S(2)}, u32[]{:S(2)}) collective-permute-start(bf16[2,64,1024]{2,1,0:T(8,128)(2,1)S(1)} %broadcast_select_fusion.2), channel_id=1, source_target_pairs={{0,16},{1,17},{2,18},{3,19},{4,20},{5,21},{6,22},{7,23},{8,24},{9,... | collective-permute-start | bytes 786440 | tf_op jit(solution)/shard_map/ppermute | solution.py:49
  34.6 26.1 %collective-permute-start.10 = (bf16[2,128,1024]{2,1,0:T(8,128)(2,1)S(1)}, bf16[2,128,1024]{2,1,0:T(8,128)(2,1)S(1)}, u32[]{:S(2)}, u32[]{:S(2)}) collective-permute-start(bf16[2,128,1024]{2,1,0:T(8,128)(2,1)S(1)} %pad_maximum_fusion.1), channel_id=1, source_target_pairs={{0,4},{1,5},{2,6},{3,7},{4,0},{5,1},{6,2},{7,3},{8,12},{9,13},{10,... | collective-permute-start | bytes 1572872 | tf_op jit(solution)/shard_map/ppermute | solution.py:59
  37.9 29.1 %collective-permute-start.8 = (bf16[2,128,1024]{2,1,0:T(8,128)(2,1)S(1)}, bf16[2,128,1024]{2,1,0:T(8,128)(2,1)S(1)}, u32[]{:S(2)}, u32[]{:S(2)}) collective-permute-start(bf16[2,128,1024]{2,1,0:T(8,128)(2,1)S(1)} %pad_maximum_fusion.1), channel_id=1, source_target_pairs={{0,16},{1,17},{2,18},{3,19},{4,20},{5,21},{6,22},{7,23},{8,24},{9,... | collective-permute-start | bytes 1572872 | tf_op jit(solution)/shard_map/ppermute | solution.py:59
  38.0 19.2 %collective-permute-start = (bf16[2,64,1024]{2,1,0:T(8,128)(2,1)S(1)}, bf16[2,64,1024]{2,1,0:T(8,128)(2,1)}, u32[]{:S(2)}, u32[]{:S(2)}) collective-permute-start(bf16[2,64,1024]{2,1,0:T(8,128)(2,1)S(1)} %get-tuple-element.48), channel_id=1, source_target_pairs={{0,1},{1,2},{2,3},{3,4},{4,5},{5,6},{6,7},{7,8},{8,9},{9,10},{10,1... | collective-permute-start | bytes 786440 | tf_op jit(solution)/shard_map/ppermute | solution.py:24
  40.0 17.8 %collective-permute-start.1 = (bf16[2,64,1024]{2,1,0:T(8,128)(2,1)S(1)}, bf16[2,64,1024]{2,1,0:T(8,128)(2,1)}, u32[]{:S(2)}, u32[]{:S(2)}) collective-permute-start(bf16[2,64,1024]{2,1,0:T(8,128)(2,1)S(1)} %get-tuple-element.49), channel_id=1, source_target_pairs={{1,0},{2,1},{3,2},{4,3},{5,4},{6,5},{7,6},{8,7},{9,8},{10,9},{11,1... | collective-permute-start | bytes 786440 | tf_op jit(solution)/shard_map/ppermute | solution.py:25
  57.0 2.9 %collective-permute-start.7 = (bf16[2,64,1024]{2,1,0:T(8,128)(2,1)S(1)}, bf16[2,64,1024]{2,1,0:T(8,128)(2,1)S(1)}, u32[]{:S(2)}, u32[]{:S(2)}) collective-permute-start(bf16[2,64,1024]{2,1,0:T(8,128)(2,1)S(1)} %broadcast_select_fusion.3), channel_id=1, source_target_pairs={{0,1},{1,0},{2,3},{3,2},{4,5},{5,4},{6,7},{7,6},{8,9},{9,8},{10,11... | collective-permute-start | bytes 786440 | tf_op jit(solution)/shard_map/ppermute | solution.py:52
  57.2 21.3 %collective-permute-start.9 = (bf16[2,128,1024]{2,1,0:T(8,128)(2,1)S(1)}, bf16[2,128,1024]{2,1,0:T(8,128)(2,1)S(1)}, u32[]{:S(2)}, u32[]{:S(2)}) collective-permute-start(bf16[2,128,1024]{2,1,0:T(8,128)(2,1)S(1)} %pad_maximum_fusion.1), channel_id=1, source_target_pairs={{0,8},{1,9},{2,10},{3,11},{4,12},{5,13},{6,14},{7,15},{8,0},{9,1},... | collective-permute-start | bytes 1572872 | tf_op jit(solution)/shard_map/ppermute | solution.py:59
  60.8 17.7 %copy-start.4 = (bf16[2,128,1024]{2,1,0:T(8,128)(2,1)}, bf16[2,128,1024]{2,1,0:T(8,128)(2,1)S(1)}, u32[]{:S(2)}) copy-start(bf16[2,128,1024]{2,1,0:T(8,128)(2,1)S(1)} %collective-permute-done.10.rest_2_) | copy-start | bytes 1572868
  67.0 11.5 %copy-start.5 = (bf16[2,128,1024]{2,1,0:T(8,128)(2,1)}, bf16[2,128,1024]{2,1,0:T(8,128)(2,1)S(1)}, u32[]{:S(2)}) copy-start(bf16[2,128,1024]{2,1,0:T(8,128)(2,1)S(1)} %collective-permute-done.8.rest_0_) | copy-start | bytes 1572868
  78.5 0.8 copy-start.6
  92.5 3.3 %copy-start.1 = (f32[3,2,128,1024]{3,2,1,0:T(8,128)S(1)}, f32[3,2,128,1024]{3,2,1,0:T(8,128)}, u32[]{:S(2)}) copy-start(f32[3,2,128,1024]{3,2,1,0:T(8,128)} %get-tuple-element.35) | copy-start | bytes 9437188
  94.4 11.1 %collective-permute-start.11 = (bf16[2,64,1024]{2,1,0:T(8,128)(2,1)S(1)}, bf16[2,64,1024]{2,1,0:T(8,128)(2,1)S(1)}, u32[]{:S(2)}, u32[]{:S(2)}) collective-permute-start(bf16[2,64,1024]{2,1,0:T(8,128)(2,1)S(1)} %get-tuple-element.42), channel_id=1, source_target_pairs={{1,0},{2,1},{3,2},{4,3},{5,4},{6,5},{7,6},{8,7},{9,8},{10,9},{11,1... | collective-permute-start | bytes 786440 | tf_op jit(solution)/shard_map/ppermute | solution.py:65
  96.0 9.4 %copy-start = (f32[2,256,1024]{2,1,0:T(8,128)S(1)}, f32[2,256,1024]{2,1,0:T(8,128)}, u32[]{:S(2)}) copy-start(f32[2,256,1024]{2,1,0:T(8,128)} %get-tuple-element.34) | copy-start | bytes 6291460
  96.1 32.6 %collective-permute-start.13 = (bf16[2,128,1024]{2,1,0:T(8,128)(2,1)S(1)}, bf16[2,128,1024]{2,1,0:T(8,128)(2,1)S(1)}, u32[]{:S(2)}, u32[]{:S(2)}) collective-permute-start(bf16[2,128,1024]{2,1,0:T(8,128)(2,1)S(1)} %get-tuple-element.38), channel_id=1, source_target_pairs={{0,16},{1,17},{2,18},{3,19},{4,20},{5,21},{6,22},{7,23},{8,24},{9,... | collective-permute-start | bytes 1572872 | tf_op jit(solution)/shard_map/ppermute | solution.py:59
  102.5 26.2 %collective-permute-start.15 = (bf16[2,128,1024]{2,1,0:T(8,128)(2,1)S(1)}, bf16[2,128,1024]{2,1,0:T(8,128)(2,1)S(1)}, u32[]{:S(2)}, u32[]{:S(2)}) collective-permute-start(bf16[2,128,1024]{2,1,0:T(8,128)(2,1)S(1)} %get-tuple-element.39), channel_id=1, source_target_pairs={{0,4},{1,5},{2,6},{3,7},{4,0},{5,1},{6,2},{7,3},{8,12},{9,13},{10,... | collective-permute-start | bytes 1572872 | tf_op jit(solution)/shard_map/ppermute | solution.py:59
  102.5 26.2 %collective-permute-start.14 = (bf16[2,128,1024]{2,1,0:T(8,128)(2,1)S(1)}, bf16[2,128,1024]{2,1,0:T(8,128)(2,1)S(1)}, u32[]{:S(2)}, u32[]{:S(2)}) collective-permute-start(bf16[2,128,1024]{2,1,0:T(8,128)(2,1)S(1)} %get-tuple-element.40), channel_id=1, source_target_pairs={{0,8},{1,9},{2,10},{3,11},{4,12},{5,13},{6,14},{7,15},{8,0},{9,1},... | collective-permute-start | bytes 1572872 | tf_op jit(solution)/shard_map/ppermute | solution.py:59
  103.9 2.6 %collective-permute-start.12 = (bf16[2,64,1024]{2,1,0:T(8,128)(2,1)S(1)}, bf16[2,64,1024]{2,1,0:T(8,128)(2,1)S(1)}, u32[]{:S(2)}, u32[]{:S(2)}) collective-permute-start(bf16[2,64,1024]{2,1,0:T(8,128)(2,1)S(1)} %get-tuple-element.41), channel_id=1, source_target_pairs={{0,1},{1,2},{2,3},{3,4},{4,5},{5,6},{6,7},{7,8},{8,9},{9,10},{10,1... | collective-permute-start | bytes 786440 | tf_op jit(solution)/shard_map/ppermute | solution.py:65

commit v8 on v7

--- a/solution.py
+++ b/solution.py
@@ -70,7 +70,7 @@
 
 def attend_kernel(meta_ref, q_ref, g_ref, win_ref, glob_ref, *rest):
     partner_refs = rest[:RAND]
-    att_ref, gq_ref, gwin_ref, gpart_ref = rest[RAND:]
+    att_ref, gq_ref, gwin_ref, gpart_ref, stats_ref = rest[RAND:]
     block_count = q_ref.shape[0] // BLOCK
     listed = 3 + GLOBALS + RAND
     scale_factor = HEAD_DIM ** (-0.5)
@@ -123,6 +123,11 @@
             gq = jnp.where(heads[h], gq_all[h * BLOCK : (h + 1) * BLOCK], gq)
         gk = lax.dot_general(grad_scores, qm, tn, preferred_element_type=jnp.float32)
         gv = lax.dot_general(probs_low, gm, tn, preferred_element_type=jnp.float32)
+        stacked_rows = per_pair * BLOCK
+        for t, stat in enumerate((highest, weight_total, inner)):
+            stats_ref[0, pl.ds((j * 3 + t) * stacked_rows, stacked_rows), :] = jnp.broadcast_to(
+                stat, (stacked_rows, LANES)
+            )
         att_ref[rows, :] = att.astype(att_ref.dtype)
         gq_ref[rows, :] = gq.astype(gq_ref.dtype)
         window = pl.ds(j * BLOCK, 3 * BLOCK)
@@ -138,6 +143,7 @@
     tok_rows, width = queries.shape
     framed = padded.shape[1]
     pairs = width // LANES
+    stat_rows = 3 * tok_rows * (LANES // HEAD_DIM)
     row_spec = pl.BlockSpec((tok_rows, LANES), lambda p, m: (0, p))
     win_spec = pl.BlockSpec((2, framed, LANES), lambda p, m: (0, 0, p))
     glob_spec = pl.BlockSpec((2, glob.shape[1], LANES), lambda p, m: (0, 0, p))
@@ -147,12 +153,14 @@
         row_spec,
         win_spec,
         pl.BlockSpec((RAND, 2, tok_rows, LANES), lambda p, m: (0, 0, 0, p)),
+        pl.BlockSpec((1, stat_rows, LANES), lambda p, m: (p, 0, 0)),
     ]
     out_shape = [
         jax.ShapeDtypeStruct((tok_rows, width), jnp.bfloat16),
         jax.ShapeDtypeStruct((tok_rows, width), jnp.bfloat16),
         jax.ShapeDtypeStruct((2, framed, width), jnp.float32),
         jax.ShapeDtypeStruct((RAND, 2, tok_rows, width), jnp.float32),
+        jax.ShapeDtypeStruct((pairs, stat_rows, LANES), jnp.float32),
     ]
     return pl.pallas_call(
         attend_kernel,
@@ -165,6 +173,55 @@
         out_shape=out_shape,
         compiler_params=pltpu.CompilerParams(dimension_semantics=("arbitrary",)),
     )(meta, queries, grad_out, padded, glob, *partners)
+
+
+def partner_kernel(pick_ref, qd_ref, st_ref, kv_ref, out_ref):
+    block_count = qd_ref.shape[1] // BLOCK
+    per_pair = LANES // HEAD_DIM
+    stacked_rows = per_pair * BLOCK
+    scale_factor = HEAD_DIM ** (-0.5)
+    nt = (((1,), (1,)), ((), ()))
+    tn = (((0,), (0,)), ((), ()))
+    out_ref[...] = jnp.zeros_like(out_ref)
+    lane = lax.broadcasted_iota(jnp.int32, (BLOCK, LANES), 1)
+    heads = [(lane >= h * HEAD_DIM) & (lane < (h + 1) * HEAD_DIM) for h in range(per_pair)]
+    for j in range(block_count):
+        rows = pl.ds(j * BLOCK, BLOCK)
+        q = qd_ref[0, rows, :]
+        g = qd_ref[1, rows, :]
+        qm = jnp.concatenate([jnp.where(m, q, jnp.zeros_like(q)) for m in heads], axis=0)
+        gm = jnp.concatenate([jnp.where(m, g, jnp.zeros_like(g)) for m in heads], axis=0)
+        pick = pl.ds(pl.multiple_of(pick_ref[j] * BLOCK, BLOCK), BLOCK)
+        k = kv_ref[0, pick, :]
+        v = kv_ref[1, pick, :]
+        highest, weight_total, inner = (
+            st_ref[0, pl.ds((j * 3 + t) * stacked_rows, stacked_rows), :][:, :BLOCK]
+            for t in range(3)
+        )
+        scores = lax.dot_general(qm, k, nt, preferred_element_type=jnp.float32) * scale_factor
+        probs = jnp.exp(scores - highest) / weight_total
+        probs_low = probs.astype(jnp.bfloat16)
+        grad_probs = lax.dot_general(gm, v, nt, preferred_element_type=jnp.float32)
+        grad_scores = (scale_factor * probs * (grad_probs - inner)).astype(jnp.bfloat16)
+        out_ref[0, pick, :] += lax.dot_general(grad_scores, qm, tn, preferred_element_type=jnp.float32)
+        out_ref[1, pick, :] += lax.dot_general(probs_low, gm, tn, preferred_element_type=jnp.float32)
+
+
+def partner_terms(picks, qd, stats, stacked):
+    _, tok_rows, width = stacked.shape
+    pairs, stat_rows, _ = stats.shape
+    slab_spec = pl.BlockSpec((2, tok_rows, LANES), lambda p, m: (0, 0, p))
+    return pl.pallas_call(
+        partner_kernel,
+        grid_spec=pltpu.PrefetchScalarGridSpec(
+            num_scalar_prefetch=1,
+            grid=(pairs,),
+            in_specs=[slab_spec, pl.BlockSpec((1, stat_rows, LANES), lambda p, m: (p, 0, 0)), slab_spec],
+            out_specs=slab_spec,
+        ),
+        out_shape=jax.ShapeDtypeStruct((2, tok_rows, width), jnp.float32),
+        compiler_params=pltpu.CompilerParams(dimension_semantics=("arbitrary",)),
+    )(picks, qd, stats, stacked)
 
 
 def local_body(queries, keys, values, grad_out, rand_blocks, global_ids):
@@ -180,8 +237,11 @@
     local_ids = global_ids % block_count
     spread = [top_bit - 1 - matching for matching in range(RAND)]
     partners = []
-    for bit in spread:
+    for matching, bit in enumerate(spread):
         partners.append(partner_2(stacked, "ctx", bit))
+        if matching == 0:
+            far_qd = partner_2(jnp.stack([queries, grad_out]), "ctx", bit)
+            far_picks = partner_2(rand_blocks[:, 0].astype(jnp.float32), "ctx", bit)
     candidates = [
         lax.dynamic_slice_in_dim(stacked, local_ids[global_slot] * BLOCK, BLOCK, 1)
         for global_slot in range(GLOBALS)
@@ -197,7 +257,7 @@
             (global_block < seq_blocks - 1).astype(jnp.int32),
         ]
     )
-    attended_out, grad_queries, gwin, gpart = attend(
+    attended_out, grad_queries, gwin, gpart, stats = attend(
         meta, queries, grad_out, padded, glob, partners
     )
     low = jnp.bfloat16
@@ -206,10 +266,13 @@
     own_total = gwin[:, BLOCK:-BLOCK]
     own_total = own_total.at[:, tok_rows - BLOCK :].add(from_right)
     own_total = own_total.at[:, :BLOCK].add(from_left)
-    for matching in range(RAND):
+    for matching in range(1, RAND):
         own_total = own_total + partner_2(gpart[matching].astype(low), "ctx", spread[matching]).astype(
             jnp.float32
         )
+    far_stats = partner_2(stats[:, :, 0], "ctx", spread[0])
+    far_stats = jnp.broadcast_to(far_stats[:, :, None], stats.shape)
+    own_total = own_total + partner_terms(far_picks.astype(jnp.int32), far_qd, far_stats, stacked)
     grad_keys = own_total[0].astype(jnp.bfloat16)
     grad_values = own_total[1].astype(jnp.bfloat16)
     return (attended_out, grad_queries, grad_keys, grad_values)

time: 130 us -> 137 us (1.054)
  the two profiles are of different devices: /device:TPU:2 before, /device:TPU:36 now
where the time goes in v8:
time: 137 us; the launch traced here: 136 us
  starting transfers between devices  48.8 us (36%)
  waiting for transfers between devices  40.8 us (30%)
  Pallas kernels  21.8 us (16%)
  other arithmetic  14.3 us (10%)
  local copies, waits for them, and re-layouts  8.43 us (6%)
  between operations  2.26 us (2%)
    ppermute x8, starting transfers between devices, partner_2(): lax.ppermute(array, axis, [(i, i ^ 1 << distance) for i in range(lax.axis...  28.3 us
    ppermute x4, waiting for transfers between devices, from_root(): received = lax.ppermute(carried, axis, [(i, i ^ step) for i in range(size)])  27.4 us
    pallas_call x1, Pallas kernels, attend(): pl.pallas_call(attend_kernel, grid_spec=pltpu.PrefetchScalarGridSpec(num_...  13.3 us
    ppermute x4, starting transfers between devices, from_root(): received = lax.ppermute(carried, axis, [(i, i ^ step) for i in range(size)])  8.5 us
    pallas_call x1, Pallas kernels, partner_terms(): pl.pallas_call(partner_kernel, grid_spec=pltpu.PrefetchScalarGridSpec(num...  8.42 us
    ppermute x1, waiting for transfers between devices, padded_2(): after = lax.ppermute(first, axis, down)  6.77 us
    ppermute x1, starting transfers between devices, padded_2(): after = lax.ppermute(first, axis, down)  5.75 us
    ppermute x2, waiting for transfers between devices, passed_along(): return lax.ppermute(array, axis, pairs)  4.88 us
  transfers between devices with their start and end apart: 18, of which 8 were waited for; matrix products, arithmetic and copies ran while one was open for 11% of the time, Pallas kernels for 16%

profile of v8, /device:TPU:36, one launch (start us, length us, event | category | flops | bytes accessed | tf_op | source)
XLA Modules:
  0.0 136.4 jit_solution(17027828222425129447)
XLA Ops:
  0.6 0.7 and_select_fusion
  1.4 0.6 fusion.11
  3.3 2.1 %fusion.7 = (bf16[1,2,64,1024]{3,2,0,1:T(8,128)(2,1)S(1)}, bf16[2,64,1024]{2,1,0:T(8,128)(2,1)}, bf16[2,64,1024]{2,1,0:T(8,128)(2,1)S(1)}, bf16[1,2,64,1024]{3,2,0,1:T(8,128)(2,1)S(1)}) fusion(s32[]{:T(128)S(6)} %select_n.73, bf16[1,128,1024]{2,1,0:T(8,128)(2,1)} %bitcast.41, bf16[1,128,1024]{2,1,0:T(8,128)(2,1)} %bitcast.44, s32[]{:T(128)S(6)} %select_n.74), kind=kLoop, calls=%fused_computation.28 | loop fusion | flops 2097152 | bytes 1572872 | tf_op jit(solution)/shard_map/stack | solution.py:249
  5.4 0.1 collective-permute-start.2
  5.6 1.5 %collective-permute-done.2 = bf16[2,64,1024]{2,1,0:T(8,128)(2,1)S(1)} collective-permute-done((bf16[2,64,1024]{2,1,0:T(8,128)(2,1)S(1)}, bf16[2,64,1024]{2,1,0:T(8,128)(2,1)S(1)}, u32[]{:S(2)}, u32[]{:S(2)}) %collective-permute-start.2) | collective-permute-done | bytes 262176 | tf_op jit(solution)/shard_map/ppermute | solution.py:42
  7.1 0.1 fusion.2
  7.2 1.7 %collective-permute-start.3 = (bf16[2,64,1024]{2,1,0:T(8,128)(2,1)S(1)}, bf16[2,64,1024]{2,1,0:T(8,128)(2,1)S(1)}, u32[]{:S(2)}, u32[]{:S(2)}) collective-permute-start(bf16[2,64,1024]{2,1,0:T(8,128)(2,1)S(1)} %fusion.2), channel_id=1, source_target_pairs={{0,2},{1,3},{2,0},{3,1},{4,6},{5,7},{6,4},{7,5},{8,10},{9,11},{10,... | collective-permute-start | bytes 786440 | tf_op jit(solution)/shard_map/ppermute | solution.py:49
  8.8 6.8 %collective-permute-done.3 = bf16[2,64,1024]{2,1,0:T(8,128)(2,1)S(1)} collective-permute-done((bf16[2,64,1024]{2,1,0:T(8,128)(2,1)S(1)}, bf16[2,64,1024]{2,1,0:T(8,128)(2,1)S(1)}, u32[]{:S(2)}, u32[]{:S(2)}) %collective-permute-start.3) | collective-permute-done | bytes 262176 | tf_op jit(solution)/shard_map/ppermute | solution.py:49
  15.6 0.1 broadcast_select_fusion
  15.7 3.3 %collective-permute-start.4 = (bf16[2,64,1024]{2,1,0:T(8,128)(2,1)S(1)}, bf16[2,64,1024]{2,1,0:T(8,128)(2,1)S(1)}, u32[]{:S(2)}, u32[]{:S(2)}) collective-permute-start(bf16[2,64,1024]{2,1,0:T(8,128)(2,1)S(1)} %broadcast_select_fusion), channel_id=1, source_target_pairs={{0,4},{1,5},{2,6},{3,7},{4,0},{5,1},{6,2},{7,3},{8,12},{9,13},{10,... | collective-permute-start | bytes 786440 | tf_op jit(solution)/shard_map/ppermute | solution.py:49
  19.0 5.8 %collective-permute-done.4 = bf16[2,64,1024]{2,1,0:T(8,128)(2,1)S(1)} collective-permute-done((bf16[2,64,1024]{2,1,0:T(8,128)(2,1)S(1)}, bf16[2,64,1024]{2,1,0:T(8,128)(2,1)S(1)}, u32[]{:S(2)}, u32[]{:S(2)}) %collective-permute-start.4) | collective-permute-done | bytes 262176 | tf_op jit(solution)/shard_map/ppermute | solution.py:49
  24.8 0.1 broadcast_select_fusion.1
  24.9 0.2 collective-permute-start.5
  25.1 6.5 %collective-permute-done.5 = bf16[2,64,1024]{2,1,0:T(8,128)(2,1)S(1)} collective-permute-done((bf16[2,64,1024]{2,1,0:T(8,128)(2,1)S(1)}, bf16[2,64,1024]{2,1,0:T(8,128)(2,1)S(1)}, u32[]{:S(2)}, u32[]{:S(2)}) %collective-permute-start.5) | collective-permute-done | bytes 262176 | tf_op jit(solution)/shard_map/ppermute | solution.py:49
  31.6 0.1 broadcast_select_fusion.2
  31.7 3.4 %collective-permute-start.6 = (bf16[2,64,1024]{2,1,0:T(8,128)(2,1)S(1)}, bf16[2,64,1024]{2,1,0:T(8,128)(2,1)S(1)}, u32[]{:S(2)}, u32[]{:S(2)}) collective-permute-start(bf16[2,64,1024]{2,1,0:T(8,128)(2,1)S(1)} %broadcast_select_fusion.2), channel_id=1, source_target_pairs={{0,16},{1,17},{2,18},{3,19},{4,20},{5,21},{6,22},{7,23},{8,24},{9,... | collective-permute-start | bytes 786440 | tf_op jit(solution)/shard_map/ppermute | solution.py:49
  35.1 0.1 pad_maximum_fusion.1.kv_ref
  35.1 3.3 %collective-permute-start.10 = (bf16[2,128,1024]{2,1,0:T(8,128)(2,1)S(1)}, bf16[2,128,1024]{2,1,0:T(8,128)(2,1)S(1)}, u32[]{:S(2)}, u32[]{:S(2)}) collective-permute-start(bf16[2,128,1024]{2,1,0:T(8,128)(2,1)S(1)} %pad_maximum_fusion.1.kv_ref), channel_id=1, source_target_pairs={{0,4},{1,5},{2,6},{3,7},{4,0},{5,1},{6,2},{7,3},{8,12},{9,13},{10,... | collective-permute-start | bytes 1572872 | tf_op jit(solution)/shard_map/ppermute | solution.py:59
  38.4 0.0 collective-permute-start.8
  38.4 1.9 %collective-permute-start = (bf16[2,64,1024]{2,1,0:T(8,128)(2,1)}, bf16[2,64,1024]{2,1,0:T(8,128)(2,1)}, u32[]{:S(2)}, u32[]{:S(2)}) collective-permute-start(bf16[2,64,1024]{2,1,0:T(8,128)(2,1)} %get-tuple-element.49), channel_id=1, source_target_pairs={{0,1},{1,2},{2,3},{3,4},{4,5},{5,6},{6,7},{7,8},{8,9},{9,10},{10,1... | collective-permute-start | bytes 786440 | tf_op jit(solution)/shard_map/ppermute | solution.py:24
  40.4 5.8 %collective-permute-start.1 = (bf16[2,64,1024]{2,1,0:T(8,128)(2,1)S(1)}, bf16[2,64,1024]{2,1,0:T(8,128)(2,1)}, u32[]{:S(2)}, u32[]{:S(2)}) collective-permute-start(bf16[2,64,1024]{2,1,0:T(8,128)(2,1)S(1)} %get-tuple-element.50), channel_id=1, source_target_pairs={{1,0},{2,1},{3,2},{4,3},{5,4},{6,5},{7,6},{8,7},{9,8},{10,9},{11,1... | collective-permute-start | bytes 786440 | tf_op jit(solution)/shard_map/ppermute | solution.py:25
  46.1 0.1 convert_reduce_fusion
  46.3 0.8 pad_maximum_fusion.3
  47.1 8.3 %collective-permute-done.6 = bf16[2,64,1024]{2,1,0:T(8,128)(2,1)S(1)} collective-permute-done((bf16[2,64,1024]{2,1,0:T(8,128)(2,1)S(1)}, bf16[2,64,1024]{2,1,0:T(8,128)(2,1)S(1)}, u32[]{:S(2)}, u32[]{:S(2)}) %collective-permute-start.6) | collective-permute-done | bytes 262176 | tf_op jit(solution)/shard_map/ppermute | solution.py:49
  55.4 0.7 copy-done.12
  56.1 1.0 broadcast_select_fusion.3
  57.1 0.1 collective-permute-start.7
  57.3 0.1 reshape.98
  57.3 0.0 collective-permute-done
  57.3 2.2 %collective-permute-start.9 = (bf16[2,128,1024]{2,1,0:T(8,128)(2,1)S(1)}, bf16[2,128,1024]{2,1,0:T(8,128)(2,1)S(1)}, u32[]{:S(2)}, u32[]{:S(2)}) collective-permute-start(bf16[2,128,1024]{2,1,0:T(8,128)(2,1)S(1)} %pad_maximum_fusion.1.kv_ref), channel_id=1, source_target_pairs={{0,8},{1,9},{2,10},{3,11},{4,12},{5,13},{6,14},{7,15},{8,0},{9,1},... | collective-permute-start | bytes 1572872 | tf_op jit(solution)/shard_map/ppermute | solution.py:59
  59.6 0.6 pad_add_fusion.meta_ref
  60.2 6.8 %collective-permute-done.1 = bf16[2,64,1024]{2,1,0:T(8,128)(2,1)} collective-permute-done((bf16[2,64,1024]{2,1,0:T(8,128)(2,1)S(1)}, bf16[2,64,1024]{2,1,0:T(8,128)(2,1)}, u32[]{:S(2)}, u32[]{:S(2)}) %collective-permute-start.1) | collective-permute-done | bytes 262176 | tf_op jit(solution)/shard_map/ppermute | solution.py:25
  66.9 17.7 %collective-permute-start.16 = (bf16[2,128,1024]{2,1,0:T(8,128)(2,1)}, bf16[2,128,1024]{2,1,0:T(8,128)(2,1)}, u32[]{:S(2)}, u32[]{:S(2)}) collective-permute-start(bf16[2,128,1024]{2,1,0:T(8,128)(2,1)} %pad_maximum_fusion.3), channel_id=1, source_target_pairs={{0,16},{1,17},{2,18},{3,19},{4,20},{5,21},{6,22},{7,23},{8,24},{9,... | collective-permute-start | bytes 1572872 | tf_op jit(solution)/shard_map/ppermute | solution.py:59
  84.6 2.1 %pad_maximum_fusion.win_ref = bf16[2,256,1024]{2,1,0:T(8,128)(2,1)} fusion(bf16[2,64,1024]{2,1,0:T(8,128)(2,1)} %collective-permute-done.1, bf16[1,128,1024]{2,1,0:T(8,128)(2,1)S(1)} %bitcast.46, bf16[1,128,1024]{2,1,0:T(8,128)(2,1)S(1)} %bitcast.43, bf16[2,64,1024]{2,1,0:T(8,128)(2,1)} %collective-permute-done), kind=kLoop, calls=%fused_computation.1 | loop fusion | flops 4194304 | bytes 2097152 | tf_op jit(solution)/shard_map/concatenate | solution.py:26
  86.7 0.0 collective-permute-done.7
  86.7 0.0 collective-permute-start.15
  86.8 0.8 pad_maximum_fusion.2
  87.6 0.0 collective-permute-done.9.rest_1_
  87.7 0.8 copy-done.9
  88.4 0.2 copy-done.10
  88.6 0.2 copy-done.11
  88.8 13.3 %shard_map.93 = (bf16[128,1024]{1,0:T(8,128)(2,1)}, bf16[128,1024]{1,0:T(8,128)(2,1)}, f32[2,256,1024]{2,1,0:T(8,128)}, f32[3,2,128,1024]{3,2,1,0:T(8,128)}, f32[8,768,128]{2,1,0:T(8,128)}) custom-call(s32[10]{0:T(128)} %pad_add_fusion.meta_ref, bf16[128,1024]{1,0:T(8,128)(2,1)} %q_ref.1, bf16[128,1024]{1,0:T(8,128)(2,1)} %g_ref.1, ...), custom_call_target="tpu_custom_call" | custom-call | tf_op jit(solution)/shard_map/pallas_call | solution.py:165
  102.2 1.9 %convert.12 = bf16[2,256,1024]{2,1,0:T(8,128)(2,1)S(1)} convert(f32[2,256,1024]{2,1,0:T(8,128)} %get-tuple-element.35) | non-fusion elementwise | flops 524288 | bytes 3145728 | tf_op jit(solution)/shard_map/convert.5
  104.1 0.8 fusion.10
  104.9 2.2 %collective-permute-start.11 = (bf16[2,64,1024]{2,1,0:T(8,128)(2,1)}, bf16[2,64,1024]{2,1,0:T(8,128)(2,1)S(1)}, u32[]{:S(2)}, u32[]{:S(2)}) collective-permute-start(bf16[2,64,1024]{2,1,0:T(8,128)(2,1)} %get-tuple-element.43), channel_id=1, source_target_pairs={{1,0},{2,1},{3,2},{4,3},{5,4},{6,5},{7,6},{8,7},{9,8},{10,9},{11,1... | collective-permute-start | bytes 786440 | tf_op jit(solution)/shard_map/ppermute | solution.py:65
  107.2 0.9 slice_reduce_fusion
  108.0 4.7 %collective-permute-start.17 = (f32[8,768]{1,0:T(8,128)S(1)}, f32[8,768]{1,0:T(8,128)S(1)}, u32[]{:S(2)}, u32[]{:S(2)}) collective-permute-start(f32[8,768]{1,0:T(8,128)S(1)} %slice_reduce_fusion), channel_id=1, source_target_pairs={{0,16},{1,17},{2,18},{3,19},{4,20},{5,21},{6,22},{7,23},{8,24},{9,... | collective-permute-start | bytes 73736 | tf_op jit(solution)/shard_map/ppermute | solution.py:59
  112.8 0.2 convert.13
  113.0 1.1 slice_bitcast_fusion.1
  114.1 0.4 collective-permute-start.13
  114.5 0.0 collective-permute-done.16.qd_ref
  114.5 1.9 %collective-permute-start.12 = (bf16[2,64,1024]{2,1,0:T(8,128)(2,1)}, bf16[2,64,1024]{2,1,0:T(8,128)(2,1)}, u32[]{:S(2)}, u32[]{:S(2)}) collective-permute-start(bf16[2,64,1024]{2,1,0:T(8,128)(2,1)} %get-tuple-element.42), channel_id=1, source_target_pairs={{0,1},{1,2},{2,3},{3,4},{4,5},{5,6},{6,7},{7,8},{8,9},{9,10},{10,1... | collective-permute-start | bytes 786440 | tf_op jit(solution)/shard_map/ppermute | solution.py:65
  116.4 0.6 convert_element_type.55.pick_ref
  117.0 0.1 slice.108
  117.1 0.3 collective-permute-done.17
  117.4 2.1 %broadcast_in_dim.39.st_ref = f32[8,768,128]{2,1,0:T(8,128)} broadcast(f32[8,768]{1,0:T(8,128)S(1)} %collective-permute-done.17), dimensions={0,1} | broadcast | bytes 3170304 | tf_op jit(solution)/shard_map/broadcast_in_dim | solution.py:274
  119.5 8.4 %shard_map.94 = f32[2,128,1024]{2,1,0:T(8,128)} custom-call(s32[2]{0:T(128)} %convert_element_type.55.pick_ref, bf16[2,128,1024]{2,1,0:T(8,128)(2,1)} %collective-permute-done.16.qd_ref, f32[8,768,128]{2,1,0:T(8,128)} %broadcast_in_dim.39.st_ref, bf16[2,128,1024]{2,1,0:T(8,128)(2,1)} %copy-done.6), custom_call_target="tpu_custom_call" | custom-call | tf_op jit(solution)/shard_map/pallas_call | solution.py:214
  127.9 0.0 collective-permute-done.11
  127.9 0.1 add_dynamic-update-slice_fusion
  128.0 4.9 %collective-permute-done.12 = bf16[2,64,1024]{2,1,0:T(8,128)(2,1)} collective-permute-done((bf16[2,64,1024]{2,1,0:T(8,128)(2,1)}, bf16[2,64,1024]{2,1,0:T(8,128)(2,1)}, u32[]{:S(2)}, u32[]{:S(2)}) %collective-permute-start.12) | collective-permute-done | bytes 262176 | tf_op jit(solution)/shard_map/ppermute | solution.py:65
  132.9 1.1 fusion
  134.0 0.0 collective-permute-done.13
  134.0 1.5 %add_convert_fusion = bf16[2,128,1024]{2,1,0:T(8,128)(2,1)S(1)} fusion(f32[2,128,1024]{2,1,0:T(8,128)S(1)} %copy-done.1, bf16[2,128,1024]{2,1,0:T(8,128)(2,1)} %collective-permute-done.14, f32[2,128,1024]{2,1,0:T(8,128)S(1)} %fusion, bf16[2,128,1024]{2,1,0:T(8,128)(2,1)} %collective-permute-done.13), kind=kLoop, calls=%fused_computation.2 | loop fusion | flops 1572864 | bytes 3670016 | tf_op jit(solution)/shard_map/convert.1
  135.5 0.8 slice_bitcast_fusion.2
  (36 shorter events, 0.2 us)
Async XLA Ops:
  0.6 4.9 %copy-start.13 = (s32[2]{0:T(128)S(1)}, s32[2]{0:T(128)}, u32[]{:S(2)}) copy-start(s32[2]{0:T(128)} %param.15) | copy-start | bytes 28
  5.4 29.7 %copy-start.4 = (bf16[128,1024]{1,0:T(8,128)(2,1)S(1)}, bf16[128,1024]{1,0:T(8,128)(2,1)}, u32[]{:S(2)}) copy-start(bf16[128,1024]{1,0:T(8,128)(2,1)} %param.11) | copy-start | bytes 786436
  5.4 29.7 %copy-start.5 = (bf16[128,1024]{1,0:T(8,128)(2,1)S(1)}, bf16[128,1024]{1,0:T(8,128)(2,1)}, u32[]{:S(2)}) copy-start(bf16[128,1024]{1,0:T(8,128)(2,1)} %param.12) | copy-start | bytes 786436
  5.4 1.6 %collective-permute-start.2 = (bf16[2,64,1024]{2,1,0:T(8,128)(2,1)S(1)}, bf16[2,64,1024]{2,1,0:T(8,128)(2,1)S(1)}, u32[]{:S(2)}, u32[]{:S(2)}) collective-permute-start(bf16[2,64,1024]{2,1,0:T(8,128)(2,1)S(1)} %select_bitcast_fusion.2), channel_id=1, source_target_pairs={{0,1},{1,0},{2,3},{3,2},{4,5},{5,4},{6,7},{7,6},{8,9},{9,8},{10,11... | collective-permute-start | bytes 786440 | tf_op jit(solution)/shard_map/ppermute | solution.py:42
  7.0 39.1 %copy-start.14 = (s32[2,3]{1,0:T(2,128)S(1)}, s32[2,3]{1,0:T(2,128)}, u32[]{:S(2)}) copy-start(s32[2,3]{1,0:T(2,128)} %param.14) | copy-start | bytes 76
  7.1 39.2 %copy-start.7 = (bf16[128,1024]{1,0:T(8,128)(2,1)S(1)}, bf16[128,1024]{1,0:T(8,128)(2,1)}, u32[]{:S(2)}) copy-start(bf16[128,1024]{1,0:T(8,128)(2,1)} %q_ref.1) | copy-start | bytes 786436
  7.1 39.2 %copy-start.8 = (bf16[128,1024]{1,0:T(8,128)(2,1)S(1)}, bf16[128,1024]{1,0:T(8,128)(2,1)}, u32[]{:S(2)}) copy-start(bf16[128,1024]{1,0:T(8,128)(2,1)} %g_ref.1) | copy-start | bytes 786436
  7.2 8.4 %collective-permute-start.3 = (bf16[2,64,1024]{2,1,0:T(8,128)(2,1)S(1)}, bf16[2,64,1024]{2,1,0:T(8,128)(2,1)S(1)}, u32[]{:S(2)}, u32[]{:S(2)}) collective-permute-start(bf16[2,64,1024]{2,1,0:T(8,128)(2,1)S(1)} %fusion.2), channel_id=1, source_target_pairs={{0,2},{1,3},{2,0},{3,1},{4,6},{5,7},{6,4},{7,5},{8,10},{9,11},{10,... | collective-permute-start | bytes 786440 | tf_op jit(solution)/shard_map/ppermute | solution.py:49
  15.7 9.1 %collective-permute-start.4 = (bf16[2,64,1024]{2,1,0:T(8,128)(2,1)S(1)}, bf16[2,64,1024]{2,1,0:T(8,128)(2,1)S(1)}, u32[]{:S(2)}, u32[]{:S(2)}) collective-permute-start(bf16[2,64,1024]{2,1,0:T(8,128)(2,1)S(1)} %broadcast_select_fusion), channel_id=1, source_target_pairs={{0,4},{1,5},{2,6},{3,7},{4,0},{5,1},{6,2},{7,3},{8,12},{9,13},{10,... | collective-permute-start | bytes 786440 | tf_op jit(solution)/shard_map/ppermute | solution.py:49
  24.9 6.7 %collective-permute-start.5 = (bf16[2,64,1024]{2,1,0:T(8,128)(2,1)S(1)}, bf16[2,64,1024]{2,1,0:T(8,128)(2,1)S(1)}, u32[]{:S(2)}, u32[]{:S(2)}) collective-permute-start(bf16[2,64,1024]{2,1,0:T(8,128)(2,1)S(1)} %broadcast_select_fusion.1), channel_id=1, source_target_pairs={{0,8},{1,9},{2,10},{3,11},{4,12},{5,13},{6,14},{7,15},{8,0},{9,1},... | collective-permute-start | bytes 786440 | tf_op jit(solution)/shard_map/ppermute | solution.py:49
  31.7 23.7 %collective-permute-start.6 = (bf16[2,64,1024]{2,1,0:T(8,128)(2,1)S(1)}, bf16[2,64,1024]{2,1,0:T(8,128)(2,1)S(1)}, u32[]{:S(2)}, u32[]{:S(2)}) collective-permute-start(bf16[2,64,1024]{2,1,0:T(8,128)(2,1)S(1)} %broadcast_select_fusion.2), channel_id=1, source_target_pairs={{0,16},{1,17},{2,18},{3,19},{4,20},{5,21},{6,22},{7,23},{8,24},{9,... | collective-permute-start | bytes 786440 | tf_op jit(solution)/shard_map/ppermute | solution.py:49
  35.1 51.7 %copy-start.6 = (bf16[2,128,1024]{2,1,0:T(8,128)(2,1)}, bf16[2,128,1024]{2,1,0:T(8,128)(2,1)S(1)}, u32[]{:S(2)}) copy-start(bf16[2,128,1024]{2,1,0:T(8,128)(2,1)S(1)} %pad_maximum_fusion.1.kv_ref) | copy-start | bytes 1572868
  35.1 52.5 %collective-permute-start.10 = (bf16[2,128,1024]{2,1,0:T(8,128)(2,1)S(1)}, bf16[2,128,1024]{2,1,0:T(8,128)(2,1)S(1)}, u32[]{:S(2)}, u32[]{:S(2)}) collective-permute-start(bf16[2,128,1024]{2,1,0:T(8,128)(2,1)S(1)} %pad_maximum_fusion.1.kv_ref), channel_id=1, source_target_pairs={{0,4},{1,5},{2,6},{3,7},{4,0},{5,1},{6,2},{7,3},{8,12},{9,13},{10,... | collective-permute-start | bytes 1572872 | tf_op jit(solution)/shard_map/ppermute | solution.py:59
  38.4 49.2 %collective-permute-start.8 = (bf16[2,128,1024]{2,1,0:T(8,128)(2,1)S(1)}, bf16[2,128,1024]{2,1,0:T(8,128)(2,1)S(1)}, u32[]{:S(2)}, u32[]{:S(2)}) collective-permute-start(bf16[2,128,1024]{2,1,0:T(8,128)(2,1)S(1)} %pad_maximum_fusion.1.kv_ref), channel_id=1, source_target_pairs={{0,16},{1,17},{2,18},{3,19},{4,20},{5,21},{6,22},{7,23},{8,24},{9,... | collective-permute-start | bytes 1572872 | tf_op jit(solution)/shard_map/ppermute | solution.py:59
  38.4 18.9 %collective-permute-start = (bf16[2,64,1024]{2,1,0:T(8,128)(2,1)}, bf16[2,64,1024]{2,1,0:T(8,128)(2,1)}, u32[]{:S(2)}, u32[]{:S(2)}) collective-permute-start(bf16[2,64,1024]{2,1,0:T(8,128)(2,1)} %get-tuple-element.49), channel_id=1, source_target_pairs={{0,1},{1,2},{2,3},{3,4},{4,5},{5,6},{6,7},{7,8},{8,9},{9,10},{10,1... | collective-permute-start | bytes 786440 | tf_op jit(solution)/shard_map/ppermute | solution.py:24
  40.4 26.6 %collective-permute-start.1 = (bf16[2,64,1024]{2,1,0:T(8,128)(2,1)S(1)}, bf16[2,64,1024]{2,1,0:T(8,128)(2,1)}, u32[]{:S(2)}, u32[]{:S(2)}) collective-permute-start(bf16[2,64,1024]{2,1,0:T(8,128)(2,1)S(1)} %get-tuple-element.50), channel_id=1, source_target_pairs={{1,0},{2,1},{3,2},{4,3},{5,4},{6,5},{7,6},{8,7},{9,8},{10,9},{11,1... | collective-permute-start | bytes 786440 | tf_op jit(solution)/shard_map/ppermute | solution.py:25
  55.4 0.7 copy-start.12
  57.1 29.6 %collective-permute-start.7 = (bf16[2,64,1024]{2,1,0:T(8,128)(2,1)S(1)}, bf16[2,64,1024]{2,1,0:T(8,128)(2,1)S(1)}, u32[]{:S(2)}, u32[]{:S(2)}) collective-permute-start(bf16[2,64,1024]{2,1,0:T(8,128)(2,1)S(1)} %broadcast_select_fusion.3), channel_id=1, source_target_pairs={{0,1},{1,0},{2,3},{3,2},{4,5},{5,4},{6,7},{7,6},{8,9},{9,8},{10,11... | collective-permute-start | bytes 786440 | tf_op jit(solution)/shard_map/ppermute | solution.py:52
  57.3 30.3 %collective-permute-start.9 = (bf16[2,128,1024]{2,1,0:T(8,128)(2,1)S(1)}, bf16[2,128,1024]{2,1,0:T(8,128)(2,1)S(1)}, u32[]{:S(2)}, u32[]{:S(2)}) collective-permute-start(bf16[2,128,1024]{2,1,0:T(8,128)(2,1)S(1)} %pad_maximum_fusion.1.kv_ref), channel_id=1, source_target_pairs={{0,8},{1,9},{2,10},{3,11},{4,12},{5,13},{6,14},{7,15},{8,0},{9,1},... | collective-permute-start | bytes 1572872 | tf_op jit(solution)/shard_map/ppermute | solution.py:59
  66.9 47.6 %collective-permute-start.16 = (bf16[2,128,1024]{2,1,0:T(8,128)(2,1)}, bf16[2,128,1024]{2,1,0:T(8,128)(2,1)}, u32[]{:S(2)}, u32[]{:S(2)}) collective-permute-start(bf16[2,128,1024]{2,1,0:T(8,128)(2,1)} %pad_maximum_fusion.3), channel_id=1, source_target_pairs={{0,16},{1,17},{2,18},{3,19},{4,20},{5,21},{6,22},{7,23},{8,24},{9,... | collective-permute-start | bytes 1572872 | tf_op jit(solution)/shard_map/ppermute | solution.py:59
  86.7 27.8 %collective-permute-start.15 = (f32[2]{0:T(128)S(1)}, f32[2]{0:T(128)S(1)}, u32[]{:S(2)}, u32[]{:S(2)}) collective-permute-start(f32[2]{0:T(128)S(1)} %convert_reduce_fusion), channel_id=1, source_target_pairs={{0,16},{1,17},{2,18},{3,19},{4,20},{5,21},{6,22},{7,23},{8,24},{9,... | collective-permute-start | bytes 32 | tf_op jit(solution)/shard_map/ppermute | solution.py:59
  87.6 0.8 copy-start.9
  87.6 1.0 copy-start.10
  87.6 1.2 copy-start.11
  102.2 5.0 %copy-start.3 = (f32[8,768,128]{2,1,0:T(8,128)S(1)}, f32[8,768,128]{2,1,0:T(8,128)}, u32[]{:S(2)}) copy-start(f32[8,768,128]{2,1,0:T(8,128)} %get-tuple-element.37) | copy-start | bytes 9437188
  104.1 8.7 %copy-start.2 = (f32[3,2,128,1024]{3,2,1,0:T(8,128)S(1)}, f32[3,2,128,1024]{3,2,1,0:T(8,128)}, u32[]{:S(2)}) copy-start(f32[3,2,128,1024]{3,2,1,0:T(8,128)} %get-tuple-element.36) | copy-start | bytes 9437188
  104.9 23.0 %collective-permute-start.11 = (bf16[2,64,1024]{2,1,0:T(8,128)(2,1)}, bf16[2,64,1024]{2,1,0:T(8,128)(2,1)S(1)}, u32[]{:S(2)}, u32[]{:S(2)}) collective-permute-start(bf16[2,64,1024]{2,1,0:T(8,128)(2,1)} %get-tuple-element.43), channel_id=1, source_target_pairs={{1,0},{2,1},{3,2},{4,3},{5,4},{6,5},{7,6},{8,7},{9,8},{10,9},{11,1... | collective-permute-start | bytes 786440 | tf_op jit(solution)/shard_map/ppermute | solution.py:65
  108.0 9.4 %collective-permute-start.17 = (f32[8,768]{1,0:T(8,128)S(1)}, f32[8,768]{1,0:T(8,128)S(1)}, u32[]{:S(2)}, u32[]{:S(2)}) collective-permute-start(f32[8,768]{1,0:T(8,128)S(1)} %slice_reduce_fusion), channel_id=1, source_target_pairs={{0,16},{1,17},{2,18},{3,19},{4,20},{5,21},{6,22},{7,23},{8,24},{9,... | collective-permute-start | bytes 73736 | tf_op jit(solution)/shard_map/ppermute | solution.py:59
  113.0 4.0 %copy-start = (f32[2,256,1024]{2,1,0:T(8,128)S(1)}, f32[2,256,1024]{2,1,0:T(8,128)}, u32[]{:S(2)}) copy-start(f32[2,256,1024]{2,1,0:T(8,128)} %get-tuple-element.35) | copy-start | bytes 6291460
  114.1 19.8 %collective-permute-start.13 = (bf16[2,128,1024]{2,1,0:T(8,128)(2,1)}, bf16[2,128,1024]{2,1,0:T(8,128)(2,1)}, u32[]{:S(2)}, u32[]{:S(2)}) collective-permute-start(bf16[2,128,1024]{2,1,0:T(8,128)(2,1)} %get-tuple-element.40), channel_id=1, source_target_pairs={{0,8},{1,9},{2,10},{3,11},{4,12},{5,13},{6,14},{7,15},{8,0},{9,1},... | collective-permute-start | bytes 1572872 | tf_op jit(solution)/shard_map/ppermute | solution.py:59
  114.5 19.5 %collective-permute-start.14 = (bf16[2,128,1024]{2,1,0:T(8,128)(2,1)}, bf16[2,128,1024]{2,1,0:T(8,128)(2,1)}, u32[]{:S(2)}, u32[]{:S(2)}) collective-permute-start(bf16[2,128,1024]{2,1,0:T(8,128)(2,1)} %get-tuple-element.41), channel_id=1, source_target_pairs={{0,4},{1,5},{2,6},{3,7},{4,0},{5,1},{6,2},{7,3},{8,12},{9,13},{10,... | collective-permute-start | bytes 1572872 | tf_op jit(solution)/shard_map/ppermute | solution.py:59
  114.5 18.4 %collective-permute-start.12 = (bf16[2,64,1024]{2,1,0:T(8,128)(2,1)}, bf16[2,64,1024]{2,1,0:T(8,128)(2,1)}, u32[]{:S(2)}, u32[]{:S(2)}) collective-permute-start(bf16[2,64,1024]{2,1,0:T(8,128)(2,1)} %get-tuple-element.42), channel_id=1, source_target_pairs={{0,1},{1,2},{2,3},{3,4},{4,5},{5,6},{6,7},{7,8},{8,9},{9,10},{10,1... | collective-permute-start | bytes 786440 | tf_op jit(solution)/shard_map/ppermute | solution.py:65
  127.9 6.0 %copy-start.1 = (f32[2,128,1024]{2,1,0:T(8,128)S(1)}, f32[2,128,1024]{2,1,0:T(8,128)}, u32[]{:S(2)}) copy-start(f32[2,128,1024]{2,1,0:T(8,128)} %shard_map.94) | copy-start | bytes 3145732

commit v9 on v8

--- a/solution.py
+++ b/solution.py
@@ -42,7 +42,8 @@
     received = lax.ppermute(theirs, axis, sibling)
     carried = jnp.where(holds(position ^ 1), received, mine)
     mask = mask | 1
-    for level in range(1, size.bit_length() - 1):
+    levels = list(range(1, size.bit_length() - 1))
+    for level in levels:
         step = 1 << level
         if mask & step:
             continue
@@ -125,9 +126,8 @@
         gv = lax.dot_general(probs_low, gm, tn, preferred_element_type=jnp.float32)
         stacked_rows = per_pair * BLOCK
         for t, stat in enumerate((highest, weight_total, inner)):
-            stats_ref[0, pl.ds((j * 3 + t) * stacked_rows, stacked_rows), :] = jnp.broadcast_to(
-                stat, (stacked_rows, LANES)
-            )
+            spread_out = jnp.transpose(jnp.broadcast_to(stat, (stacked_rows, stacked_rows)))
+            stats_ref[0, pl.ds(j * 3 + t, 1), :] = spread_out[:1]
         att_ref[rows, :] = att.astype(att_ref.dtype)
         gq_ref[rows, :] = gq.astype(gq_ref.dtype)
         window = pl.ds(j * BLOCK, 3 * BLOCK)
@@ -143,7 +143,7 @@
     tok_rows, width = queries.shape
     framed = padded.shape[1]
     pairs = width // LANES
-    stat_rows = 3 * tok_rows * (LANES // HEAD_DIM)
+    stat_rows = 3 * (tok_rows // BLOCK)
     row_spec = pl.BlockSpec((tok_rows, LANES), lambda p, m: (0, p))
     win_spec = pl.BlockSpec((2, framed, LANES), lambda p, m: (0, 0, p))
     glob_spec = pl.BlockSpec((2, glob.shape[1], LANES), lambda p, m: (0, 0, p))
@@ -195,7 +195,9 @@
         k = kv_ref[0, pick, :]
         v = kv_ref[1, pick, :]
         highest, weight_total, inner = (
-            st_ref[0, pl.ds((j * 3 + t) * stacked_rows, stacked_rows), :][:, :BLOCK]
+            jnp.transpose(
+                jnp.broadcast_to(st_ref[0, pl.ds(j * 3 + t, 1), :], (stacked_rows, stacked_rows))
+            )[:, :BLOCK]
             for t in range(3)
         )
         scores = lax.dot_general(qm, k, nt, preferred_element_type=jnp.float32) * scale_factor
@@ -237,11 +239,10 @@
     local_ids = global_ids % block_count
     spread = [top_bit - 1 - matching for matching in range(RAND)]
     partners = []
-    for matching, bit in enumerate(spread):
+    for bit in spread:
         partners.append(partner_2(stacked, "ctx", bit))
-        if matching == 0:
-            far_qd = partner_2(jnp.stack([queries, grad_out]), "ctx", bit)
-            far_picks = partner_2(rand_blocks[:, 0].astype(jnp.float32), "ctx", bit)
+    far_qd = partner_2(jnp.stack([queries, grad_out]), "ctx", spread[0])
+    far_picks = partner_2(rand_blocks[:, 0].astype(jnp.float32), "ctx", spread[0])
     candidates = [
         lax.dynamic_slice_in_dim(stacked, local_ids[global_slot] * BLOCK, BLOCK, 1)
         for global_slot in range(GLOBALS)
@@ -270,8 +271,7 @@
         own_total = own_total + partner_2(gpart[matching].astype(low), "ctx", spread[matching]).astype(
             jnp.float32
         )
-    far_stats = partner_2(stats[:, :, 0], "ctx", spread[0])
-    far_stats = jnp.broadcast_to(far_stats[:, :, None], stats.shape)
+    far_stats = partner_2(stats, "ctx", spread[0])
     own_total = own_total + partner_terms(far_picks.astype(jnp.int32), far_qd, far_stats, stacked)
     grad_keys = own_total[0].astype(jnp.bfloat16)
     grad_values = own_total[1].astype(jnp.bfloat16)

time: 137 us -> 136 us (level)
  the two profiles are of different devices: /device:TPU:36 before, /device:TPU:38 now
where the time goes in v9:
time: 136 us
  starting transfers between devices  48.6 us (36%)
  waiting for transfers between devices  42.9 us (32%)
  Pallas kernels  21.1 us (16%)
  other arithmetic  14.3 us (11%)
  local copies, waits for them, and re-layouts  6.43 us (5%)
  between operations  2.26 us (2%)
    ppermute x8, starting transfers between devices, partner_2(): lax.ppermute(array, axis, [(i, i ^ 1 << distance) for i in range(lax.axis...  28.2 us
    ppermute x4, waiting for transfers between devices, from_root(): received = lax.ppermute(carried, axis, [(i, i ^ step) for i in range(size)])  27.4 us
    pallas_call x1, Pallas kernels, attend(): pl.pallas_call(attend_kernel, grid_spec=pltpu.PrefetchScalarGridSpec(num_...  13.2 us
    ppermute x4, starting transfers between devices, from_root(): received = lax.ppermute(carried, axis, [(i, i ^ step) for i in range(size)])  8.5 us
    pallas_call x1, Pallas kernels, partner_terms(): pl.pallas_call(partner_kernel, grid_spec=pltpu.PrefetchScalarGridSpec(num...  7.9 us
    ppermute x1, waiting for transfers between devices, padded_2(): after = lax.ppermute(first, axis, down)  6.77 us
    ppermute x1, starting transfers between devices, padded_2(): after = lax.ppermute(first, axis, down)  5.75 us
    ppermute x2, waiting for transfers between devices, passed_along(): return lax.ppermute(array, axis, pairs)  5.69 us
  transfers between devices with their start and end apart: 18, of which 8 were waited for; matrix products, arithmetic and copies ran while one was open for 9% of the time, Pallas kernels for 16%

profile of v9, /device:TPU:38, one launch (start us, length us, event | category | flops | bytes accessed | tf_op | source)
XLA Modules:
  0.0 135.6 jit_solution(4457183418480735541)
XLA Ops:
  0.6 0.7 and_select_fusion
  1.4 0.6 fusion.11
  3.3 2.1 %fusion.7 = (bf16[1,2,64,1024]{3,2,0,1:T(8,128)(2,1)S(1)}, bf16[2,64,1024]{2,1,0:T(8,128)(2,1)}, bf16[2,64,1024]{2,1,0:T(8,128)(2,1)S(1)}, bf16[1,2,64,1024]{3,2,0,1:T(8,128)(2,1)S(1)}) fusion(s32[]{:T(128)S(6)} %select_n.73, bf16[1,128,1024]{2,1,0:T(8,128)(2,1)} %bitcast.41, bf16[1,128,1024]{2,1,0:T(8,128)(2,1)} %bitcast.44, s32[]{:T(128)S(6)} %select_n.74), kind=kLoop, calls=%fused_computation.27 | loop fusion | flops 2097152 | bytes 1572872 | tf_op jit(solution)/shard_map/stack | solution.py:250
  5.4 0.1 collective-permute-start.2
  5.6 1.5 %collective-permute-done.2 = bf16[2,64,1024]{2,1,0:T(8,128)(2,1)S(1)} collective-permute-done((bf16[2,64,1024]{2,1,0:T(8,128)(2,1)S(1)}, bf16[2,64,1024]{2,1,0:T(8,128)(2,1)S(1)}, u32[]{:S(2)}, u32[]{:S(2)}) %collective-permute-start.2) | collective-permute-done | bytes 262176 | tf_op jit(solution)/shard_map/ppermute | solution.py:42
  7.1 0.1 fusion.2
  7.2 1.7 %collective-permute-start.3 = (bf16[2,64,1024]{2,1,0:T(8,128)(2,1)S(1)}, bf16[2,64,1024]{2,1,0:T(8,128)(2,1)S(1)}, u32[]{:S(2)}, u32[]{:S(2)}) collective-permute-start(bf16[2,64,1024]{2,1,0:T(8,128)(2,1)S(1)} %fusion.2), channel_id=1, source_target_pairs={{0,2},{1,3},{2,0},{3,1},{4,6},{5,7},{6,4},{7,5},{8,10},{9,11},{10,... | collective-permute-start | bytes 786440 | tf_op jit(solution)/shard_map/ppermute | solution.py:50
  8.8 6.8 %collective-permute-done.3 = bf16[2,64,1024]{2,1,0:T(8,128)(2,1)S(1)} collective-permute-done((bf16[2,64,1024]{2,1,0:T(8,128)(2,1)S(1)}, bf16[2,64,1024]{2,1,0:T(8,128)(2,1)S(1)}, u32[]{:S(2)}, u32[]{:S(2)}) %collective-permute-start.3) | collective-permute-done | bytes 262176 | tf_op jit(solution)/shard_map/ppermute | solution.py:50
  15.6 0.1 broadcast_select_fusion
  15.7 3.3 %collective-permute-start.4 = (bf16[2,64,1024]{2,1,0:T(8,128)(2,1)S(1)}, bf16[2,64,1024]{2,1,0:T(8,128)(2,1)S(1)}, u32[]{:S(2)}, u32[]{:S(2)}) collective-permute-start(bf16[2,64,1024]{2,1,0:T(8,128)(2,1)S(1)} %broadcast_select_fusion), channel_id=1, source_target_pairs={{0,4},{1,5},{2,6},{3,7},{4,0},{5,1},{6,2},{7,3},{8,12},{9,13},{10,... | collective-permute-start | bytes 786440 | tf_op jit(solution)/shard_map/ppermute | solution.py:50
  19.0 5.8 %collective-permute-done.4 = bf16[2,64,1024]{2,1,0:T(8,128)(2,1)S(1)} collective-permute-done((bf16[2,64,1024]{2,1,0:T(8,128)(2,1)S(1)}, bf16[2,64,1024]{2,1,0:T(8,128)(2,1)S(1)}, u32[]{:S(2)}, u32[]{:S(2)}) %collective-permute-start.4) | collective-permute-done | bytes 262176 | tf_op jit(solution)/shard_map/ppermute | solution.py:50
  24.8 0.1 broadcast_select_fusion.1
  24.9 0.2 collective-permute-start.5
  25.1 6.5 %collective-permute-done.5 = bf16[2,64,1024]{2,1,0:T(8,128)(2,1)S(1)} collective-permute-done((bf16[2,64,1024]{2,1,0:T(8,128)(2,1)S(1)}, bf16[2,64,1024]{2,1,0:T(8,128)(2,1)S(1)}, u32[]{:S(2)}, u32[]{:S(2)}) %collective-permute-start.5) | collective-permute-done | bytes 262176 | tf_op jit(solution)/shard_map/ppermute | solution.py:50
  31.6 0.1 broadcast_select_fusion.2
  31.7 3.4 %collective-permute-start.6 = (bf16[2,64,1024]{2,1,0:T(8,128)(2,1)S(1)}, bf16[2,64,1024]{2,1,0:T(8,128)(2,1)S(1)}, u32[]{:S(2)}, u32[]{:S(2)}) collective-permute-start(bf16[2,64,1024]{2,1,0:T(8,128)(2,1)S(1)} %broadcast_select_fusion.2), channel_id=1, source_target_pairs={{0,16},{1,17},{2,18},{3,19},{4,20},{5,21},{6,22},{7,23},{8,24},{9,... | collective-permute-start | bytes 786440 | tf_op jit(solution)/shard_map/ppermute | solution.py:50
  35.1 0.1 pad_maximum_fusion.1.kv_ref
  35.1 3.3 %collective-permute-start.10 = (bf16[2,128,1024]{2,1,0:T(8,128)(2,1)S(1)}, bf16[2,128,1024]{2,1,0:T(8,128)(2,1)S(1)}, u32[]{:S(2)}, u32[]{:S(2)}) collective-permute-start(bf16[2,128,1024]{2,1,0:T(8,128)(2,1)S(1)} %pad_maximum_fusion.1.kv_ref), channel_id=1, source_target_pairs={{0,4},{1,5},{2,6},{3,7},{4,0},{5,1},{6,2},{7,3},{8,12},{9,13},{10,... | collective-permute-start | bytes 1572872 | tf_op jit(solution)/shard_map/ppermute | solution.py:60
  38.4 0.0 collective-permute-start.8
  38.4 1.9 %collective-permute-start = (bf16[2,64,1024]{2,1,0:T(8,128)(2,1)}, bf16[2,64,1024]{2,1,0:T(8,128)(2,1)}, u32[]{:S(2)}, u32[]{:S(2)}) collective-permute-start(bf16[2,64,1024]{2,1,0:T(8,128)(2,1)} %get-tuple-element.49), channel_id=1, source_target_pairs={{0,1},{1,2},{2,3},{3,4},{4,5},{5,6},{6,7},{7,8},{8,9},{9,10},{10,1... | collective-permute-start | bytes 786440 | tf_op jit(solution)/shard_map/ppermute | solution.py:24
  40.4 5.8 %collective-permute-start.1 = (bf16[2,64,1024]{2,1,0:T(8,128)(2,1)S(1)}, bf16[2,64,1024]{2,1,0:T(8,128)(2,1)}, u32[]{:S(2)}, u32[]{:S(2)}) collective-permute-start(bf16[2,64,1024]{2,1,0:T(8,128)(2,1)S(1)} %get-tuple-element.50), channel_id=1, source_target_pairs={{1,0},{2,1},{3,2},{4,3},{5,4},{6,5},{7,6},{8,7},{9,8},{10,9},{11,1... | collective-permute-start | bytes 786440 | tf_op jit(solution)/shard_map/ppermute | solution.py:25
  46.1 0.1 convert_reduce_fusion
  46.3 0.9 pad_maximum_fusion.3
  47.1 8.3 %collective-permute-done.6 = bf16[2,64,1024]{2,1,0:T(8,128)(2,1)S(1)} collective-permute-done((bf16[2,64,1024]{2,1,0:T(8,128)(2,1)S(1)}, bf16[2,64,1024]{2,1,0:T(8,128)(2,1)S(1)}, u32[]{:S(2)}, u32[]{:S(2)}) %collective-permute-start.6) | collective-permute-done | bytes 262176 | tf_op jit(solution)/shard_map/ppermute | solution.py:50
  55.4 0.7 copy-done.11
  56.1 1.0 broadcast_select_fusion.3
  57.1 0.1 collective-permute-start.7
  57.3 0.1 reshape.97
  57.3 0.0 collective-permute-done
  57.3 2.2 %collective-permute-start.9 = (bf16[2,128,1024]{2,1,0:T(8,128)(2,1)S(1)}, bf16[2,128,1024]{2,1,0:T(8,128)(2,1)S(1)}, u32[]{:S(2)}, u32[]{:S(2)}) collective-permute-start(bf16[2,128,1024]{2,1,0:T(8,128)(2,1)S(1)} %pad_maximum_fusion.1.kv_ref), channel_id=1, source_target_pairs={{0,8},{1,9},{2,10},{3,11},{4,12},{5,13},{6,14},{7,15},{8,0},{9,1},... | collective-permute-start | bytes 1572872 | tf_op jit(solution)/shard_map/ppermute | solution.py:60
  59.6 0.6 pad_add_fusion.meta_ref
  60.2 6.8 %collective-permute-done.1 = bf16[2,64,1024]{2,1,0:T(8,128)(2,1)} collective-permute-done((bf16[2,64,1024]{2,1,0:T(8,128)(2,1)S(1)}, bf16[2,64,1024]{2,1,0:T(8,128)(2,1)}, u32[]{:S(2)}, u32[]{:S(2)}) %collective-permute-start.1) | collective-permute-done | bytes 262176 | tf_op jit(solution)/shard_map/ppermute | solution.py:25
  66.9 17.7 %collective-permute-start.16 = (bf16[2,128,1024]{2,1,0:T(8,128)(2,1)}, bf16[2,128,1024]{2,1,0:T(8,128)(2,1)}, u32[]{:S(2)}, u32[]{:S(2)}) collective-permute-start(bf16[2,128,1024]{2,1,0:T(8,128)(2,1)} %pad_maximum_fusion.3), channel_id=1, source_target_pairs={{0,16},{1,17},{2,18},{3,19},{4,20},{5,21},{6,22},{7,23},{8,24},{9,... | collective-permute-start | bytes 1572872 | tf_op jit(solution)/shard_map/ppermute | solution.py:60
  84.6 2.1 %pad_maximum_fusion.win_ref = bf16[2,256,1024]{2,1,0:T(8,128)(2,1)} fusion(bf16[2,64,1024]{2,1,0:T(8,128)(2,1)} %collective-permute-done.1, bf16[1,128,1024]{2,1,0:T(8,128)(2,1)S(1)} %bitcast.46, bf16[1,128,1024]{2,1,0:T(8,128)(2,1)S(1)} %bitcast.43, bf16[2,64,1024]{2,1,0:T(8,128)(2,1)} %collective-permute-done), kind=kLoop, calls=%fused_computation | loop fusion | flops 4194304 | bytes 2097152 | tf_op jit(solution)/shard_map/concatenate | solution.py:26
  86.7 0.0 collective-permute-done.7
  86.7 0.0 collective-permute-start.15
  86.8 0.9 pad_maximum_fusion.2
  87.7 0.0 collective-permute-done.10.rest_2_
  87.7 0.0 collective-permute-done.8.rest_0_
  87.7 0.7 copy-done.8
  88.5 0.2 copy-done.9
  88.7 0.2 copy-done.10
  88.8 13.2 %shard_map.93 = (bf16[128,1024]{1,0:T(8,128)(2,1)}, bf16[128,1024]{1,0:T(8,128)(2,1)}, f32[2,256,1024]{2,1,0:T(8,128)}, f32[3,2,128,1024]{3,2,1,0:T(8,128)}, f32[8,6,128]{2,1,0:T(8,128)}) custom-call(s32[10]{0:T(128)} %pad_add_fusion.meta_ref, bf16[128,1024]{1,0:T(8,128)(2,1)} %q_ref.1, bf16[128,1024]{1,0:T(8,128)(2,1)} %g_ref.1, ...), custom_call_target="tpu_custom_call" | custom-call | tf_op jit(solution)/shard_map/pallas_call | solution.py:165
  102.1 1.9 %convert.12 = bf16[2,256,1024]{2,1,0:T(8,128)(2,1)S(1)} convert(f32[2,256,1024]{2,1,0:T(8,128)} %get-tuple-element.35) | non-fusion elementwise | flops 524288 | bytes 3145728 | tf_op jit(solution)/shard_map/convert.5
  104.0 0.8 fusion.10
  104.8 2.1 %collective-permute-start.11 = (bf16[2,64,1024]{2,1,0:T(8,128)(2,1)}, bf16[2,64,1024]{2,1,0:T(8,128)(2,1)S(1)}, u32[]{:S(2)}, u32[]{:S(2)}) collective-permute-start(bf16[2,64,1024]{2,1,0:T(8,128)(2,1)} %get-tuple-element.43), channel_id=1, source_target_pairs={{1,0},{2,1},{3,2},{4,3},{5,4},{6,5},{7,6},{8,7},{9,8},{10,9},{11,1... | collective-permute-start | bytes 786440 | tf_op jit(solution)/shard_map/ppermute | solution.py:66
  106.9 0.2 convert.13
  107.1 0.5 copy-done.14
  107.6 4.6 %collective-permute-start.17 = (f32[8,6,128]{2,1,0:T(8,128)S(1)}, f32[8,6,128]{2,1,0:T(8,128)S(1)}, u32[]{:S(2)}, u32[]{:S(2)}) collective-permute-start(f32[8,6,128]{2,1,0:T(8,128)S(1)} %copy-done.14), channel_id=1, source_target_pairs={{0,16},{1,17},{2,18},{3,19},{4,20},{5,21},{6,22},{7,23},{8,24},{9,... | collective-permute-start | bytes 73736 | tf_op jit(solution)/shard_map/ppermute | solution.py:60
  112.3 1.0 slice_bitcast_fusion.1
  113.3 0.4 collective-permute-start.13
  113.7 0.0 collective-permute-done.15
  113.7 0.0 collective-permute-start.14
  113.7 1.9 %collective-permute-start.12 = (bf16[2,64,1024]{2,1,0:T(8,128)(2,1)}, bf16[2,64,1024]{2,1,0:T(8,128)(2,1)}, u32[]{:S(2)}, u32[]{:S(2)}) collective-permute-start(bf16[2,64,1024]{2,1,0:T(8,128)(2,1)} %get-tuple-element.42), channel_id=1, source_target_pairs={{0,1},{1,2},{2,3},{3,4},{4,5},{5,6},{6,7},{7,8},{8,9},{9,10},{10,1... | collective-permute-start | bytes 786440 | tf_op jit(solution)/shard_map/ppermute | solution.py:66
  115.6 0.5 convert_element_type.55.pick_ref
  116.2 0.1 slice.105
  116.3 1.6 %collective-permute-done.17.st_ref = f32[8,6,128]{2,1,0:T(8,128)S(1)} collective-permute-done((f32[8,6,128]{2,1,0:T(8,128)S(1)}, f32[8,6,128]{2,1,0:T(8,128)S(1)}, u32[]{:S(2)}, u32[]{:S(2)}) %collective-permute-start.17) | collective-permute-done | bytes 24608 | tf_op jit(solution)/shard_map/ppermute | solution.py:60
  117.8 0.6 copy-done.12
  118.4 7.9 %shard_map.94 = f32[2,128,1024]{2,1,0:T(8,128)} custom-call(s32[2]{0:T(128)} %convert_element_type.55.pick_ref, bf16[2,128,1024]{2,1,0:T(8,128)(2,1)} %collective-permute-done.16.qd_ref, f32[8,6,128]{2,1,0:T(8,128)} %copy-done.12, bf16[2,128,1024]{2,1,0:T(8,128)(2,1)} %copy-done.5), custom_call_target="tpu_custom_call" | custom-call | tf_op jit(solution)/shard_map/pallas_call | solution.py:216
  126.3 0.1 add_dynamic-update-slice_fusion
  126.4 5.7 %collective-permute-done.12 = bf16[2,64,1024]{2,1,0:T(8,128)(2,1)} collective-permute-done((bf16[2,64,1024]{2,1,0:T(8,128)(2,1)}, bf16[2,64,1024]{2,1,0:T(8,128)(2,1)}, u32[]{:S(2)}, u32[]{:S(2)}) %collective-permute-start.12) | collective-permute-done | bytes 262176 | tf_op jit(solution)/shard_map/ppermute | solution.py:66
  132.1 1.1 fusion
  133.2 1.5 %add_convert_fusion = bf16[2,128,1024]{2,1,0:T(8,128)(2,1)S(1)} fusion(f32[2,128,1024]{2,1,0:T(8,128)S(1)} %copy-done.1, bf16[2,128,1024]{2,1,0:T(8,128)(2,1)} %collective-permute-done.14, f32[2,128,1024]{2,1,0:T(8,128)S(1)} %fusion, bf16[2,128,1024]{2,1,0:T(8,128)(2,1)} %collective-permute-done.13), kind=kLoop, calls=%fused_computation.1 | loop fusion | flops 1572864 | bytes 3670016 | tf_op jit(solution)/shard_map/convert.1
  134.7 0.8 slice_bitcast_fusion.2
  (36 shorter events, 0.2 us)
Async XLA Ops:
  0.6 4.9 %copy-start.13 = (s32[2]{0:T(128)S(1)}, s32[2]{0:T(128)}, u32[]{:S(2)}) copy-start(s32[2]{0:T(128)} %param.15) | copy-start | bytes 28
  5.4 29.7 %copy-start.3 = (bf16[128,1024]{1,0:T(8,128)(2,1)S(1)}, bf16[128,1024]{1,0:T(8,128)(2,1)}, u32[]{:S(2)}) copy-start(bf16[128,1024]{1,0:T(8,128)(2,1)} %param.11) | copy-start | bytes 786436
  5.4 29.7 %copy-start.4 = (bf16[128,1024]{1,0:T(8,128)(2,1)S(1)}, bf16[128,1024]{1,0:T(8,128)(2,1)}, u32[]{:S(2)}) copy-start(bf16[128,1024]{1,0:T(8,128)(2,1)} %param.12) | copy-start | bytes 786436
  5.4 1.6 %collective-permute-start.2 = (bf16[2,64,1024]{2,1,0:T(8,128)(2,1)S(1)}, bf16[2,64,1024]{2,1,0:T(8,128)(2,1)S(1)}, u32[]{:S(2)}, u32[]{:S(2)}) collective-permute-start(bf16[2,64,1024]{2,1,0:T(8,128)(2,1)S(1)} %select_bitcast_fusion.2), channel_id=1, source_target_pairs={{0,1},{1,0},{2,3},{3,2},{4,5},{5,4},{6,7},{7,6},{8,9},{9,8},{10,11... | collective-permute-start | bytes 786440 | tf_op jit(solution)/shard_map/ppermute | solution.py:42
  7.0 39.1 %copy-start.15 = (s32[2,3]{1,0:T(2,128)S(1)}, s32[2,3]{1,0:T(2,128)}, u32[]{:S(2)}) copy-start(s32[2,3]{1,0:T(2,128)} %param.14) | copy-start | bytes 76
  7.1 39.2 %copy-start.6 = (bf16[128,1024]{1,0:T(8,128)(2,1)S(1)}, bf16[128,1024]{1,0:T(8,128)(2,1)}, u32[]{:S(2)}) copy-start(bf16[128,1024]{1,0:T(8,128)(2,1)} %q_ref.1) | copy-start | bytes 786436
  7.1 39.2 %copy-start.7 = (bf16[128,1024]{1,0:T(8,128)(2,1)S(1)}, bf16[128,1024]{1,0:T(8,128)(2,1)}, u32[]{:S(2)}) copy-start(bf16[128,1024]{1,0:T(8,128)(2,1)} %g_ref.1) | copy-start | bytes 786436
  7.2 8.4 %collective-permute-start.3 = (bf16[2,64,1024]{2,1,0:T(8,128)(2,1)S(1)}, bf16[2,64,1024]{2,1,0:T(8,128)(2,1)S(1)}, u32[]{:S(2)}, u32[]{:S(2)}) collective-permute-start(bf16[2,64,1024]{2,1,0:T(8,128)(2,1)S(1)} %fusion.2), channel_id=1, source_target_pairs={{0,2},{1,3},{2,0},{3,1},{4,6},{5,7},{6,4},{7,5},{8,10},{9,11},{10,... | collective-permute-start | bytes 786440 | tf_op jit(solution)/shard_map/ppermute | solution.py:50
  15.7 9.1 %collective-permute-start.4 = (bf16[2,64,1024]{2,1,0:T(8,128)(2,1)S(1)}, bf16[2,64,1024]{2,1,0:T(8,128)(2,1)S(1)}, u32[]{:S(2)}, u32[]{:S(2)}) collective-permute-start(bf16[2,64,1024]{2,1,0:T(8,128)(2,1)S(1)} %broadcast_select_fusion), channel_id=1, source_target_pairs={{0,4},{1,5},{2,6},{3,7},{4,0},{5,1},{6,2},{7,3},{8,12},{9,13},{10,... | collective-permute-start | bytes 786440 | tf_op jit(solution)/shard_map/ppermute | solution.py:50
  24.9 6.7 %collective-permute-start.5 = (bf16[2,64,1024]{2,1,0:T(8,128)(2,1)S(1)}, bf16[2,64,1024]{2,1,0:T(8,128)(2,1)S(1)}, u32[]{:S(2)}, u32[]{:S(2)}) collective-permute-start(bf16[2,64,1024]{2,1,0:T(8,128)(2,1)S(1)} %broadcast_select_fusion.1), channel_id=1, source_target_pairs={{0,8},{1,9},{2,10},{3,11},{4,12},{5,13},{6,14},{7,15},{8,0},{9,1},... | collective-permute-start | bytes 786440 | tf_op jit(solution)/shard_map/ppermute | solution.py:50
  31.7 23.7 %collective-permute-start.6 = (bf16[2,64,1024]{2,1,0:T(8,128)(2,1)S(1)}, bf16[2,64,1024]{2,1,0:T(8,128)(2,1)S(1)}, u32[]{:S(2)}, u32[]{:S(2)}) collective-permute-start(bf16[2,64,1024]{2,1,0:T(8,128)(2,1)S(1)} %broadcast_select_fusion.2), channel_id=1, source_target_pairs={{0,16},{1,17},{2,18},{3,19},{4,20},{5,21},{6,22},{7,23},{8,24},{9,... | collective-permute-start | bytes 786440 | tf_op jit(solution)/shard_map/ppermute | solution.py:50
  35.1 51.7 %copy-start.5 = (bf16[2,128,1024]{2,1,0:T(8,128)(2,1)}, bf16[2,128,1024]{2,1,0:T(8,128)(2,1)S(1)}, u32[]{:S(2)}) copy-start(bf16[2,128,1024]{2,1,0:T(8,128)(2,1)S(1)} %pad_maximum_fusion.1.kv_ref) | copy-start | bytes 1572868
  35.1 52.5 %collective-permute-start.10 = (bf16[2,128,1024]{2,1,0:T(8,128)(2,1)S(1)}, bf16[2,128,1024]{2,1,0:T(8,128)(2,1)S(1)}, u32[]{:S(2)}, u32[]{:S(2)}) collective-permute-start(bf16[2,128,1024]{2,1,0:T(8,128)(2,1)S(1)} %pad_maximum_fusion.1.kv_ref), channel_id=1, source_target_pairs={{0,4},{1,5},{2,6},{3,7},{4,0},{5,1},{6,2},{7,3},{8,12},{9,13},{10,... | collective-permute-start | bytes 1572872 | tf_op jit(solution)/shard_map/ppermute | solution.py:60
  38.4 49.3 %collective-permute-start.8 = (bf16[2,128,1024]{2,1,0:T(8,128)(2,1)S(1)}, bf16[2,128,1024]{2,1,0:T(8,128)(2,1)S(1)}, u32[]{:S(2)}, u32[]{:S(2)}) collective-permute-start(bf16[2,128,1024]{2,1,0:T(8,128)(2,1)S(1)} %pad_maximum_fusion.1.kv_ref), channel_id=1, source_target_pairs={{0,16},{1,17},{2,18},{3,19},{4,20},{5,21},{6,22},{7,23},{8,24},{9,... | collective-permute-start | bytes 1572872 | tf_op jit(solution)/shard_map/ppermute | solution.py:60
  38.4 18.9 %collective-permute-start = (bf16[2,64,1024]{2,1,0:T(8,128)(2,1)}, bf16[2,64,1024]{2,1,0:T(8,128)(2,1)}, u32[]{:S(2)}, u32[]{:S(2)}) collective-permute-start(bf16[2,64,1024]{2,1,0:T(8,128)(2,1)} %get-tuple-element.49), channel_id=1, source_target_pairs={{0,1},{1,2},{2,3},{3,4},{4,5},{5,6},{6,7},{7,8},{8,9},{9,10},{10,1... | collective-permute-start | bytes 786440 | tf_op jit(solution)/shard_map/ppermute | solution.py:24
  40.4 26.6 %collective-permute-start.1 = (bf16[2,64,1024]{2,1,0:T(8,128)(2,1)S(1)}, bf16[2,64,1024]{2,1,0:T(8,128)(2,1)}, u32[]{:S(2)}, u32[]{:S(2)}) collective-permute-start(bf16[2,64,1024]{2,1,0:T(8,128)(2,1)S(1)} %get-tuple-element.50), channel_id=1, source_target_pairs={{1,0},{2,1},{3,2},{4,3},{5,4},{6,5},{7,6},{8,7},{9,8},{10,9},{11,1... | collective-permute-start | bytes 786440 | tf_op jit(solution)/shard_map/ppermute | solution.py:25
  55.4 0.7 copy-start.11
  57.1 29.6 %collective-permute-start.7 = (bf16[2,64,1024]{2,1,0:T(8,128)(2,1)S(1)}, bf16[2,64,1024]{2,1,0:T(8,128)(2,1)S(1)}, u32[]{:S(2)}, u32[]{:S(2)}) collective-permute-start(bf16[2,64,1024]{2,1,0:T(8,128)(2,1)S(1)} %broadcast_select_fusion.3), channel_id=1, source_target_pairs={{0,1},{1,0},{2,3},{3,2},{4,5},{5,4},{6,7},{7,6},{8,9},{9,8},{10,11... | collective-permute-start | bytes 786440 | tf_op jit(solution)/shard_map/ppermute | solution.py:53
  57.3 30.3 %collective-permute-start.9 = (bf16[2,128,1024]{2,1,0:T(8,128)(2,1)S(1)}, bf16[2,128,1024]{2,1,0:T(8,128)(2,1)S(1)}, u32[]{:S(2)}, u32[]{:S(2)}) collective-permute-start(bf16[2,128,1024]{2,1,0:T(8,128)(2,1)S(1)} %pad_maximum_fusion.1.kv_ref), channel_id=1, source_target_pairs={{0,8},{1,9},{2,10},{3,11},{4,12},{5,13},{6,14},{7,15},{8,0},{9,1},... | collective-permute-start | bytes 1572872 | tf_op jit(solution)/shard_map/ppermute | solution.py:60
  66.9 46.8 %collective-permute-start.16 = (bf16[2,128,1024]{2,1,0:T(8,128)(2,1)}, bf16[2,128,1024]{2,1,0:T(8,128)(2,1)}, u32[]{:S(2)}, u32[]{:S(2)}) collective-permute-start(bf16[2,128,1024]{2,1,0:T(8,128)(2,1)} %pad_maximum_fusion.3), channel_id=1, source_target_pairs={{0,16},{1,17},{2,18},{3,19},{4,20},{5,21},{6,22},{7,23},{8,24},{9,... | collective-permute-start | bytes 1572872 | tf_op jit(solution)/shard_map/ppermute | solution.py:60
  86.7 27.0 %collective-permute-start.15 = (f32[2]{0:T(128)S(1)}, f32[2]{0:T(128)S(1)}, u32[]{:S(2)}, u32[]{:S(2)}) collective-permute-start(f32[2]{0:T(128)S(1)} %convert_reduce_fusion), channel_id=1, source_target_pairs={{0,16},{1,17},{2,18},{3,19},{4,20},{5,21},{6,22},{7,23},{8,24},{9,... | collective-permute-start | bytes 32 | tf_op jit(solution)/shard_map/ppermute | solution.py:60
  87.7 0.8 copy-start.8
  87.7 1.0 copy-start.9
  87.7 1.1 copy-start.10
  102.1 4.8 %copy-start.2 = (f32[3,2,128,1024]{3,2,1,0:T(8,128)S(1)}, f32[3,2,128,1024]{3,2,1,0:T(8,128)}, u32[]{:S(2)}) copy-start(f32[3,2,128,1024]{3,2,1,0:T(8,128)} %get-tuple-element.36) | copy-start | bytes 9437188
  104.8 21.5 %collective-permute-start.11 = (bf16[2,64,1024]{2,1,0:T(8,128)(2,1)}, bf16[2,64,1024]{2,1,0:T(8,128)(2,1)S(1)}, u32[]{:S(2)}, u32[]{:S(2)}) collective-permute-start(bf16[2,64,1024]{2,1,0:T(8,128)(2,1)} %get-tuple-element.43), channel_id=1, source_target_pairs={{1,0},{2,1},{3,2},{4,3},{5,4},{6,5},{7,6},{8,7},{9,8},{10,9},{11,1... | collective-permute-start | bytes 786440 | tf_op jit(solution)/shard_map/ppermute | solution.py:66
  106.9 0.8 copy-start.14
  107.1 9.0 %copy-start = (f32[2,256,1024]{2,1,0:T(8,128)S(1)}, f32[2,256,1024]{2,1,0:T(8,128)}, u32[]{:S(2)}) copy-start(f32[2,256,1024]{2,1,0:T(8,128)} %get-tuple-element.35) | copy-start | bytes 6291460
  107.6 10.2 %collective-permute-start.17 = (f32[8,6,128]{2,1,0:T(8,128)S(1)}, f32[8,6,128]{2,1,0:T(8,128)S(1)}, u32[]{:S(2)}, u32[]{:S(2)}) collective-permute-start(f32[8,6,128]{2,1,0:T(8,128)S(1)} %copy-done.14), channel_id=1, source_target_pairs={{0,16},{1,17},{2,18},{3,19},{4,20},{5,21},{6,22},{7,23},{8,24},{9,... | collective-permute-start | bytes 73736 | tf_op jit(solution)/shard_map/ppermute | solution.py:60
  113.3 19.8 %collective-permute-start.13 = (bf16[2,128,1024]{2,1,0:T(8,128)(2,1)}, bf16[2,128,1024]{2,1,0:T(8,128)(2,1)}, u32[]{:S(2)}, u32[]{:S(2)}) collective-permute-start(bf16[2,128,1024]{2,1,0:T(8,128)(2,1)} %get-tuple-element.40), channel_id=1, source_target_pairs={{0,8},{1,9},{2,10},{3,11},{4,12},{5,13},{6,14},{7,15},{8,0},{9,1},... | collective-permute-start | bytes 1572872 | tf_op jit(solution)/shard_map/ppermute | solution.py:60
  113.7 19.5 %collective-permute-start.14 = (bf16[2,128,1024]{2,1,0:T(8,128)(2,1)}, bf16[2,128,1024]{2,1,0:T(8,128)(2,1)}, u32[]{:S(2)}, u32[]{:S(2)}) collective-permute-start(bf16[2,128,1024]{2,1,0:T(8,128)(2,1)} %get-tuple-element.41), channel_id=1, source_target_pairs={{0,4},{1,5},{2,6},{3,7},{4,0},{5,1},{6,2},{7,3},{8,12},{9,13},{10,... | collective-permute-start | bytes 1572872 | tf_op jit(solution)/shard_map/ppermute | solution.py:60
  113.7 18.4 %collective-permute-start.12 = (bf16[2,64,1024]{2,1,0:T(8,128)(2,1)}, bf16[2,64,1024]{2,1,0:T(8,128)(2,1)}, u32[]{:S(2)}, u32[]{:S(2)}) collective-permute-start(bf16[2,64,1024]{2,1,0:T(8,128)(2,1)} %get-tuple-element.42), channel_id=1, source_target_pairs={{0,1},{1,2},{2,3},{3,4},{4,5},{5,6},{6,7},{7,8},{8,9},{9,10},{10,1... | collective-permute-start | bytes 786440 | tf_op jit(solution)/shard_map/ppermute | solution.py:66
  117.8 0.6 copy-start.12
  126.3 6.9 %copy-start.1 = (f32[2,128,1024]{2,1,0:T(8,128)S(1)}, f32[2,128,1024]{2,1,0:T(8,128)}, u32[]{:S(2)}) copy-start(f32[2,128,1024]{2,1,0:T(8,128)} %shard_map.94) | copy-start | bytes 3145732
